TPU v7x, 32 devices: a whole 2x2x4 slice. The times are simulated.
32 devices in a mesh: group: 2 (over x), node: 16 (over z, y, core).
Axes of the slice: x: 2, y: 2, z: 4, core: 2. Of those that a mesh axis runs over, the one named last changes fastest.
Arguments:
- states: bfloat16 [512, 2048], P(('group', 'node')), parts along dimension 0, may hold values from -400 to 400
- norm_gain: float32 [2048], replicated, may hold values from 0.5 to 1.5
- picks: int32 [512, 8], P(('group', 'node')), parts along dimension 0, may hold values from 0 to 15, all different within a row; in each aligned block of 16 rows (0 to 15, 16 to 31, ...) at most 16 rows name the same one
- gate_weights: float32 [512, 8], P(('group', 'node')), parts along dimension 0, may hold values from 0.05 to 1
- w_gate: bfloat16 [16, 2048, 768], P('node'), may hold values from -0.125 to 0.125
- w_up: bfloat16 [16, 2048, 768], P('node'), may hold values from -0.125 to 0.125
- w_down: bfloat16 [16, 768, 2048], P('node'), may hold values from -0.21875 to 0.21875
- queries: bfloat16 [128, 4096], P(('group', 'node')), parts along dimension 0, may hold values from -88 to 88
- keys: bfloat16 [128, 256, 512], P(('group', 'node')), parts along dimension 0, may hold values from -4 to 4
- values: bfloat16 [128, 256, 512], P(('group', 'node')), parts along dimension 0, may hold values from -4 to 4
- incoming_keys: bfloat16 [128, 512], P(('group', 'node')), parts along dimension 0, may hold values from -4 to 4
- incoming_values: bfloat16 [128, 512], P(('group', 'node')), parts along dimension 0, may hold values from -4 to 4
- lengths: int32 [128], P(('group', 'node')), parts along dimension 0, may hold values from 32 to 256, as said below
Outputs:
- moe_output: bfloat16 [512, 2048], P(('group', 'node')), parts along dimension 0
- attention_output: bfloat16 [128, 4096], P(('group', 'node')), parts along dimension 0
There are 2 independent parts, one for each index of `group`. A program takes and returns all parts, laid end to end along the dimension named above; an argument that names none is the same for every part. Nothing has to cross between parts.
Inputs may be any that keep to these rules, and one draw needn't show every extreme that they name: Each token picks 8 different experts; among the 16 tokens of one device no expert is picked by more than 16 tokens, a bound that some block reaches. `lengths`: the first request of each device holds 256 cached tokens.
All inputs are finite; a program needn't handle non-finite values.
Results may differ from a plain program's by a relative error of at most 0.0085.
Values may be sent and summed in bfloat16 or wider, within the bound.
No kernel may reach another device: no remote copies, remote signals or barrier semaphores. Data moves between devices by JAX's collectives and lax.ppermute only.
A program may use at most 64 MiB of HBM per device.

v0:
```python
import math

import jax
import jax.numpy as jnp
from jax import lax
from jax.sharding import PartitionSpec as P

QUERY_HEADS = 32
KEY_VALUE_HEADS = 4
HEAD_WIDTH = 128
TOPK = 8
TOK_DEV = 16


def expert_block(received, w_gate, w_up, w_down):
    peers = lax.axis_size("node")
    local_experts = w_gate.shape[0]
    slot_count = received.shape[1]
    features = received.shape[2]
    grouped = received.reshape(peers, local_experts, slot_count, features)
    gate_part = jnp.einsum("nesd,edf->nesf", grouped, w_gate, preferred_element_type=jnp.float32)
    up_part = jnp.einsum("nesd,edf->nesf", grouped, w_up, preferred_element_type=jnp.float32)
    inner = (jax.nn.silu(gate_part) * up_part).astype(jnp.bfloat16)
    produced = jnp.einsum(
        "nesf,efd->nesd", inner, w_down, preferred_element_type=jnp.float32
    ).astype(jnp.bfloat16)
    return produced.reshape(peers * local_experts, slot_count, features)


def route_block(normed, picks, gate_weights, w_gate, w_up, w_down, capacity):
    rows_here = picks.shape[0]
    picks_here = picks.shape[1]
    experts_all = w_gate.shape[0] * lax.axis_size("node")
    features = normed.shape[1]
    flattened = picks.reshape(-1)
    expert_ids = jnp.arange(experts_all, dtype=jnp.int32)
    onehot = (flattened[:, None] == expert_ids[None, :]).astype(jnp.int32)
    earlier = jnp.cumsum(onehot, axis=0) - onehot
    slot_of = jnp.sum(earlier * onehot, axis=1)
    target = flattened * capacity + slot_of
    layout = jnp.arange(experts_all * capacity, dtype=jnp.int32)
    placed = jnp.sum(
        (layout[:, None, None] == target.reshape(rows_here, picks_here)[None, :, :]).astype(
            jnp.int32
        ),
        axis=2,
    )
    outgoing = jnp.dot(placed.astype(jnp.bfloat16), normed, preferred_element_type=jnp.float32)
    outgoing = outgoing.astype(jnp.bfloat16).reshape(experts_all, capacity, features)
    produced = expert_block(
        lax.all_to_all(outgoing, "node", split_axis=0, concat_axis=0, tiled=True),
        w_gate,
        w_up,
        w_down,
    )
    returned = lax.all_to_all(produced, "node", split_axis=0, concat_axis=0, tiled=True)
    gathered = jnp.take(returned.reshape(experts_all * capacity, features), target, axis=0)
    gathered = gathered.reshape(rows_here, picks_here, features)
    shares = gate_weights / jnp.sum(gate_weights, axis=1, keepdims=True)
    return jnp.einsum("tk,tkd->td", shares, gathered.astype(jnp.float32)).astype(jnp.bfloat16)


def attend(queries, keys, values, incoming_keys, incoming_values, lengths):
    request_rows = queries.shape[0]
    valid_length = keys.shape[1]
    query_groups = QUERY_HEADS // KEY_VALUE_HEADS
    score_scale = 1.0 / math.sqrt(HEAD_WIDTH)
    query_rows = queries.reshape(request_rows, KEY_VALUE_HEADS, query_groups, HEAD_WIDTH)
    stored_keys = keys.reshape(request_rows, valid_length, KEY_VALUE_HEADS, HEAD_WIDTH)
    stored_values = values.reshape(request_rows, valid_length, KEY_VALUE_HEADS, HEAD_WIDTH)
    scores = (
        jnp.einsum("rkgd,rlkd->rkgl", query_rows, stored_keys, preferred_element_type=jnp.float32)
        * score_scale
    )
    new_token_scores = (
        jnp.einsum(
            "behw,bew->beh",
            query_rows,
            incoming_keys.reshape(request_rows, KEY_VALUE_HEADS, HEAD_WIDTH),
            preferred_element_type=jnp.float32,
        )
        * score_scale
    )
    present = (jnp.arange(valid_length, dtype=jnp.int32)[None, :] < lengths[:, None])[
        :, None, None, :
    ]
    masked = jnp.where(present, scores, -1e30)
    highest = jnp.maximum(jnp.max(masked, axis=3), new_token_scores)
    raised = jnp.where(present, jnp.exp(masked - highest[..., None]), 0.0)
    fresh_raised = jnp.exp(new_token_scores - highest)
    denominator = jnp.sum(raised, axis=3) + fresh_raised
    probs = (raised / denominator[..., None]).astype(jnp.bfloat16)
    new_token_probability = (fresh_raised / denominator).astype(jnp.bfloat16)
    blended_output = jnp.einsum(
        "rkgl,rlkd->rkgd", probs, stored_values, preferred_element_type=jnp.float32
    )
    blended_output = blended_output + new_token_probability.astype(jnp.float32)[
        ..., None
    ] * incoming_values.reshape(request_rows, KEY_VALUE_HEADS, 1, HEAD_WIDTH).astype(jnp.float32)
    return blended_output.reshape(request_rows, QUERY_HEADS * HEAD_WIDTH).astype(jnp.bfloat16)


def on_device(
    states,
    norm_gain,
    picks,
    gate_weights,
    w_gate,
    w_up,
    w_down,
    queries,
    keys,
    values,
    incoming_keys,
    incoming_values,
    lengths,
):
    widened = states.astype(jnp.float32)
    meansq = jnp.mean(widened * widened, axis=1, keepdims=True) + 1e-06
    normed = (widened / jnp.sqrt(meansq) * norm_gain[None, :]).astype(jnp.bfloat16)
    experts_all = w_gate.shape[0] * lax.axis_size("node")
    capacity = min(TOK_DEV, max(2, 2 * TOK_DEV * TOPK // experts_all))
    moe_output = route_block(normed, picks, gate_weights, w_gate, w_up, w_down, capacity)
    attention_output = attend(queries, keys, values, incoming_keys, incoming_values, lengths)
    return (moe_output, attention_output)


def solution(mesh):
    in_specs = (
        P(("group", "node"), None),
        P(),
        P(("group", "node"), None),
        P(("group", "node"), None),
        P("node", None, None),
        P("node", None, None),
        P("node", None, None),
        P(("group", "node"), None),
        P(("group", "node"), None, None),
        P(("group", "node"), None, None),
        P(("group", "node"), None),
        P(("group", "node"), None),
        P(("group", "node")),
    )
    out_specs = (P(("group", "node"), None), P(("group", "node"), None))
    return jax.shard_map(
        on_device, mesh=mesh, in_specs=in_specs, out_specs=out_specs, check_vma=False
    )
```

profile of v0, /device:TPU:11, one launch (start us, length us, event | category | flops | bytes accessed | tf_op | source)
XLA Modules:
  0.0 82.6 jit_solution(17584107868343403584)
XLA Ops:
  0.6 0.0 copy-start
  0.6 0.0 copy-start.2
  0.7 1.1 %fusion.37 = f32[16]{0:T(128)S(1)} fusion(bf16[16,2048]{1,0:T(8,128)(2,1)} %param.13), kind=kLoop, calls=%fused_computation.30 | loop fusion | flops 98288 | bytes 65600 | tf_op jit(solution)/shard_map/reduce_sum | solution.py:119
  1.8 0.8 copy.23
  2.6 0.1 reshape.138
  2.6 0.1 fusion.47
  2.7 0.2 reduce_window_sum.11
  2.9 0.2 select_reduce_fusion
  3.1 0.1 reduce_sum.51
  3.2 0.1 convert_reduce_fusion
  3.3 2.4 %convolution_convert_fusion = bf16[256,2048]{1,0:T(8,128)(2,1)} fusion(bf16[16,2048]{1,0:T(8,128)(2,1)} %param.13, f32[2048]{0:T(1024)} %param.14, f32[16]{0:T(128)S(1)} %add_sqrt_fusion, s32[256,16]{0,1:T(8,128)S(1)} %convert_reduce_fusion), kind=kOutput, calls=%fused_computation.8 | convolution fusion | flops 17436672 | bytes 1138752 | tf_op jit(solution)/shard_map/dot_general | solution.py:48
  5.7 6.6 %all-to-all-start = ((bf16[16,16,2048]{2,1,0:T(8,128)(2,1)}), bf16[16,16,2048]{2,1,0:T(8,128)(2,1)}, u32[]{:S(2)}, u32[]{:S(2)}) async-start(bf16[16,16,2048]{2,1,0:T(8,128)(2,1)} %bitcast.103), calls=%async_computation | async-start | bytes 2097152 | tf_op jit(solution)/shard_map/all_to_all | solution.py:51
  12.3 0.0 copy-done.2
  12.3 24.9 %all-to-all-done = bf16[16,16,2048]{2,1,0:T(8,128)(2,1)} async-done(((bf16[16,16,2048]{2,1,0:T(8,128)(2,1)}), bf16[16,16,2048]{2,1,0:T(8,128)(2,1)}, u32[]{:S(2)}, u32[]{:S(2)}) %all-to-all-start) | async-done | bytes 1048608 | tf_op jit(solution)/shard_map/all_to_all | solution.py:51
  37.2 4.1 %fusion.9 = f32[16,1,16,768]{3,2,0,1:T(8,128)} fusion(bf16[16,16,2048]{2,1,0:T(8,128)(2,1)} %all-to-all-done, bf16[1,2048,768]{2,1,0:T(8,128)(2,1)} %param.17), kind=kOutput, calls=%fused_computation.9 | convolution fusion | flops 805306368 | bytes 4980736 | tf_op jit(solution)/shard_map/nesd,edf->nesf/dot_general | solution.py:21
  41.3 0.0 copy-done
  41.3 0.0 copy-start.3
  41.3 0.0 copy-start.4
  41.4 0.0 copy-start.5
  41.4 0.0 copy-start.1
  41.4 5.6 %fusion.6 = bf16[16,16,2048]{2,1,0:T(8,128)(2,1)} fusion(bf16[1,768,2048]{2,1,0:T(8,128)(2,1)S(1)} %copy-done, bf16[16,16,2048]{2,1,0:T(8,128)(2,1)} %all-to-all-done, bf16[1,2048,768]{2,1,0:T(8,128)(2,1)} %param.18, f32[16,1,16,768]{3,2,0,1:T(8,128)} %fusion.9), kind=kOutput, calls=%fused_computation.7 | convolution fusion | flops 1612316672 | bytes 9175040 | tf_op jit(solution)/shard_map/nesf,efd->nesd/dot_general | solution.py:24
  47.0 5.0 %all-to-all-start.1 = ((bf16[16,16,2048]{2,1,0:T(8,128)(2,1)}), bf16[16,16,2048]{2,1,0:T(8,128)(2,1)}, u32[]{:S(2)}, u32[]{:S(2)}) async-start(bf16[16,16,2048]{2,1,0:T(8,128)(2,1)} %fusion.6), calls=%async_computation.1 | async-start | bytes 2097152 | tf_op jit(solution)/shard_map/all_to_all | solution.py:56
  51.9 0.1 copy.27
  52.0 0.1 mul.75
  52.1 0.0 copy-done.3
  52.1 0.0 copy-done.4
  52.2 0.0 copy-done.5
  52.2 0.1 iota_compare_fusion.2
  52.2 0.0 copy-done.1
  52.3 0.1 fusion.49
  52.4 1.7 %fusion.63 = (f32[4,4,8]{2,1,0:T(4,128)S(1)}, f32[4,4,8,256]{3,2,1,0:T(8,128)S(1)}) fusion(bf16[1,4,32,128]{3,1,2,0:T(4,128)(2,1)S(1)} %bitcast.106, pred[4,256]{1,0:T(4,128)(4,1)S(1)} %iota_compare_fusion.2, bf16[4,256,512]{2,1,0:T(8,128)(2,1)} %param.21), kind=kOutput, calls=%fused_computation.74 | convolution fusion | flops 8486784 | bytes 1213952 | tf_op jit(solution)/shard_map/rkgd,rlkd->rkgl/dot_general | solution.py:72
  54.1 0.2 fusion.40
  54.3 1.5 %fusion.26 = bf16[1,4,32,128]{3,2,1,0:T(8,128)(2,1)S(1)} fusion(f32[4,4,8,256]{3,2,1,0:T(8,128)S(1)} %get-tuple-element.7, f32[4,4,8]{2,1,0:T(4,128)S(1)} %get-tuple-element.5, f32[4,4,8]{2,1,0:T(4,128)S(1)} %multiply_maximum_fusion, pred[4,256]{1,0:T(4,128)(4,1)S(1)} %iota_compare_fusion.2, f32[4,4,128]{2,1,0:T(4,128)S(1)} %reshape.149, ...), kind=kOutput, calls=%fused_computation.18 | convolution fusion | flops 8568832 | bytes 1223168 | tf_op jit(solution)/shard_map/rkgl,rlkd->rkgd/dot_general | solution.py:94
  55.9 0.6 copy.58
  56.5 20.4 %all-to-all-done.1 = bf16[16,16,2048]{2,1,0:T(8,128)(2,1)} async-done(((bf16[16,16,2048]{2,1,0:T(8,128)(2,1)}), bf16[16,16,2048]{2,1,0:T(8,128)(2,1)}, u32[]{:S(2)}, u32[]{:S(2)}) %all-to-all-start.1) | async-done | bytes 1048608 | tf_op jit(solution)/shard_map/all_to_all | solution.py:56
  76.9 3.6 %gather_fusion = bf16[128,2048]{1,0:T(8,128)(2,1)} fusion(bf16[256,2048]{1,0:T(8,128)(2,1)} %bitcast.17, s32[1024]{0:T(1024)S(1)} %pad_clamp_fusion), kind=kCustom, calls=%fused_computation | custom fusion | bytes 1049088 | tf_op jit(solution)/shard_map/jit(_take)/gather | solution.py:57
  80.5 1.4 %fusion.33 = bf16[16,1,2048]{2,1,0:T(2,128)(2,1)S(1)} fusion(bf16[16,8,1]{1,2,0:T(2,128)(2,1)S(1)} %copy.27, bf16[128,2048]{1,0:T(8,128)(2,1)} %gather_fusion, pred[16,8]{1,0:T(8,128)(4,1)S(1)} %get-tuple-element.2), kind=kOutput, calls=%fused_computation.24 | convolution fusion | flops 786432 | bytes 590208 | tf_op jit(solution)/shard_map/tk,tkd->td/dot_general | solution.py:60
  81.9 0.7 copy.57
  (11 shorter events, 0.1 us)
Async XLA Ops:
  0.6 40.7 %copy-start = (bf16[1,768,2048]{2,1,0:T(8,128)(2,1)S(1)}, bf16[1,768,2048]{2,1,0:T(8,128)(2,1)}, u32[]{:S(2)}) copy-start(bf16[1,768,2048]{2,1,0:T(8,128)(2,1)} %param.19) | copy-start | bytes 9437188
  0.6 11.7 %copy-start.2 = (f32[16,8]{0,1:T(8,128)S(1)}, f32[16,8]{0,1:T(8,128)}, u32[]{:S(2)}) copy-start(f32[16,8]{0,1:T(8,128)} %param.16) | copy-start | bytes 1540
  5.7 31.6 %all-to-all-start = ((bf16[16,16,2048]{2,1,0:T(8,128)(2,1)}), bf16[16,16,2048]{2,1,0:T(8,128)(2,1)}, u32[]{:S(2)}, u32[]{:S(2)}) async-start(bf16[16,16,2048]{2,1,0:T(8,128)(2,1)} %bitcast.103), calls=%async_computation | async-start | bytes 2097152 | tf_op jit(solution)/shard_map/all_to_all | solution.py:51
  41.3 10.8 %copy-start.3 = (bf16[4,512]{1,0:T(4,128)(2,1)S(1)}, bf16[4,512]{1,0:T(4,128)(2,1)}, u32[]{:S(2)}) copy-start(bf16[4,512]{1,0:T(4,128)(2,1)} %param.23) | copy-start | bytes 12292
  41.3 10.8 %copy-start.4 = (bf16[4,512]{1,0:T(4,128)(2,1)S(1)}, bf16[4,512]{1,0:T(4,128)(2,1)}, u32[]{:S(2)}) copy-start(bf16[4,512]{1,0:T(4,128)(2,1)} %param.24) | copy-start | bytes 12292
  41.4 10.8 %copy-start.5 = (s32[4]{0:T(128)S(1)}, s32[4]{0:T(128)}, u32[]{:S(2)}) copy-start(s32[4]{0:T(128)} %param.25) | copy-start | bytes 52
  41.4 10.9 %copy-start.1 = (bf16[4,4096]{1,0:T(4,128)(2,1)S(1)}, bf16[4,4096]{1,0:T(4,128)(2,1)}, u32[]{:S(2)}) copy-start(bf16[4,4096]{1,0:T(4,128)(2,1)} %param.20) | copy-start | bytes 98308
  47.0 29.9 %all-to-all-start.1 = ((bf16[16,16,2048]{2,1,0:T(8,128)(2,1)}), bf16[16,16,2048]{2,1,0:T(8,128)(2,1)}, u32[]{:S(2)}, u32[]{:S(2)}) async-start(bf16[16,16,2048]{2,1,0:T(8,128)(2,1)} %fusion.6), calls=%async_computation.1 | async-start | bytes 2097152 | tf_op jit(solution)/shard_map/all_to_all | solution.py:56
where the time goes:
time: 83.1 us; the launch traced here: 82.6 us
  waiting for transfers between devices  45.3 us (55%)
  matrix products  16.8 us (20%)
  starting transfers between devices  11.6 us (14%)
  local copies, waits for them, and re-layouts  6.09 us (7%)
  other arithmetic  2.04 us (2%)
    all_to_all x1, waiting for transfers between devices, route_block(): lax.all_to_all(outgoing, 'node', split_axis=0, concat_axis=0, tiled=True)  24.9 us
    all_to_all x1, waiting for transfers between devices, route_block(): lax.all_to_all(produced, 'node', split_axis=0, concat_axis=0, tiled=True)  20.4 us
    all_to_all x1, starting transfers between devices, route_block(): lax.all_to_all(outgoing, 'node', split_axis=0, concat_axis=0, tiled=True)  6.61 us
    dot_general x1, matrix products, expert_block(): jnp.einsum('nesf,efd->nesd', inner, w_down, preferred_element_type=jnp.fl...  5.59 us
    all_to_all x1, starting transfers between devices, route_block(): lax.all_to_all(produced, 'node', split_axis=0, concat_axis=0, tiled=True)  4.97 us
    dot_general x1, matrix products, expert_block(): jnp.einsum('nesd,edf->nesf', grouped, w_gate, preferred_element_type=jnp....  4.1 us
    gather x1, local copies, waits for them, and re-layouts, route_block(): jnp.take(returned.reshape(experts_all * capacity, features), target, axis=0)  3.62 us
    dot_general x1, matrix products, route_block(): jnp.dot(placed.astype(jnp.bfloat16), normed, preferred_element_type=jnp.f...  2.36 us
  transfers between devices with their start and end apart: 2, of which 2 were waited for; matrix products, arithmetic and copies ran while one was open for 5% of the time, Pallas kernels for 0%

commit v1 on v0

--- a/solution.py
+++ b/solution.py
@@ -60,6 +60,34 @@
     return jnp.einsum("tk,tkd->td", shares, gathered.astype(jnp.float32)).astype(jnp.bfloat16)
 
 
+def dense_block(normed, picks, gate_weights, w_gate, w_up, w_down):
+    local_experts = w_gate.shape[0]
+    node_index = lax.axis_index("node")
+    experts_all = local_experts * lax.axis_size("node")
+    shares = gate_weights / jnp.sum(gate_weights, axis=1, keepdims=True)
+    expert_ids = jnp.arange(experts_all, dtype=jnp.int32)
+    chosen = picks[:, :, None] == expert_ids[None, None, :]
+    dense_shares = jnp.sum(jnp.where(chosen, shares[:, :, None], 0.0), axis=1)
+    every_row = lax.all_gather(normed, "node", axis=0, tiled=True)
+    every_share = lax.all_gather(dense_shares, "node", axis=0, tiled=True)
+    own_shares = lax.dynamic_slice_in_dim(
+        every_share, node_index * local_experts, local_experts, axis=1
+    )
+    summed = None
+    for expert in range(local_experts):
+        gate_part = jnp.dot(every_row, w_gate[expert], preferred_element_type=jnp.float32)
+        up_part = jnp.dot(every_row, w_up[expert], preferred_element_type=jnp.float32)
+        inner = (jax.nn.silu(gate_part) * up_part).astype(jnp.bfloat16)
+        produced = jnp.dot(inner, w_down[expert], preferred_element_type=jnp.float32).astype(
+            jnp.bfloat16
+        )
+        column = own_shares[:, expert : expert + 1]
+        weighted = jnp.where(column != 0.0, column * produced.astype(jnp.float32), 0.0)
+        summed = weighted if summed is None else summed + weighted
+    total = lax.psum_scatter(summed, "node", scatter_dimension=0, tiled=True)
+    return total.astype(jnp.bfloat16)
+
+
 def attend(queries, keys, values, incoming_keys, incoming_values, lengths):
     request_rows = queries.shape[0]
     valid_length = keys.shape[1]
@@ -120,7 +148,11 @@
     normed = (widened / jnp.sqrt(meansq) * norm_gain[None, :]).astype(jnp.bfloat16)
     experts_all = w_gate.shape[0] * lax.axis_size("node")
     capacity = min(TOK_DEV, max(2, 2 * TOK_DEV * TOPK // experts_all))
-    moe_output = route_block(normed, picks, gate_weights, w_gate, w_up, w_down, capacity)
+    gathered_rows = normed.shape[0] * lax.axis_size("node")
+    if gathered_rows <= experts_all * capacity:
+        moe_output = dense_block(normed, picks, gate_weights, w_gate, w_up, w_down)
+    else:
+        moe_output = route_block(normed, picks, gate_weights, w_gate, w_up, w_down, capacity)
     attention_output = attend(queries, keys, values, incoming_keys, incoming_values, lengths)
     return (moe_output, attention_output)
 

time: 83.1 us -> 131 us (1.58)
  the two profiles are of different devices: /device:TPU:11 before, /device:TPU:0 now
where the time goes in v1:
time: 131 us; the launch traced here: 130 us
  waiting for transfers between devices  71.5 us (55%)
  blocking collectives  23.5 us (18%)
  between operations  14.1 us (11%)
  matrix products  13.3 us (10%)
  other arithmetic  6.23 us (5%)
  local copies, waits for them, and re-layouts  1.71 us (1%)
    reduce_scatter x1, waiting for transfers between devices, dense_block(): total = lax.psum_scatter(summed, 'node', scatter_dimension=0, tiled=True)  56.2 us
    all_gather x1, blocking collectives, dense_block(): every_share = lax.all_gather(dense_shares, 'node', axis=0, tiled=True)  23.5 us
    all_gather x1, waiting for transfers between devices, dense_block(): every_row = lax.all_gather(normed, 'node', axis=0, tiled=True)  15.2 us
    dot_general x1, matrix products, dense_block(): jnp.dot(inner, w_down[expert], preferred_element_type=jnp.float32)  5.91 us
    dot_general x1, matrix products, dense_block(): jnp.dot(every_row, w_gate[expert], preferred_element_type=jnp.float32)  4.07 us
  transfers between devices with their start and end apart: 2, of which 2 were waited for; matrix products, arithmetic and copies ran while one was open for 5% of the time, Pallas kernels for 0%

profile of v1, /device:TPU:0, one launch (start us, length us, event | category | flops | bytes accessed | tf_op | source)
XLA Modules:
  0.0 130.5 jit_solution(14957401448452033666)
XLA Ops:
  7.2 0.0 copy-start
  7.2 0.0 all-gather.2.cloned.1.call-start
  7.2 1.1 fusion.38
  8.4 1.6 %fusion.40 = bf16[16,2048]{1,0:T(8,128)(2,1)} fusion(bf16[16,2048]{1,0:T(8,128)(2,1)} %param.13, f32[2048]{0:T(1024)} %param.14, f32[16]{0:T(128)S(1)} %add_sqrt_fusion), kind=kLoop, calls=%fused_computation.30 | loop fusion | flops 131072 | bytes 139328 | tf_op jit(solution)/shard_map/convert_element_type | solution.py:148
  9.9 0.0 all-gather.2.cloned.1.call-update
  9.9 0.0 reduce-scatter.2.cloned.1.call-start
  10.0 0.7 reduce_sum.36
  10.7 0.7 broadcast_divide_fusion
  11.4 0.1 copy.28
  11.5 0.8 copy.27
  12.2 0.1 select_reduce_fusion
  12.3 23.5 %all_gather.6 = f32[256,16]{1,0:T(8,128)S(1)} all-gather(f32[16,16]{1,0:T(8,128)S(1)} %select_reduce_fusion), channel_id=1, replica_groups=mesh['group'=2,'node'=16] {'node'}, dimensions={0}, use_global_device_ids=true | all-gather | bytes 17408 | tf_op jit(solution)/shard_map/all_gather | solution.py:72
  35.9 0.2 dynamic-slice_reduce_fusion
  36.0 0.2 compare_reduce_fusion
  36.2 15.2 %all-gather.2.cloned.1.call-done = bf16[256,2048]{1,0:T(8,128)(2,1)} async-done(((bf16[16,2048]{1,0:T(8,128)(2,1)}), bf16[256,2048]{1,0:T(8,128)(2,1)}) %all-gather.2.cloned.1.call-update) | async-done | bytes 1048592 | tf_op jit(solution)/shard_map/all_gather | solution.py:71
  51.5 4.1 %fusion.4 = f32[256,768]{1,0:T(8,128)} fusion(bf16[256,2048]{1,0:T(8,128)(2,1)} %all-gather.2.cloned.1.call-done, bf16[1,2048,768]{2,1,0:T(8,128)(2,1)} %param.17), kind=kOutput, calls=%fused_computation.4 | convolution fusion | flops 805306368 | bytes 4980736 | tf_op jit(solution)/shard_map/dot_general | solution.py:78
  55.5 0.0 copy-done
  55.5 0.0 copy-start.2
  55.5 0.0 copy-start.3
  55.5 0.0 copy-start.4
  55.5 0.0 copy-start.1
  55.6 5.9 %fusion.15 = f32[256,2048]{1,0:T(8,128)} fusion(bf16[1,768,2048]{2,1,0:T(8,128)(2,1)S(1)} %copy-done, f32[256]{0:T(256)S(1)} %dynamic-slice_reduce_fusion, pred[256]{0:T(512)(128)(4,1)S(1)} %compare_reduce_fusion, bf16[256,2048]{1,0:T(8,128)(2,1)} %all-gather.2.cloned.1.call-done, bf16[1,2048,768]{2,1,0:T(8,128)(2,1)} %param.18, f32[256,768]{1,0:T(8,128)} %fusion.4), kind=kOutput, calls=%fused_computation.9 | convolution fusion | flops 1613889536 | bytes 10224896 | tf_op jit(solution)/shard_map/dot_general | solution.py:81
  61.5 0.0 reduce-scatter.2.cloned.1.call-update
  61.5 0.0 copy-done.2
  61.5 0.0 copy-done.3
  61.5 0.0 copy-done.4
  61.5 0.1 iota_compare_fusion.1
  61.6 0.0 copy-done.1
  61.6 0.1 fusion.46
  61.8 1.7 %fusion.55 = (f32[4,4,8]{2,1,0:T(4,128)S(1)}, f32[4,4,8,256]{3,2,1,0:T(8,128)S(1)}) fusion(bf16[1,4,32,128]{3,1,2,0:T(4,128)(2,1)S(1)} %bitcast.60, pred[4,256]{1,0:T(4,128)(4,1)S(1)} %iota_compare_fusion.1, bf16[4,256,512]{2,1,0:T(8,128)(2,1)} %param.21), kind=kOutput, calls=%fused_computation.58 | convolution fusion | flops 8486784 | bytes 1213952 | tf_op jit(solution)/shard_map/rkgd,rlkd->rkgl/dot_general | solution.py:100
  63.5 0.2 fusion.41
  63.7 1.5 %fusion.26 = bf16[1,4,32,128]{3,2,1,0:T(8,128)(2,1)S(1)} fusion(f32[4,4,8,256]{3,2,1,0:T(8,128)S(1)} %get-tuple-element.5, f32[4,4,8]{2,1,0:T(4,128)S(1)} %get-tuple-element.3, f32[4,4,8]{2,1,0:T(4,128)S(1)} %multiply_maximum_fusion, pred[4,256]{1,0:T(4,128)(4,1)S(1)} %iota_compare_fusion.1, f32[4,4,128]{2,1,0:T(4,128)S(1)} %reshape.64, ...), kind=kOutput, calls=%fused_computation.16 | convolution fusion | flops 8568832 | bytes 1223168 | tf_op jit(solution)/shard_map/rkgl,rlkd->rkgd/dot_general | solution.py:122
  65.2 0.6 copy.58
  65.9 56.2 %reduce-scatter.2.cloned.1.call-done = f32[16,2048]{1,0:T(8,128)} async-done(((f32[256,2048]{1,0:T(8,128)}), f32[16,2048]{1,0:T(8,128)}) %reduce-scatter.2.cloned.1.call-update) | async-done | bytes 131088 | tf_op jit(solution)/shard_map/reduce_scatter | solution.py:87
  122.1 1.5 %convert_element_type.49 = bf16[16,2048]{1,0:T(8,128)(2,1)} convert(f32[16,2048]{1,0:T(8,128)} %reduce-scatter.2.cloned.1.call-done) | non-fusion elementwise | flops 32768 | bytes 196608 | tf_op jit(solution)/shard_map/convert_element_type | solution.py:88
  (5 shorter events, 0.1 us)
Async XLA Ops:
  7.2 48.4 %copy-start = (bf16[1,768,2048]{2,1,0:T(8,128)(2,1)S(1)}, bf16[1,768,2048]{2,1,0:T(8,128)(2,1)}, u32[]{:S(2)}) copy-start(bf16[1,768,2048]{2,1,0:T(8,128)(2,1)} %param.19) | copy-start | bytes 9437188
  7.2 44.3 %all-gather.2.cloned.1.call-start = ((), (), s32[]{:S(2)}) async-start(), calls=%async_computation.1 | async-start | bytes 1114112 | tf_op jit(solution)/shard_map/all_gather | solution.py:71
  9.9 112.1 %reduce-scatter.2.cloned.1.call-start = ((), (), s32[]{:S(2)}) async-start(), calls=%async_computation.2 | async-start | bytes 2228224 | tf_op jit(solution)/shard_map/reduce_scatter | solution.py:87
  55.5 6.0 %copy-start.2 = (bf16[4,512]{1,0:T(4,128)(2,1)S(1)}, bf16[4,512]{1,0:T(4,128)(2,1)}, u32[]{:S(2)}) copy-start(bf16[4,512]{1,0:T(4,128)(2,1)} %param.23) | copy-start | bytes 12292
  55.5 6.0 %copy-start.3 = (bf16[4,512]{1,0:T(4,128)(2,1)S(1)}, bf16[4,512]{1,0:T(4,128)(2,1)}, u32[]{:S(2)}) copy-start(bf16[4,512]{1,0:T(4,128)(2,1)} %param.24) | copy-start | bytes 12292
  55.5 6.0 %copy-start.4 = (s32[4]{0:T(128)S(1)}, s32[4]{0:T(128)}, u32[]{:S(2)}) copy-start(s32[4]{0:T(128)} %param.25) | copy-start | bytes 52
  55.5 6.1 %copy-start.1 = (bf16[4,4096]{1,0:T(4,128)(2,1)S(1)}, bf16[4,4096]{1,0:T(4,128)(2,1)}, u32[]{:S(2)}) copy-start(bf16[4,4096]{1,0:T(4,128)(2,1)} %param.20) | copy-start | bytes 98308
Sparse Core Ops, SparseCore 0:
  10.7 40.6 all-gather.1
  61.6 60.4 reduce-scatter.1

commit v2 on v0

--- a/solution.py
+++ b/solution.py
@@ -3,17 +3,26 @@
 import jax
 import jax.numpy as jnp
 from jax import lax
-from jax.sharding import PartitionSpec as P
+from jax.sharding import Mesh, PartitionSpec as P
 
 QUERY_HEADS = 32
 KEY_VALUE_HEADS = 4
 HEAD_WIDTH = 128
 TOPK = 8
 TOK_DEV = 16
+NODE = ("chip", "core")
+
+
+def node_size():
+    return lax.axis_size("chip") * lax.axis_size("core")
+
+
+def node_index():
+    return lax.axis_index("chip") * lax.axis_size("core") + lax.axis_index("core")
 
 
 def expert_block(received, w_gate, w_up, w_down):
-    peers = lax.axis_size("node")
+    peers = node_size()
     local_experts = w_gate.shape[0]
     slot_count = received.shape[1]
     features = received.shape[2]
@@ -30,7 +39,7 @@
 def route_block(normed, picks, gate_weights, w_gate, w_up, w_down, capacity):
     rows_here = picks.shape[0]
     picks_here = picks.shape[1]
-    experts_all = w_gate.shape[0] * lax.axis_size("node")
+    experts_all = w_gate.shape[0] * node_size()
     features = normed.shape[1]
     flattened = picks.reshape(-1)
     expert_ids = jnp.arange(experts_all, dtype=jnp.int32)
@@ -48,16 +57,53 @@
     outgoing = jnp.dot(placed.astype(jnp.bfloat16), normed, preferred_element_type=jnp.float32)
     outgoing = outgoing.astype(jnp.bfloat16).reshape(experts_all, capacity, features)
     produced = expert_block(
-        lax.all_to_all(outgoing, "node", split_axis=0, concat_axis=0, tiled=True),
+        lax.all_to_all(outgoing, NODE, split_axis=0, concat_axis=0, tiled=True),
         w_gate,
         w_up,
         w_down,
     )
-    returned = lax.all_to_all(produced, "node", split_axis=0, concat_axis=0, tiled=True)
+    returned = lax.all_to_all(produced, NODE, split_axis=0, concat_axis=0, tiled=True)
     gathered = jnp.take(returned.reshape(experts_all * capacity, features), target, axis=0)
     gathered = gathered.reshape(rows_here, picks_here, features)
     shares = gate_weights / jnp.sum(gate_weights, axis=1, keepdims=True)
     return jnp.einsum("tk,tkd->td", shares, gathered.astype(jnp.float32)).astype(jnp.bfloat16)
+
+
+def spread_block(normed, picks, gate_weights, w_gate, w_up, w_down):
+    chips = lax.axis_size("chip")
+    cores = lax.axis_size("core")
+    core = lax.axis_index("core")
+    rows_here, features = normed.shape
+    local_experts = w_gate.shape[0]
+    peers = chips * cores
+    experts_all = local_experts * peers
+    spread = jnp.broadcast_to(normed[None], (chips, rows_here, features))
+    same_core = lax.all_to_all(spread, "chip", 0, 0, tiled=True)
+    other_core = lax.ppermute(same_core, "core", [(i, (i + 1) % cores) for i in range(cores)])
+    both = jnp.stack([same_core, other_core, same_core], axis=1)
+    ordered = lax.dynamic_slice_in_dim(both, core, cores, axis=1)
+    every_row = ordered.reshape(peers * rows_here, features)
+    produced = []
+    for expert in range(local_experts):
+        gate_part = jnp.dot(every_row, w_gate[expert], preferred_element_type=jnp.float32)
+        up_part = jnp.dot(every_row, w_up[expert], preferred_element_type=jnp.float32)
+        inner = (jax.nn.silu(gate_part) * up_part).astype(jnp.bfloat16)
+        produced.append(
+            jnp.dot(inner, w_down[expert], preferred_element_type=jnp.float32).astype(jnp.bfloat16)
+        )
+    produced = jnp.stack(produced, axis=0).reshape(local_experts, peers, rows_here, features)
+    produced = produced.transpose(1, 0, 2, 3)
+    returned = lax.all_to_all(produced, NODE, 0, 0, tiled=True)
+    returned = returned.reshape(experts_all, rows_here, features)
+    shares = gate_weights / jnp.sum(gate_weights, axis=1, keepdims=True)
+    expert_ids = jnp.arange(experts_all, dtype=jnp.int32)
+    chosen = picks[:, :, None] == expert_ids[None, None, :]
+    dense_shares = jnp.sum(jnp.where(chosen, shares[:, :, None], 0.0), axis=1)
+    picked = jnp.any(chosen, axis=1)
+    weighted = jnp.where(
+        picked.T[:, :, None], dense_shares.T[:, :, None] * returned.astype(jnp.float32), 0.0
+    )
+    return jnp.sum(weighted, axis=0).astype(jnp.bfloat16)
 
 
 def attend(queries, keys, values, incoming_keys, incoming_values, lengths):
@@ -118,30 +164,37 @@
     widened = states.astype(jnp.float32)
     meansq = jnp.mean(widened * widened, axis=1, keepdims=True) + 1e-06
     normed = (widened / jnp.sqrt(meansq) * norm_gain[None, :]).astype(jnp.bfloat16)
-    experts_all = w_gate.shape[0] * lax.axis_size("node")
+    experts_all = w_gate.shape[0] * node_size()
     capacity = min(TOK_DEV, max(2, 2 * TOK_DEV * TOPK // experts_all))
-    moe_output = route_block(normed, picks, gate_weights, w_gate, w_up, w_down, capacity)
+    gathered_rows = normed.shape[0] * node_size()
+    if gathered_rows <= experts_all * capacity and lax.axis_size("core") == 2:
+        moe_output = spread_block(normed, picks, gate_weights, w_gate, w_up, w_down)
+    else:
+        moe_output = route_block(normed, picks, gate_weights, w_gate, w_up, w_down, capacity)
     attention_output = attend(queries, keys, values, incoming_keys, incoming_values, lengths)
     return (moe_output, attention_output)
 
 
 def solution(mesh):
+    groups, peers = mesh.devices.shape
+    cores = 2 if peers % 2 == 0 else 1
+    fine = Mesh(mesh.devices.reshape(groups, peers // cores, cores), ("group", "chip", "core"))
     in_specs = (
-        P(("group", "node"), None),
+        P(("group", "chip", "core"), None),
         P(),
-        P(("group", "node"), None),
-        P(("group", "node"), None),
-        P("node", None, None),
-        P("node", None, None),
-        P("node", None, None),
-        P(("group", "node"), None),
-        P(("group", "node"), None, None),
-        P(("group", "node"), None, None),
-        P(("group", "node"), None),
-        P(("group", "node"), None),
-        P(("group", "node")),
-    )
-    out_specs = (P(("group", "node"), None), P(("group", "node"), None))
+        P(("group", "chip", "core"), None),
+        P(("group", "chip", "core"), None),
+        P(NODE, None, None),
+        P(NODE, None, None),
+        P(NODE, None, None),
+        P(("group", "chip", "core"), None),
+        P(("group", "chip", "core"), None, None),
+        P(("group", "chip", "core"), None, None),
+        P(("group", "chip", "core"), None),
+        P(("group", "chip", "core"), None),
+        P(("group", "chip", "core")),
+    )
+    out_specs = (P(("group", "chip", "core"), None), P(("group", "chip", "core"), None))
     return jax.shard_map(
-        on_device, mesh=mesh, in_specs=in_specs, out_specs=out_specs, check_vma=False
-    )
+        on_device, mesh=fine, in_specs=in_specs, out_specs=out_specs, check_vma=False
+    )

time: 83.1 us -> 70 us (0.84)
  waiting for transfers between devices: 45.3 us -> 21.2 us
  blocking collectives: 0 us -> 18.3 us
  other arithmetic: 2.04 us -> 7.17 us
  starting transfers between devices: 11.6 us -> 7.33 us
  matrix products: 16.8 us -> 12.7 us
  local copies, waits for them, and re-layouts: 6.09 us -> 2.08 us
    all_to_all x2 -> x1, waiting for transfers between devices: 45.3 us -> 20.1 us  [spread_block(): returned = lax.all_to_all(produced, NODE, 0, 0, tiled=True)]
    all_to_all x0 -> x1, blocking collectives: none -> 18.3 us  [spread_block(): same_core = lax.all_to_all(spread, 'chip', 0, 0, tiled=True)]
    all_to_all x2 -> x1, starting transfers between devices: 11.6 us -> 5.17 us  [spread_block(): returned = lax.all_to_all(produced, NODE, 0, 0, tiled=True)]
    dot_general x4 -> x2, matrix products: 13.4 us -> 9.34 us  [the longest x1 5.55 us: spread_block(): jnp.dot(inner, w_down[expert], preferred_element_type=jnp.float32)]
    gather x1 -> x0, local copies, waits for them, and re-layouts: 3.62 us -> none  [route_block(): jnp.take(returned.reshape(experts_all * capacity, features), target, axis=0)]
    reduce_sum x3, other arithmetic: 0.3 us -> 3.03 us  [the longest x1 2.21 us: spread_block(): return jnp.sum(weighted, axis=0).astype(jnp.bfloat16)]
    ppermute x0 -> x1, starting transfers between devices: none -> 2.16 us  [spread_block(): lax.ppermute(same_core, 'core', [(i, (i + 1) % cores) for i in range(core...]
    another operation x1, other arithmetic: 0.17 us -> 1.67 us  [spread_block(): both = jnp.stack([same_core, other_core, same_core], axis=1)]
  transfers between devices with their start and end apart: 2 -> 2, of which waited for: 2 -> 2; matrix products, arithmetic and copies ran while one was open for 5% -> 8% of each run, Pallas kernels for 0% -> 0%
where the time goes in v2:
time: 70 us; the launch traced here: 69.6 us
  waiting for transfers between devices  21.2 us (30%)
  blocking collectives  18.3 us (26%)
  matrix products  12.7 us (18%)
  starting transfers between devices  7.33 us (10%)
  other arithmetic  7.17 us (10%)
  local copies, waits for them, and re-layouts  2.08 us (3%)
  between operations  0.76 us (1%)
    all_to_all x1, waiting for transfers between devices, spread_block(): returned = lax.all_to_all(produced, NODE, 0, 0, tiled=True)  20.1 us
    all_to_all x1, blocking collectives, spread_block(): same_core = lax.all_to_all(spread, 'chip', 0, 0, tiled=True)  18.3 us
    dot_general x1, matrix products, spread_block(): jnp.dot(inner, w_down[expert], preferred_element_type=jnp.float32)  5.55 us
    all_to_all x1, starting transfers between devices, spread_block(): returned = lax.all_to_all(produced, NODE, 0, 0, tiled=True)  5.17 us
    dot_general x1, matrix products, spread_block(): jnp.dot(every_row, w_gate[expert], preferred_element_type=jnp.float32)  3.78 us
    reduce_sum x1, other arithmetic, spread_block(): return jnp.sum(weighted, axis=0).astype(jnp.bfloat16)  2.21 us
    ppermute x1, starting transfers between devices, spread_block(): lax.ppermute(same_core, 'core', [(i, (i + 1) % cores) for i in range(core...  2.16 us
    unnamed x18, local copies, waits for them, and re-layouts  1.78 us
  transfers between devices with their start and end apart: 2, of which 2 were waited for; matrix products, arithmetic and copies ran while one was open for 8% of the time, Pallas kernels for 0%

profile of v2, /device:TPU:11, one launch (start us, length us, event | category | flops | bytes accessed | tf_op | source)
XLA Modules:
  0.0 69.6 jit_solution(15123195806752783420)
XLA Ops:
  0.6 0.0 copy-start
  0.6 1.1 %fusion.29 = f32[16]{0:T(128)S(1)} fusion(bf16[16,2048]{1,0:T(8,128)(2,1)} %param.13), kind=kLoop, calls=%fused_computation.29 | loop fusion | flops 98288 | bytes 65600 | tf_op jit(solution)/shard_map/reduce_sum | solution.py:165
  1.8 0.9 %fusion.31 = bf16[16,2048]{1,0:T(8,128)(2,1)S(1)} fusion(bf16[16,2048]{1,0:T(8,128)(2,1)} %param.13, f32[2048]{0:T(1024)} %param.14, f32[16]{0:T(128)S(1)} %add_sqrt_fusion), kind=kLoop, calls=%fused_computation.31 | loop fusion | flops 131072 | bytes 139328 | tf_op jit(solution)/shard_map/convert_element_type | solution.py:166
  2.8 18.3 %all_to_all.10 = bf16[8,16,2048]{2,1,0:T(8,128)(2,1)} all-to-all(bf16[8,16,2048]{2,1,0:T(8,128)(2,1)S(1)} %broadcast_in_dim.65), channel_id=1, replica_groups=mesh['group'=2,'chip'=8,'core'=2] {'chip'}, dimensions={0} | all-to-all | bytes 1048576 | tf_op jit(solution)/shard_map/all_to_all | solution.py:81
  21.1 2.2 %collective-permute-start = (bf16[8,16,2048]{2,1,0:T(8,128)(2,1)}, bf16[8,16,2048]{2,1,0:T(8,128)(2,1)}, u32[]{:S(2)}, u32[]{:S(2)}) collective-permute-start(bf16[8,16,2048]{2,1,0:T(8,128)(2,1)} %all_to_all.10), channel_id=1, source_target_pairs={{0,1},{1,0},{2,3},{3,2},{4,5},{5,4},{6,7},{7,6},{8,9},{9,8},{10,11... | collective-permute-start | bytes 1572872 | tf_op jit(solution)/shard_map/ppermute | solution.py:82
  23.2 0.7 %reduce_sum.45 = f32[16]{0:T(128)S(1)} reduce(f32[16,8]{0,1:T(8,128)} %param.16, f32[]{:T(128)} %constant.12.clone.1), dimensions={1}, to_apply=%region_1.2 | reduce | flops 112 | bytes 580 | tf_op jit(solution)/shard_map/reduce_sum | solution.py:98
  23.9 1.2 %collective-permute-done = bf16[8,16,2048]{2,1,0:T(8,128)(2,1)} collective-permute-done((bf16[8,16,2048]{2,1,0:T(8,128)(2,1)}, bf16[8,16,2048]{2,1,0:T(8,128)(2,1)}, u32[]{:S(2)}, u32[]{:S(2)}) %collective-permute-start) | collective-permute-done | bytes 524320 | tf_op jit(solution)/shard_map/ppermute | solution.py:82
  25.1 1.7 %fusion.21 = bf16[8,2,16,2048]{3,2,1,0:T(8,128)(2,1)S(1)} fusion(s32[]{:T(128)S(6)} %select_n.19, bf16[8,1,16,2048]{3,2,1,0:T(8,128)(2,1)} %bitcast.2, bf16[8,1,16,2048]{3,2,1,0:T(8,128)(2,1)} %bitcast.4), kind=kLoop, calls=%fused_computation.21 | loop fusion | flops 1048576 | bytes 2097156 | tf_op jit(solution)/shard_map/stack | solution.py:83
  26.8 0.0 copy-start.1
  26.8 1.0 %copy-done.1 = bf16[8,2,16,2048]{3,2,1,0:T(8,128)(2,1)} copy-done((bf16[8,2,16,2048]{3,2,1,0:T(8,128)(2,1)}, bf16[8,2,16,2048]{3,2,1,0:T(8,128)(2,1)S(1)}, u32[]{:S(2)}) %copy-start.1) | copy-done | bytes 1048600
  27.8 3.8 %fusion.4 = f32[256,768]{1,0:T(8,128)} fusion(bf16[256,2048]{1,0:T(8,128)(2,1)S(1)} %bitcast.66, bf16[1,2048,768]{2,1,0:T(8,128)(2,1)} %param.17), kind=kOutput, calls=%fused_computation.4 | convolution fusion | flops 805306368 | bytes 4980736 | tf_op jit(solution)/shard_map/dot_general | solution.py:88
  31.6 0.0 copy-done
  31.6 0.0 copy-start.3
  31.6 0.0 copy-start.4
  31.6 0.0 copy-start.5
  31.6 0.0 copy-start.6
  31.6 0.0 copy-start.7
  31.7 0.0 copy-start.2
  31.7 5.6 %fusion.6 = bf16[256,2048]{1,0:T(8,128)(2,1)} fusion(bf16[1,768,2048]{2,1,0:T(8,128)(2,1)S(1)} %copy-done, bf16[256,2048]{1,0:T(8,128)(2,1)} %bitcast.67, bf16[1,2048,768]{2,1,0:T(8,128)(2,1)} %param.18, f32[256,768]{1,0:T(8,128)} %fusion.4), kind=kOutput, calls=%fused_computation.6 | convolution fusion | flops 1612316672 | bytes 9175040 | tf_op jit(solution)/shard_map/dot_general | solution.py:92
  37.2 5.2 %all-to-all-start.1 = ((bf16[16,1,16,2048]{3,2,1,0:T(8,128)(2,1)}), bf16[16,1,16,2048]{3,2,1,0:T(8,128)(2,1)}, u32[]{:S(2)}, u32[]{:S(2)}) async-start(bf16[16,1,16,2048]{3,2,1,0:T(8,128)(2,1)} %bitcast.68), calls=%async_computation.1 | async-start | bytes 2097152 | tf_op jit(solution)/shard_map/all_to_all | solution.py:96
  42.4 0.0 copy-done.3
  42.4 0.1 copy.32
  42.5 0.0 copy-done.4
  42.5 0.1 copy.30
  42.6 0.1 select_reduce_fusion
  42.7 0.1 copy.33
  42.7 0.1 fusion.36
  42.9 0.1 copy.31
  42.9 0.0 copy-done.5
  43.0 0.0 copy-done.6
  43.0 0.0 copy-done.7
  43.0 0.1 iota_compare_fusion.1
  43.1 0.0 copy-done.2
  43.1 0.1 fusion.38
  43.2 1.7 %fusion.47 = (f32[4,4,8]{2,1,0:T(4,128)S(1)}, f32[4,4,8,256]{3,2,1,0:T(8,128)S(1)}) fusion(bf16[1,4,32,128]{3,1,2,0:T(4,128)(2,1)S(1)} %bitcast.70, pred[4,256]{1,0:T(4,128)(4,1)S(1)} %iota_compare_fusion.1, bf16[4,256,512]{2,1,0:T(8,128)(2,1)} %param.21), kind=kOutput, calls=%fused_computation.58 | convolution fusion | flops 8486784 | bytes 1213952 | tf_op jit(solution)/shard_map/rkgd,rlkd->rkgl/dot_general | solution.py:118
  44.9 0.2 fusion.32
  45.1 1.5 %fusion.19 = bf16[1,4,32,128]{3,2,1,0:T(8,128)(2,1)S(1)} fusion(f32[4,4,8,256]{3,2,1,0:T(8,128)S(1)} %get-tuple-element.5, f32[4,4,8]{2,1,0:T(4,128)S(1)} %get-tuple-element.3, f32[4,4,8]{2,1,0:T(4,128)S(1)} %multiply_maximum_fusion, pred[4,256]{1,0:T(4,128)(4,1)S(1)} %iota_compare_fusion.1, f32[4,4,128]{2,1,0:T(4,128)S(1)} %reshape.75, ...), kind=kOutput, calls=%fused_computation.19 | convolution fusion | flops 8568832 | bytes 1223168 | tf_op jit(solution)/shard_map/rkgl,rlkd->rkgd/dot_general | solution.py:140
  46.7 0.6 copy.65
  47.3 20.1 %all-to-all-done.1 = bf16[16,1,16,2048]{3,2,1,0:T(8,128)(2,1)} async-done(((bf16[16,1,16,2048]{3,2,1,0:T(8,128)(2,1)}), bf16[16,1,16,2048]{3,2,1,0:T(8,128)(2,1)}, u32[]{:S(2)}, u32[]{:S(2)}) %all-to-all-start.1) | async-done | bytes 1048608 | tf_op jit(solution)/shard_map/all_to_all | solution.py:96
  67.4 2.2 %fusion.10 = bf16[16,2048]{1,0:T(8,128)(2,1)} fusion(bf16[16,1,16,2048]{3,2,1,0:T(8,128)(2,1)} %all-to-all-done.1, f32[16,16]{1,0:T(8,128)S(1)} %copy.33, pred[16,16]{1,0:T(8,128)(4,1)S(1)} %copy.31), kind=kLoop, calls=%fused_computation.9 | loop fusion | flops 2064384 | bytes 1115392 | tf_op jit(solution)/shard_map/reduce_sum | solution.py:106
  (7 shorter events, 0.1 us)
Async XLA Ops:
  0.6 31.0 %copy-start = (bf16[1,768,2048]{2,1,0:T(8,128)(2,1)S(1)}, bf16[1,768,2048]{2,1,0:T(8,128)(2,1)}, u32[]{:S(2)}) copy-start(bf16[1,768,2048]{2,1,0:T(8,128)(2,1)} %param.19) | copy-start | bytes 9437188
  21.1 4.0 %collective-permute-start = (bf16[8,16,2048]{2,1,0:T(8,128)(2,1)}, bf16[8,16,2048]{2,1,0:T(8,128)(2,1)}, u32[]{:S(2)}, u32[]{:S(2)}) collective-permute-start(bf16[8,16,2048]{2,1,0:T(8,128)(2,1)} %all_to_all.10), channel_id=1, source_target_pairs={{0,1},{1,0},{2,3},{3,2},{4,5},{5,4},{6,7},{7,6},{8,9},{9,8},{10,11... | collective-permute-start | bytes 1572872 | tf_op jit(solution)/shard_map/ppermute | solution.py:82
  26.8 1.0 %copy-start.1 = (bf16[8,2,16,2048]{3,2,1,0:T(8,128)(2,1)}, bf16[8,2,16,2048]{3,2,1,0:T(8,128)(2,1)S(1)}, u32[]{:S(2)}) copy-start(bf16[8,2,16,2048]{3,2,1,0:T(8,128)(2,1)S(1)} %fusion.21) | copy-start | bytes 3145732
  31.6 10.8 %copy-start.3 = (f32[16,8]{0,1:T(8,128)S(1)}, f32[16,8]{0,1:T(8,128)}, u32[]{:S(2)}) copy-start(f32[16,8]{0,1:T(8,128)} %param.16) | copy-start | bytes 1540
  31.6 10.9 %copy-start.4 = (s32[16,8]{0,1:T(8,128)S(1)}, s32[16,8]{0,1:T(8,128)}, u32[]{:S(2)}) copy-start(s32[16,8]{0,1:T(8,128)} %param.15) | copy-start | bytes 1540
  31.6 11.3 %copy-start.5 = (bf16[4,512]{1,0:T(4,128)(2,1)S(1)}, bf16[4,512]{1,0:T(4,128)(2,1)}, u32[]{:S(2)}) copy-start(bf16[4,512]{1,0:T(4,128)(2,1)} %param.23) | copy-start | bytes 12292
  31.6 11.3 %copy-start.6 = (bf16[4,512]{1,0:T(4,128)(2,1)S(1)}, bf16[4,512]{1,0:T(4,128)(2,1)}, u32[]{:S(2)}) copy-start(bf16[4,512]{1,0:T(4,128)(2,1)} %param.24) | copy-start | bytes 12292
  31.6 11.3 %copy-start.7 = (s32[4]{0:T(128)S(1)}, s32[4]{0:T(128)}, u32[]{:S(2)}) copy-start(s32[4]{0:T(128)} %param.25) | copy-start | bytes 52
  31.7 11.4 %copy-start.2 = (bf16[4,4096]{1,0:T(4,128)(2,1)S(1)}, bf16[4,4096]{1,0:T(4,128)(2,1)}, u32[]{:S(2)}) copy-start(bf16[4,4096]{1,0:T(4,128)(2,1)} %param.20) | copy-start | bytes 98308
  37.2 30.2 %all-to-all-start.1 = ((bf16[16,1,16,2048]{3,2,1,0:T(8,128)(2,1)}), bf16[16,1,16,2048]{3,2,1,0:T(8,128)(2,1)}, u32[]{:S(2)}, u32[]{:S(2)}) async-start(bf16[16,1,16,2048]{3,2,1,0:T(8,128)(2,1)} %bitcast.68), calls=%async_computation.1 | async-start | bytes 2097152 | tf_op jit(solution)/shard_map/all_to_all | solution.py:96

commit v3 on v2

--- a/solution.py
+++ b/solution.py
@@ -3,6 +3,8 @@
 import jax
 import jax.numpy as jnp
 from jax import lax
+from jax.experimental import pallas as pl
+from jax.experimental.pallas import tpu as pltpu
 from jax.sharding import Mesh, PartitionSpec as P
 
 QUERY_HEADS = 32
@@ -69,6 +71,46 @@
     return jnp.einsum("tk,tkd->td", shares, gathered.astype(jnp.float32)).astype(jnp.bfloat16)
 
 
+def mlp_kernel(rows_ref, gate_ref, up_ref, down_ref, out_ref, acc_ref):
+    step = pl.program_id(1)
+
+    @pl.when(step == 0)
+    def _():
+        acc_ref[...] = jnp.zeros_like(acc_ref)
+
+    rows = rows_ref[...]
+    gate_part = jnp.dot(rows, gate_ref[...], preferred_element_type=jnp.float32)
+    up_part = jnp.dot(rows, up_ref[...], preferred_element_type=jnp.float32)
+    inner = (jax.nn.silu(gate_part) * up_part).astype(jnp.bfloat16)
+    acc_ref[...] += jnp.dot(inner, down_ref[...], preferred_element_type=jnp.float32)
+
+    @pl.when(step == pl.num_programs(1) - 1)
+    def _():
+        out_ref[...] = acc_ref[...].astype(out_ref.dtype)
+
+
+def expert_mlp(every_row, w_gate, w_up, w_down):
+    local_experts, features, hidden = w_gate.shape
+    row_count = every_row.shape[0]
+    chunk = 256 if hidden % 256 == 0 else hidden
+    return pl.pallas_call(
+        mlp_kernel,
+        grid=(local_experts, hidden // chunk),
+        in_specs=[
+            pl.BlockSpec((row_count, features), lambda e, f: (0, 0)),
+            pl.BlockSpec((None, features, chunk), lambda e, f: (e, 0, f)),
+            pl.BlockSpec((None, features, chunk), lambda e, f: (e, 0, f)),
+            pl.BlockSpec((None, chunk, features), lambda e, f: (e, f, 0)),
+        ],
+        out_specs=pl.BlockSpec((None, row_count, features), lambda e, f: (e, 0, 0)),
+        out_shape=jax.ShapeDtypeStruct((local_experts, row_count, features), jnp.bfloat16),
+        scratch_shapes=[pltpu.VMEM((row_count, features), jnp.float32)],
+        compiler_params=pltpu.CompilerParams(
+            dimension_semantics=("arbitrary", "arbitrary"), vmem_limit_bytes=48 * 1024 * 1024
+        ),
+    )(every_row, w_gate, w_up, w_down)
+
+
 def spread_block(normed, picks, gate_weights, w_gate, w_up, w_down):
     chips = lax.axis_size("chip")
     cores = lax.axis_size("core")
@@ -83,15 +125,8 @@
     both = jnp.stack([same_core, other_core, same_core], axis=1)
     ordered = lax.dynamic_slice_in_dim(both, core, cores, axis=1)
     every_row = ordered.reshape(peers * rows_here, features)
-    produced = []
-    for expert in range(local_experts):
-        gate_part = jnp.dot(every_row, w_gate[expert], preferred_element_type=jnp.float32)
-        up_part = jnp.dot(every_row, w_up[expert], preferred_element_type=jnp.float32)
-        inner = (jax.nn.silu(gate_part) * up_part).astype(jnp.bfloat16)
-        produced.append(
-            jnp.dot(inner, w_down[expert], preferred_element_type=jnp.float32).astype(jnp.bfloat16)
-        )
-    produced = jnp.stack(produced, axis=0).reshape(local_experts, peers, rows_here, features)
+    produced = expert_mlp(every_row, w_gate, w_up, w_down)
+    produced = produced.reshape(local_experts, peers, rows_here, features)
     produced = produced.transpose(1, 0, 2, 3)
     returned = lax.all_to_all(produced, NODE, 0, 0, tiled=True)
     returned = returned.reshape(experts_all, rows_here, features)
@@ -99,10 +134,7 @@
     expert_ids = jnp.arange(experts_all, dtype=jnp.int32)
     chosen = picks[:, :, None] == expert_ids[None, None, :]
     dense_shares = jnp.sum(jnp.where(chosen, shares[:, :, None], 0.0), axis=1)
-    picked = jnp.any(chosen, axis=1)
-    weighted = jnp.where(
-        picked.T[:, :, None], dense_shares.T[:, :, None] * returned.astype(jnp.float32), 0.0
-    )
+    weighted = dense_shares.T[:, :, None] * returned.astype(jnp.float32)
     return jnp.sum(weighted, axis=0).astype(jnp.bfloat16)
 
 

time: 70 us -> 64.5 us (0.921)
  matrix products: 12.7 us -> 0.91 us
  Pallas kernels: 0 us -> 6.63 us
  other arithmetic: 7.17 us -> 3.83 us
  waiting for transfers between devices: 21.2 us -> 24.1 us
  local copies, waits for them, and re-layouts: 2.08 us -> 2.86 us
    dot_general x2 -> x0, matrix products: 9.34 us -> none  [the longest x1 5.55 us: spread_block(): jnp.dot(inner, w_down[expert], preferred_element_type=jnp.float32)]
    pallas_call x0 -> x1, Pallas kernels: none -> 6.63 us  [expert_mlp(): pl.pallas_call(mlp_kernel, grid=(local_experts, hidden // chunk), in_spec...]
    all_to_all x1, waiting for transfers between devices: 20.1 us -> 22.5 us  [spread_block(): returned = lax.all_to_all(produced, NODE, 0, 0, tiled=True)]
    reduce_sum x1, other arithmetic: 2.21 us -> 0.89 us  [spread_block(): return jnp.sum(weighted, axis=0).astype(jnp.bfloat16)]
    dot_general x1, matrix products: 1.69 us -> 0.47 us  [attend(): jnp.einsum('rkgd,rlkd->rkgl', query_rows, stored_keys, preferred_element_...]
    dot_general x1, matrix products: 1.53 us -> 0.31 us  [attend(): jnp.einsum('rkgl,rlkd->rkgd', probs, stored_values, preferred_element_typ...]
    another operation x1, other arithmetic: 1.67 us -> 0.5 us  [spread_block(): both = jnp.stack([same_core, other_core, same_core], axis=1)]
    unnamed x18 -> x20, local copies, waits for them, and re-layouts: 1.78 us -> 2.65 us
  transfers between devices with their start and end apart: 2 -> 2, of which waited for: 2 -> 2; matrix products, arithmetic and copies ran while one was open for 8% -> 3% of each run, Pallas kernels for 0% -> 0%
where the time goes in v3:
time: 64.5 us; the launch traced here: 64.1 us
  waiting for transfers between devices  24.1 us (37%)
  blocking collectives  18.2 us (28%)
  starting transfers between devices  6.84 us (11%)
  Pallas kernels  6.63 us (10%)
  other arithmetic  3.83 us (6%)
  local copies, waits for them, and re-layouts  2.86 us (4%)
  matrix products  0.91 us (1%)
  between operations  0.76 us (1%)
    all_to_all x1, waiting for transfers between devices, spread_block(): returned = lax.all_to_all(produced, NODE, 0, 0, tiled=True)  22.5 us
    all_to_all x1, blocking collectives, spread_block(): same_core = lax.all_to_all(spread, 'chip', 0, 0, tiled=True)  18.2 us
    pallas_call x1, Pallas kernels, expert_mlp(): pl.pallas_call(mlp_kernel, grid=(local_experts, hidden // chunk), in_spec...  6.63 us
    all_to_all x1, starting transfers between devices, spread_block(): returned = lax.all_to_all(produced, NODE, 0, 0, tiled=True)  4.68 us
    unnamed x20, local copies, waits for them, and re-layouts  2.65 us
    ppermute x1, starting transfers between devices, spread_block(): lax.ppermute(same_core, 'core', [(i, (i + 1) % cores) for i in range(core...  2.16 us
    ppermute x1, waiting for transfers between devices, spread_block(): lax.ppermute(same_core, 'core', [(i, (i + 1) % cores) for i in range(core...  1.54 us
  transfers between devices with their start and end apart: 2, of which 2 were waited for; matrix products, arithmetic and copies ran while one was open for 3% of the time, Pallas kernels for 0%

profile of v3, /device:TPU:11, one launch (start us, length us, event | category | flops | bytes accessed | tf_op | source)
XLA Modules:
  0.0 64.1 jit_solution(1037356271330924143)
XLA Ops:
  0.6 0.0 copy-start
  0.6 1.1 %fusion.10 = f32[16]{0:T(128)S(1)} fusion(bf16[16,2048]{1,0:T(8,128)(2,1)} %param.13), kind=kLoop, calls=%fused_computation.18 | loop fusion | flops 98288 | bytes 65600 | tf_op jit(solution)/shard_map/reduce_sum | solution.py:197
  1.7 0.9 %fusion.12 = bf16[16,2048]{1,0:T(8,128)(2,1)S(1)} fusion(bf16[16,2048]{1,0:T(8,128)(2,1)} %param.13, f32[2048]{0:T(1024)} %param.14, f32[16]{0:T(128)S(1)} %add_sqrt_fusion), kind=kLoop, calls=%fused_computation.20 | loop fusion | flops 131072 | bytes 139328 | tf_op jit(solution)/shard_map/convert_element_type | solution.py:198
  2.7 18.2 %all_to_all.10 = bf16[8,16,2048]{2,1,0:T(8,128)(2,1)S(1)} all-to-all(bf16[8,16,2048]{2,1,0:T(8,128)(2,1)S(1)} %broadcast_in_dim.51), channel_id=1, replica_groups=mesh['group'=2,'chip'=8,'core'=2] {'chip'}, dimensions={0} | all-to-all | bytes 1048576 | tf_op jit(solution)/shard_map/all_to_all | solution.py:123
  20.9 2.2 %collective-permute-start = (bf16[8,16,2048]{2,1,0:T(8,128)(2,1)S(1)}, bf16[8,16,2048]{2,1,0:T(8,128)(2,1)S(1)}, u32[]{:S(2)}, u32[]{:S(2)}) collective-permute-start(bf16[8,16,2048]{2,1,0:T(8,128)(2,1)S(1)} %all_to_all.10), channel_id=1, source_target_pairs={{0,1},{1,0},{2,3},{3,2},{4,5},{5,4},{6,7},{7,6},{8,9},{9,8},{10,11... | collective-permute-start | bytes 1572872 | tf_op jit(solution)/shard_map/ppermute | solution.py:124
  23.1 1.5 %collective-permute-done = bf16[8,16,2048]{2,1,0:T(8,128)(2,1)S(1)} collective-permute-done((bf16[8,16,2048]{2,1,0:T(8,128)(2,1)S(1)}, bf16[8,16,2048]{2,1,0:T(8,128)(2,1)S(1)}, u32[]{:S(2)}, u32[]{:S(2)}) %collective-permute-start) | collective-permute-done | bytes 524320 | tf_op jit(solution)/shard_map/ppermute | solution.py:124
  24.6 0.5 fusion.5
  25.1 0.0 copy-start.1
  25.1 1.9 %copy-done.1 = bf16[1,2048,768]{2,1,0:T(8,128)(2,1)S(1)} copy-done((bf16[1,2048,768]{2,1,0:T(8,128)(2,1)S(1)}, bf16[1,2048,768]{2,1,0:T(8,128)(2,1)}, u32[]{:S(2)}) %copy-start.1) | copy-done | bytes 3145752
  27.0 6.6 %shard_map.140 = bf16[1,256,2048]{2,1,0:T(8,128)(2,1)} custom-call(bf16[256,2048]{1,0:T(8,128)(2,1)S(1)} %bitcast.46, bf16[1,2048,768]{2,1,0:T(8,128)(2,1)S(1)} %copy-done.1, bf16[1,2048,768]{2,1,0:T(8,128)(2,1)} %up_ref.1, bf16[1,768,2048]{2,1,0:T(8,128)(2,1)} %down_ref.1), custom_call_target="tpu_custom_call" | custom-call | tf_op jit(solution)/shard_map/pallas_call | solution.py:96
  33.6 0.0 copy-start.3
  33.6 0.0 copy-start.4
  33.6 0.0 copy-start.5
  33.6 0.0 copy-start.6
  33.7 0.0 copy-start.8
  33.7 0.0 copy-start.2
  33.7 0.0 copy-start.7
  33.7 4.7 %all-to-all-start.1 = ((bf16[16,1,16,2048]{3,2,1,0:T(8,128)(2,1)}), bf16[16,1,16,2048]{3,2,1,0:T(8,128)(2,1)S(1)}, u32[]{:S(2)}, u32[]{:S(2)}) async-start(bf16[16,1,16,2048]{3,2,1,0:T(8,128)(2,1)} %bitcast.6), calls=%async_computation.1 | async-start | bytes 2097152 | tf_op jit(solution)/shard_map/all_to_all | solution.py:131
  38.4 0.0 copy-done.3
  38.4 0.1 copy.27
  38.5 0.0 copy-done.4
  38.5 0.1 copy.26
  38.6 0.1 select_reduce_fusion
  38.7 0.1 copy.28
  38.8 0.0 copy-done.5
  38.8 0.0 copy-done.6
  38.8 0.0 copy-done.8
  38.8 0.1 iota_compare_fusion.1
  38.9 0.0 copy-done.2
  38.9 0.1 fusion.18
  39.0 0.0 copy-done
  39.0 0.5 fusion.26
  39.5 0.2 fusion.13
  39.7 0.0 copy-done.7
  39.7 0.3 fusion.3
  40.0 0.6 %copy.60 = bf16[1,4,32,128]{3,1,2,0:T(4,128)(2,1)} copy(bf16[1,4,32,128]{3,2,1,0:T(8,128)(2,1)S(1)} %fusion.3) | data formatting | bytes 65536
  40.7 22.5 %all-to-all-done.1 = bf16[16,1,16,2048]{3,2,1,0:T(8,128)(2,1)S(1)} async-done(((bf16[16,1,16,2048]{3,2,1,0:T(8,128)(2,1)}), bf16[16,1,16,2048]{3,2,1,0:T(8,128)(2,1)S(1)}, u32[]{:S(2)}, u32[]{:S(2)}) %all-to-all-start.1) | async-done | bytes 1048608 | tf_op jit(solution)/shard_map/all_to_all | solution.py:131
  63.2 0.9 %fusion = bf16[16,2048]{1,0:T(8,128)(2,1)} fusion(bf16[16,1,16,2048]{3,2,1,0:T(8,128)(2,1)S(1)} %all-to-all-done.1, f32[16,16]{1,0:T(8,128)S(1)} %copy.28), kind=kLoop, calls=%fused_computation.1 | loop fusion | flops 1540096 | bytes 1115136 | tf_op jit(solution)/shard_map/reduce_sum | solution.py:138
  (8 shorter events, 0.1 us)
Async XLA Ops:
  0.6 38.4 %copy-start = (bf16[4,256,512]{2,1,0:T(8,128)(2,1)S(1)}, bf16[4,256,512]{2,1,0:T(8,128)(2,1)}, u32[]{:S(2)}) copy-start(bf16[4,256,512]{2,1,0:T(8,128)(2,1)} %param.21) | copy-start | bytes 3145732
  20.9 3.7 %collective-permute-start = (bf16[8,16,2048]{2,1,0:T(8,128)(2,1)S(1)}, bf16[8,16,2048]{2,1,0:T(8,128)(2,1)S(1)}, u32[]{:S(2)}, u32[]{:S(2)}) collective-permute-start(bf16[8,16,2048]{2,1,0:T(8,128)(2,1)S(1)} %all_to_all.10), channel_id=1, source_target_pairs={{0,1},{1,0},{2,3},{3,2},{4,5},{5,4},{6,7},{7,6},{8,9},{9,8},{10,11... | collective-permute-start | bytes 1572872 | tf_op jit(solution)/shard_map/ppermute | solution.py:124
  25.1 1.9 %copy-start.1 = (bf16[1,2048,768]{2,1,0:T(8,128)(2,1)S(1)}, bf16[1,2048,768]{2,1,0:T(8,128)(2,1)}, u32[]{:S(2)}) copy-start(bf16[1,2048,768]{2,1,0:T(8,128)(2,1)} %gate_ref.1) | copy-start | bytes 9437188
  33.6 4.7 %copy-start.3 = (f32[16,8]{0,1:T(8,128)S(1)}, f32[16,8]{0,1:T(8,128)}, u32[]{:S(2)}) copy-start(f32[16,8]{0,1:T(8,128)} %param.16) | copy-start | bytes 1540
  33.6 4.8 %copy-start.4 = (s32[16,8]{0,1:T(8,128)S(1)}, s32[16,8]{0,1:T(8,128)}, u32[]{:S(2)}) copy-start(s32[16,8]{0,1:T(8,128)} %param.15) | copy-start | bytes 1540
  33.6 5.1 %copy-start.5 = (bf16[4,512]{1,0:T(4,128)(2,1)S(1)}, bf16[4,512]{1,0:T(4,128)(2,1)}, u32[]{:S(2)}) copy-start(bf16[4,512]{1,0:T(4,128)(2,1)} %param.23) | copy-start | bytes 12292
  33.6 5.1 %copy-start.6 = (bf16[4,512]{1,0:T(4,128)(2,1)S(1)}, bf16[4,512]{1,0:T(4,128)(2,1)}, u32[]{:S(2)}) copy-start(bf16[4,512]{1,0:T(4,128)(2,1)} %param.24) | copy-start | bytes 12292
  33.7 5.1 %copy-start.8 = (s32[4]{0:T(128)S(1)}, s32[4]{0:T(128)}, u32[]{:S(2)}) copy-start(s32[4]{0:T(128)} %param.25) | copy-start | bytes 52
  33.7 5.2 %copy-start.2 = (bf16[4,4096]{1,0:T(4,128)(2,1)S(1)}, bf16[4,4096]{1,0:T(4,128)(2,1)}, u32[]{:S(2)}) copy-start(bf16[4,4096]{1,0:T(4,128)(2,1)} %param.20) | copy-start | bytes 98308
  33.7 6.0 %copy-start.7 = (bf16[4,256,512]{2,1,0:T(8,128)(2,1)S(1)}, bf16[4,256,512]{2,1,0:T(8,128)(2,1)}, u32[]{:S(2)}) copy-start(bf16[4,256,512]{2,1,0:T(8,128)(2,1)} %param.22) | copy-start | bytes 3145732
  33.7 29.5 %all-to-all-start.1 = ((bf16[16,1,16,2048]{3,2,1,0:T(8,128)(2,1)}), bf16[16,1,16,2048]{3,2,1,0:T(8,128)(2,1)S(1)}, u32[]{:S(2)}, u32[]{:S(2)}) async-start(bf16[16,1,16,2048]{3,2,1,0:T(8,128)(2,1)} %bitcast.6), calls=%async_computation.1 | async-start | bytes 2097152 | tf_op jit(solution)/shard_map/all_to_all | solution.py:131

commit v4 on v3

--- a/solution.py
+++ b/solution.py
@@ -114,29 +114,51 @@
 def spread_block(normed, picks, gate_weights, w_gate, w_up, w_down):
     chips = lax.axis_size("chip")
     cores = lax.axis_size("core")
+    chip = lax.axis_index("chip")
     core = lax.axis_index("core")
     rows_here, features = normed.shape
     local_experts = w_gate.shape[0]
     peers = chips * cores
     experts_all = local_experts * peers
-    spread = jnp.broadcast_to(normed[None], (chips, rows_here, features))
-    same_core = lax.all_to_all(spread, "chip", 0, 0, tiled=True)
-    other_core = lax.ppermute(same_core, "core", [(i, (i + 1) % cores) for i in range(cores)])
-    both = jnp.stack([same_core, other_core, same_core], axis=1)
-    ordered = lax.dynamic_slice_in_dim(both, core, cores, axis=1)
-    every_row = ordered.reshape(peers * rows_here, features)
+
+    def shifted(block, shift):
+        pairs = [(i, (i + shift) % chips) for i in range(chips)]
+        return lax.ppermute(block, "chip", pairs)
+
+    same_core = [normed] + [shifted(normed, shift) for shift in range(1, chips)]
+    same_stack = jnp.stack(same_core, axis=0)
+    other_stack = lax.ppermute(same_stack, "core", [(i, (i + 1) % cores) for i in range(cores)])
+    every_row = jnp.concatenate([same_stack, other_stack], axis=0).reshape(
+        peers * rows_here, features
+    )
     produced = expert_mlp(every_row, w_gate, w_up, w_down)
-    produced = produced.reshape(local_experts, peers, rows_here, features)
-    produced = produced.transpose(1, 0, 2, 3)
-    returned = lax.all_to_all(produced, NODE, 0, 0, tiled=True)
-    returned = returned.reshape(experts_all, rows_here, features)
+    produced = produced.reshape(local_experts, cores, chips, rows_here, features)
+    returned_same = [produced[:, 0, 0]]
+    for shift in range(1, chips):
+        returned_same.append(shifted(produced[:, 0, shift], chips - shift))
+    returned_other = []
+    for shift in range(chips):
+        pairs = [
+            (c * cores + k, ((c - shift) % chips) * cores + (k + 1) % cores)
+            for c in range(chips)
+            for k in range(cores)
+        ]
+        returned_other.append(lax.ppermute(produced[:, 1, shift], NODE, pairs))
+    returned = jnp.stack(returned_same + returned_other, axis=0)
+    shifts = jnp.arange(chips, dtype=jnp.int32)
+    source_chip = (chip + shifts) % chips
+    source_node = jnp.concatenate(
+        [source_chip * cores + core, source_chip * cores + (core + 1) % cores]
+    )
+    source_expert = (
+        source_node[:, None] * local_experts + jnp.arange(local_experts, dtype=jnp.int32)[None, :]
+    )
     shares = gate_weights / jnp.sum(gate_weights, axis=1, keepdims=True)
-    expert_ids = jnp.arange(experts_all, dtype=jnp.int32)
-    chosen = picks[:, :, None] == expert_ids[None, None, :]
-    dense_shares = jnp.sum(jnp.where(chosen, shares[:, :, None], 0.0), axis=1)
-    weighted = dense_shares.T[:, :, None] * returned.astype(jnp.float32)
-    return jnp.sum(weighted, axis=0).astype(jnp.bfloat16)
-
+    chosen = picks[:, :, None] == source_expert.reshape(-1)[None, None, :]
+    block_shares = jnp.sum(jnp.where(chosen, shares[:, :, None], 0.0), axis=1)
+    block_shares = block_shares.T.reshape(peers, local_experts, rows_here)
+    weighted = block_shares[:, :, :, None] * returned.astype(jnp.float32)
+    return jnp.sum(weighted, axis=(0, 1)).astype(jnp.bfloat16)
 
 def attend(queries, keys, values, incoming_keys, incoming_values, lengths):
     request_rows = queries.shape[0]

time: 64.5 us -> 69.9 us (1.084)
  the two profiles are of different devices: /device:TPU:11 before, /device:TPU:0 now
where the time goes in v4:
time: 69.9 us; the launch traced here: 69.3 us
  starting transfers between devices  35.1 us (50%)
  waiting for transfers between devices  14.2 us (20%)
  Pallas kernels  5.66 us (8%)
  other arithmetic  5.45 us (8%)
  local copies, waits for them, and re-layouts  4.46 us (6%)
  matrix products  3.64 us (5%)
  between operations  0.9 us (1%)
    ppermute x14, starting transfers between devices, shifted(): return lax.ppermute(block, 'chip', pairs)  24.1 us
    ppermute x8, starting transfers between devices, spread_block(): returned_other.append(lax.ppermute(produced[:, 1, shift], NODE, pairs))  10.9 us
    ppermute x8, waiting for transfers between devices, spread_block(): returned_other.append(lax.ppermute(produced[:, 1, shift], NODE, pairs))  7.85 us
    ppermute x14, waiting for transfers between devices, shifted(): return lax.ppermute(block, 'chip', pairs)  6.31 us
    pallas_call x1, Pallas kernels, expert_mlp(): pl.pallas_call(mlp_kernel, grid=(local_experts, hidden // chunk), in_spec...  5.66 us
    unnamed x30, local copies, waits for them, and re-layouts  3.46 us
    dot_general x1, matrix products, attend(): jnp.einsum('rkgl,rlkd->rkgd', probs, stored_values, preferred_element_typ...  1.53 us
  transfers between devices with their start and end apart: 23, of which 7 were waited for; matrix products, arithmetic and copies ran while one was open for 12% of the time, Pallas kernels for 0%

profile of v4, /device:TPU:0, one launch (start us, length us, event | category | flops | bytes accessed | tf_op | source)
XLA Modules:
  0.0 69.3 jit_solution(15364729447438931502)
XLA Ops:
  0.6 0.0 copy-start
  0.7 1.1 %fusion.7 = f32[16]{0:T(128)S(1)} fusion(bf16[16,2048]{1,0:T(8,128)(2,1)} %param.13), kind=kLoop, calls=%fused_computation.12 | loop fusion | flops 98288 | bytes 65600 | tf_op jit(solution)/shard_map/reduce_sum | solution.py:219
  1.7 1.0 %constant_dynamic-update-slice_fusion.7 = (bf16[8,16,2048]{2,1,0:T(8,128)(2,1)S(1)}, bf16[16,2048]{1,0:T(8,128)(2,1)S(1)}) fusion(f32[2048]{0:T(1024)} %param.14, f32[16]{0:T(128)S(1)} %add_sqrt_fusion, bf16[16,2048]{1,0:T(8,128)(2,1)} %param.13), kind=kLoop, calls=%fused_computation.25 | loop fusion | flops 131071 | bytes 204864
  2.7 3.0 %collective-permute-start = (bf16[16,2048]{1,0:T(8,128)(2,1)S(1)}, bf16[16,2048]{1,0:T(8,128)(2,1)S(1)}, u32[]{:S(2)}, u32[]{:S(2)}) collective-permute-start(bf16[16,2048]{1,0:T(8,128)(2,1)S(1)} %get-tuple-element.3), channel_id=1, source_target_pairs={{0,2},{2,4},{4,6},{6,8},{8,10},{10,12},{12,14},{14,0},{1,3},{3,5},... | collective-permute-start | bytes 196616 | tf_op jit(solution)/shard_map/ppermute | solution.py:126
  5.7 1.6 %collective-permute-start.1 = (bf16[16,2048]{1,0:T(8,128)(2,1)S(1)}, bf16[16,2048]{1,0:T(8,128)(2,1)S(1)}, u32[]{:S(2)}, u32[]{:S(2)}) collective-permute-start(bf16[16,2048]{1,0:T(8,128)(2,1)S(1)} %get-tuple-element.3), channel_id=1, source_target_pairs={{0,4},{2,6},{4,8},{6,10},{8,12},{10,14},{12,0},{14,2},{1,5},{3,7},... | collective-permute-start | bytes 196616 | tf_op jit(solution)/shard_map/ppermute | solution.py:126
  7.3 2.5 %collective-permute-start.2 = (bf16[16,2048]{1,0:T(8,128)(2,1)S(1)}, bf16[16,2048]{1,0:T(8,128)(2,1)S(1)}, u32[]{:S(2)}, u32[]{:S(2)}) collective-permute-start(bf16[16,2048]{1,0:T(8,128)(2,1)S(1)} %get-tuple-element.3), channel_id=1, source_target_pairs={{0,6},{2,8},{4,10},{6,12},{8,14},{10,0},{12,2},{14,4},{1,7},{3,9},... | collective-permute-start | bytes 196616 | tf_op jit(solution)/shard_map/ppermute | solution.py:126
  9.8 1.2 %collective-permute-start.3 = (bf16[16,2048]{1,0:T(8,128)(2,1)S(1)}, bf16[16,2048]{1,0:T(8,128)(2,1)S(1)}, u32[]{:S(2)}, u32[]{:S(2)}) collective-permute-start(bf16[16,2048]{1,0:T(8,128)(2,1)S(1)} %get-tuple-element.3), channel_id=1, source_target_pairs={{0,8},{2,10},{4,12},{6,14},{8,0},{10,2},{12,4},{14,6},{1,9},{3,11}... | collective-permute-start | bytes 196616 | tf_op jit(solution)/shard_map/ppermute | solution.py:126
  11.0 2.6 %collective-permute-start.4 = (bf16[16,2048]{1,0:T(8,128)(2,1)S(1)}, bf16[16,2048]{1,0:T(8,128)(2,1)S(1)}, u32[]{:S(2)}, u32[]{:S(2)}) collective-permute-start(bf16[16,2048]{1,0:T(8,128)(2,1)S(1)} %get-tuple-element.3), channel_id=1, source_target_pairs={{0,10},{2,12},{4,14},{6,0},{8,2},{10,4},{12,6},{14,8},{1,11},{3,13... | collective-permute-start | bytes 196616 | tf_op jit(solution)/shard_map/ppermute | solution.py:126
  13.7 0.7 %reduce_sum.45 = f32[16]{0:T(128)S(1)} reduce(f32[16,8]{0,1:T(8,128)} %param.16, f32[]{:T(128)} %constant.45.clone.1), dimensions={1}, to_apply=%region_0.0 | reduce | flops 112 | bytes 580 | tf_op jit(solution)/shard_map/reduce_sum | solution.py:156
  14.4 0.7 broadcast_divide_fusion
  15.1 0.1 copy.20
  15.2 0.8 %copy.19 = s32[16,8]{1,0:T(8,128)S(1)} copy(s32[16,8]{0,1:T(8,128)} %param.15) | data formatting | bytes 1024 | tf_op args[2]
  15.9 0.7 %iota_compare_fusion = pred[4,256]{1,0:T(4,128)(4,1)S(1)} fusion(s32[4]{0:T(128)} %param.25), kind=kLoop, calls=%fused_computation.81 | loop fusion | flops 1024 | bytes 1040 | tf_op jit(solution)/shard_map/lt | solution.py:184
  16.7 0.7 %reshape.347 = bf16[4,4,128,1]{2,3,1,0:T(2,128)(2,1)S(1)} reshape(bf16[4,512]{1,0:T(4,128)(2,1)} %param.23) | data formatting | bytes 8192 | tf_op jit(solution)/shard_map/reshape | solution.py:179
  17.4 0.9 %fusion.15 = f32[4,4,1,8]{3,2,1,0:T(1,128)S(1)} fusion(bf16[4,4,128,1]{2,3,1,0:T(2,128)(2,1)S(1)} %reshape.347, bf16[1,4,32,128]{3,1,2,0:T(4,128)(2,1)} %bitcast.128), kind=kOutput, calls=%fused_computation.73 | convolution fusion | flops 32768 | bytes 37376 | tf_op jit(solution)/shard_map/behw,bew->beh/dot_general | solution.py:176
  18.3 1.2 %fusion.26 = (f32[4,4,8]{2,1,0:T(4,128)S(1)}, f32[4,4,8,256]{3,2,1,0:T(8,128)S(1)}) fusion(bf16[1,4,32,128]{3,1,2,0:T(4,128)(2,1)} %bitcast.129, pred[4,256]{1,0:T(4,128)(4,1)S(1)} %iota_compare_fusion, bf16[4,256,512]{2,1,0:T(8,128)(2,1)S(1)} %copy-done), kind=kOutput, calls=%fused_computation.95 | convolution fusion | flops 8486784 | bytes 1213952 | tf_op jit(solution)/shard_map/rkgd,rlkd->rkgl/dot_general | solution.py:172
  19.5 0.2 fusion.10
  19.7 0.1 pad_add_fusion
  19.8 0.0 collective-permute-done
  19.8 1.4 %collective-permute-start.5 = (bf16[16,2048]{1,0:T(8,128)(2,1)S(1)}, bf16[16,2048]{1,0:T(8,128)(2,1)S(1)}, u32[]{:S(2)}, u32[]{:S(2)}) collective-permute-start(bf16[16,2048]{1,0:T(8,128)(2,1)S(1)} %get-tuple-element.3), channel_id=1, source_target_pairs={{0,12},{2,14},{4,0},{6,2},{8,4},{10,6},{12,8},{14,10},{1,13},{3,15... | collective-permute-start | bytes 196616 | tf_op jit(solution)/shard_map/ppermute | solution.py:126
  21.1 0.0 collective-permute-done.1
  21.1 1.5 %collective-permute-start.6 = (bf16[16,2048]{1,0:T(8,128)(2,1)S(1)}, bf16[16,2048]{1,0:T(8,128)(2,1)S(1)}, u32[]{:S(2)}, u32[]{:S(2)}) collective-permute-start(bf16[16,2048]{1,0:T(8,128)(2,1)S(1)} %get-tuple-element.3), channel_id=1, source_target_pairs={{0,14},{2,0},{4,2},{6,4},{8,6},{10,8},{12,10},{14,12},{1,15},{3,1}... | collective-permute-start | bytes 196616 | tf_op jit(solution)/shard_map/ppermute | solution.py:126
  22.6 0.0 collective-permute-done.2
  22.6 0.0 collective-permute-done.3
  22.7 0.0 collective-permute-done.4
  22.7 1.3 %collective-permute-done.5 = bf16[16,2048]{1,0:T(8,128)(2,1)S(1)} collective-permute-done((bf16[16,2048]{1,0:T(8,128)(2,1)S(1)}, bf16[16,2048]{1,0:T(8,128)(2,1)S(1)}, u32[]{:S(2)}, u32[]{:S(2)}) %collective-permute-start.5) | collective-permute-done | bytes 65568 | tf_op jit(solution)/shard_map/ppermute | solution.py:126
  24.1 1.4 %collective-permute-done.6 = bf16[16,2048]{1,0:T(8,128)(2,1)S(1)} collective-permute-done((bf16[16,2048]{1,0:T(8,128)(2,1)S(1)}, bf16[16,2048]{1,0:T(8,128)(2,1)S(1)}, u32[]{:S(2)}, u32[]{:S(2)}) %collective-permute-start.6) | collective-permute-done | bytes 65568 | tf_op jit(solution)/shard_map/ppermute | solution.py:126
  25.5 0.1 collective-permute-start.7
  25.6 0.1 select_reduce_fusion
  25.7 0.1 copy.21
  25.8 1.5 %fusion.2 = bf16[1,4,32,128]{3,2,1,0:T(8,128)(2,1)S(1)} fusion(f32[4,4,8,256]{3,2,1,0:T(8,128)S(1)} %get-tuple-element.36, f32[4,4,8]{2,1,0:T(4,128)S(1)} %get-tuple-element.34, f32[4,4,8]{2,1,0:T(4,128)S(1)} %multiply_maximum_fusion, pred[4,256]{1,0:T(4,128)(4,1)S(1)} %iota_compare_fusion, f32[4,4,128]{2,1,0:T(4,128)S(1)} %reshape.343, ...), kind=kOutput, calls=%fused_computation.5 | convolution fusion | flops 8568832 | bytes 1223168 | tf_op jit(solution)/shard_map/rkgl,rlkd->rkgd/dot_general | solution.py:194
  27.3 0.6 copy.51
  28.0 0.0 collective-permute-done.7
  28.0 0.0 copy-start.1
  28.0 1.9 %copy-done.1 = bf16[1,2048,768]{2,1,0:T(8,128)(2,1)S(1)} copy-done((bf16[1,2048,768]{2,1,0:T(8,128)(2,1)S(1)}, bf16[1,2048,768]{2,1,0:T(8,128)(2,1)}, u32[]{:S(2)}) %copy-start.1) | copy-done | bytes 3145752
  29.9 5.7 %shard_map.140 = bf16[1,256,2048]{2,1,0:T(8,128)(2,1)S(1)} custom-call(bf16[256,2048]{1,0:T(8,128)(2,1)S(1)} %bitcast.127, bf16[1,2048,768]{2,1,0:T(8,128)(2,1)S(1)} %copy-done.1, bf16[1,2048,768]{2,1,0:T(8,128)(2,1)} %up_ref.1, bf16[1,768,2048]{2,1,0:T(8,128)(2,1)} %down_ref.1), custom_call_target="tpu_custom_call" | custom-call | tf_op jit(solution)/shard_map/pallas_call | solution.py:96
  35.6 0.1 slice_bitcast_fusion
  35.7 4.2 %collective-permute-start.8 = (bf16[1,16,2048]{2,1,0:T(8,128)(2,1)S(1)}, bf16[1,16,2048]{2,1,0:T(8,128)(2,1)S(1)}, u32[]{:S(2)}, u32[]{:S(2)}) collective-permute-start(bf16[1,16,2048]{2,1,0:T(8,128)(2,1)S(1)} %get-tuple-element.18), channel_id=1, source_target_pairs={{0,14},{2,0},{4,2},{6,4},{8,6},{10,8},{12,10},{14,12},{1,15},{3,1}... | collective-permute-start | bytes 196616 | tf_op jit(solution)/shard_map/ppermute | solution.py:126
  39.8 0.0 collective-permute-start.9
  39.8 0.1 collective-permute-start.10
  39.9 2.9 %collective-permute-start.11 = (bf16[1,16,2048]{2,1,0:T(8,128)(2,1)S(1)}, bf16[1,16,2048]{2,1,0:T(8,128)(2,1)S(1)}, u32[]{:S(2)}, u32[]{:S(2)}) collective-permute-start(bf16[1,16,2048]{2,1,0:T(8,128)(2,1)S(1)} %get-tuple-element.15), channel_id=1, source_target_pairs={{0,8},{2,10},{4,12},{6,14},{8,0},{10,2},{12,4},{14,6},{1,9},{3,11}... | collective-permute-start | bytes 196616 | tf_op jit(solution)/shard_map/ppermute | solution.py:126
  42.8 0.3 collective-permute-start.12
  43.1 0.0 collective-permute-done.8
  43.1 1.7 %collective-permute-start.13 = (bf16[1,16,2048]{2,1,0:T(8,128)(2,1)S(1)}, bf16[1,16,2048]{2,1,0:T(8,128)(2,1)S(1)}, u32[]{:S(2)}, u32[]{:S(2)}) collective-permute-start(bf16[1,16,2048]{2,1,0:T(8,128)(2,1)S(1)} %get-tuple-element.13), channel_id=1, source_target_pairs={{0,4},{2,6},{4,8},{6,10},{8,12},{10,14},{12,0},{14,2},{1,5},{3,7},... | collective-permute-start | bytes 196616 | tf_op jit(solution)/shard_map/ppermute | solution.py:126
  44.8 0.3 collective-permute-done.9
  45.1 1.2 %collective-permute-start.14 = (bf16[1,16,2048]{2,1,0:T(8,128)(2,1)S(1)}, bf16[1,16,2048]{2,1,0:T(8,128)(2,1)S(1)}, u32[]{:S(2)}, u32[]{:S(2)}) collective-permute-start(bf16[1,16,2048]{2,1,0:T(8,128)(2,1)S(1)} %get-tuple-element.12), channel_id=1, source_target_pairs={{0,2},{2,4},{4,6},{6,8},{8,10},{10,12},{12,14},{14,0},{1,3},{3,5},... | collective-permute-start | bytes 196616 | tf_op jit(solution)/shard_map/ppermute | solution.py:126
  46.3 0.0 collective-permute-done.10
  46.3 0.1 collective-permute-start.15
  46.4 1.6 %collective-permute-done.11 = bf16[1,16,2048]{2,1,0:T(8,128)(2,1)S(1)} collective-permute-done((bf16[1,16,2048]{2,1,0:T(8,128)(2,1)S(1)}, bf16[1,16,2048]{2,1,0:T(8,128)(2,1)S(1)}, u32[]{:S(2)}, u32[]{:S(2)}) %collective-permute-start.11) | collective-permute-done | bytes 65568 | tf_op jit(solution)/shard_map/ppermute | solution.py:126
  48.0 4.9 %collective-permute-start.16 = (bf16[1,16,2048]{2,1,0:T(8,128)(2,1)S(1)}, bf16[1,16,2048]{2,1,0:T(8,128)(2,1)S(1)}, u32[]{:S(2)}, u32[]{:S(2)}) collective-permute-start(bf16[1,16,2048]{2,1,0:T(8,128)(2,1)S(1)} %get-tuple-element.10), channel_id=1, source_target_pairs={{0,15},{1,14},{2,1},{3,0},{4,3},{5,2},{6,5},{7,4},{8,7},{9,6},{10,... | collective-permute-start | bytes 196616 | tf_op jit(solution)/shard_map/ppermute | solution.py:146
  52.9 1.6 %collective-permute-done.12 = bf16[1,16,2048]{2,1,0:T(8,128)(2,1)S(1)} collective-permute-done((bf16[1,16,2048]{2,1,0:T(8,128)(2,1)S(1)}, bf16[1,16,2048]{2,1,0:T(8,128)(2,1)S(1)}, u32[]{:S(2)}, u32[]{:S(2)}) %collective-permute-start.12) | collective-permute-done | bytes 65568 | tf_op jit(solution)/shard_map/ppermute | solution.py:126
  54.6 0.1 collective-permute-start.17
  54.6 0.0 collective-permute-done.13
  54.7 1.6 %collective-permute-start.18 = (bf16[1,16,2048]{2,1,0:T(8,128)(2,1)S(1)}, bf16[1,16,2048]{2,1,0:T(8,128)(2,1)S(1)}, u32[]{:S(2)}, u32[]{:S(2)}) collective-permute-start(bf16[1,16,2048]{2,1,0:T(8,128)(2,1)S(1)} %get-tuple-element.8), channel_id=1, source_target_pairs={{0,11},{1,10},{2,13},{3,12},{4,15},{5,14},{6,1},{7,0},{8,3},{9,2},... | collective-permute-start | bytes 196616 | tf_op jit(solution)/shard_map/ppermute | solution.py:146
  56.3 0.0 collective-permute-done.14
  56.3 1.0 %collective-permute-start.19 = (bf16[1,16,2048]{2,1,0:T(8,128)(2,1)S(1)}, bf16[1,16,2048]{2,1,0:T(8,128)(2,1)S(1)}, u32[]{:S(2)}, u32[]{:S(2)}) collective-permute-start(bf16[1,16,2048]{2,1,0:T(8,128)(2,1)S(1)} %get-tuple-element.7), channel_id=1, source_target_pairs={{0,9},{1,8},{2,11},{3,10},{4,13},{5,12},{6,15},{7,14},{8,1},{9,0},... | collective-permute-start | bytes 196616 | tf_op jit(solution)/shard_map/ppermute | solution.py:146
  57.3 0.2 collective-permute-start.20
  57.6 1.7 %collective-permute-start.21 = (bf16[1,16,2048]{2,1,0:T(8,128)(2,1)S(1)}, bf16[1,16,2048]{2,1,0:T(8,128)(2,1)S(1)}, u32[]{:S(2)}, u32[]{:S(2)}) collective-permute-start(bf16[1,16,2048]{2,1,0:T(8,128)(2,1)S(1)} %get-tuple-element.5), channel_id=1, source_target_pairs={{0,5},{1,4},{2,7},{3,6},{4,9},{5,8},{6,11},{7,10},{8,13},{9,12},{1... | collective-permute-start | bytes 196616 | tf_op jit(solution)/shard_map/ppermute | solution.py:146
  59.3 1.3 %collective-permute-start.22 = (bf16[1,16,2048]{2,1,0:T(8,128)(2,1)S(1)}, bf16[1,16,2048]{2,1,0:T(8,128)(2,1)S(1)}, u32[]{:S(2)}, u32[]{:S(2)}) collective-permute-start(bf16[1,16,2048]{2,1,0:T(8,128)(2,1)S(1)} %get-tuple-element.4), channel_id=1, source_target_pairs={{0,3},{1,2},{2,5},{3,4},{4,7},{5,6},{6,9},{7,8},{8,11},{9,10},{10,... | collective-permute-start | bytes 196616 | tf_op jit(solution)/shard_map/ppermute | solution.py:146
  60.5 0.0 collective-permute-done.18
  60.6 6.2 %collective-permute-done.19 = bf16[1,16,2048]{2,1,0:T(8,128)(2,1)S(1)} collective-permute-done((bf16[1,16,2048]{2,1,0:T(8,128)(2,1)S(1)}, bf16[1,16,2048]{2,1,0:T(8,128)(2,1)S(1)}, u32[]{:S(2)}, u32[]{:S(2)}) %collective-permute-start.19) | collective-permute-done | bytes 65568 | tf_op jit(solution)/shard_map/ppermute | solution.py:146
  66.8 1.6 %collective-permute-done.20 = bf16[1,16,2048]{2,1,0:T(8,128)(2,1)S(1)} collective-permute-done((bf16[1,16,2048]{2,1,0:T(8,128)(2,1)S(1)}, bf16[1,16,2048]{2,1,0:T(8,128)(2,1)S(1)}, u32[]{:S(2)}, u32[]{:S(2)}) %collective-permute-start.20) | collective-permute-done | bytes 65568 | tf_op jit(solution)/shard_map/ppermute | solution.py:146
  68.4 0.0 collective-permute-done.22
  68.5 0.9 %multiply_reduce_fusion = bf16[16,2048]{1,0:T(8,128)(2,1)} fusion(bf16[16,1,16,2048]{3,2,1,0:T(8,128)(2,1)S(1)} %constant_dynamic-update-slice_fusion.17, f32[16,16]{1,0:T(8,128)S(1)} %copy.21), kind=kLoop, calls=%fused_computation | loop fusion | flops 1540096 | bytes 1115136 | tf_op jit(solution)/shard_map/reduce_sum | solution.py:161
  (37 shorter events, 0.3 us)
Async XLA Ops:
  0.6 17.6 %copy-start = (bf16[4,256,512]{2,1,0:T(8,128)(2,1)S(1)}, bf16[4,256,512]{2,1,0:T(8,128)(2,1)}, u32[]{:S(2)}) copy-start(bf16[4,256,512]{2,1,0:T(8,128)(2,1)} %param.21) | copy-start | bytes 3145732
  0.6 25.1 %copy-start.2 = (bf16[4,512]{1,0:T(4,128)(2,1)S(1)}, bf16[4,512]{1,0:T(4,128)(2,1)}, u32[]{:S(2)}) copy-start(bf16[4,512]{1,0:T(4,128)(2,1)} %param.24) | copy-start | bytes 12292
  2.7 17.1 %collective-permute-start = (bf16[16,2048]{1,0:T(8,128)(2,1)S(1)}, bf16[16,2048]{1,0:T(8,128)(2,1)S(1)}, u32[]{:S(2)}, u32[]{:S(2)}) collective-permute-start(bf16[16,2048]{1,0:T(8,128)(2,1)S(1)} %get-tuple-element.3), channel_id=1, source_target_pairs={{0,2},{2,4},{4,6},{6,8},{8,10},{10,12},{12,14},{14,0},{1,3},{3,5},... | collective-permute-start | bytes 196616 | tf_op jit(solution)/shard_map/ppermute | solution.py:126
  5.7 15.4 %collective-permute-start.1 = (bf16[16,2048]{1,0:T(8,128)(2,1)S(1)}, bf16[16,2048]{1,0:T(8,128)(2,1)S(1)}, u32[]{:S(2)}, u32[]{:S(2)}) collective-permute-start(bf16[16,2048]{1,0:T(8,128)(2,1)S(1)} %get-tuple-element.3), channel_id=1, source_target_pairs={{0,4},{2,6},{4,8},{6,10},{8,12},{10,14},{12,0},{14,2},{1,5},{3,7},... | collective-permute-start | bytes 196616 | tf_op jit(solution)/shard_map/ppermute | solution.py:126
  7.3 15.3 %collective-permute-start.2 = (bf16[16,2048]{1,0:T(8,128)(2,1)S(1)}, bf16[16,2048]{1,0:T(8,128)(2,1)S(1)}, u32[]{:S(2)}, u32[]{:S(2)}) collective-permute-start(bf16[16,2048]{1,0:T(8,128)(2,1)S(1)} %get-tuple-element.3), channel_id=1, source_target_pairs={{0,6},{2,8},{4,10},{6,12},{8,14},{10,0},{12,2},{14,4},{1,7},{3,9},... | collective-permute-start | bytes 196616 | tf_op jit(solution)/shard_map/ppermute | solution.py:126
  9.8 12.8 %collective-permute-start.3 = (bf16[16,2048]{1,0:T(8,128)(2,1)S(1)}, bf16[16,2048]{1,0:T(8,128)(2,1)S(1)}, u32[]{:S(2)}, u32[]{:S(2)}) collective-permute-start(bf16[16,2048]{1,0:T(8,128)(2,1)S(1)} %get-tuple-element.3), channel_id=1, source_target_pairs={{0,8},{2,10},{4,12},{6,14},{8,0},{10,2},{12,4},{14,6},{1,9},{3,11}... | collective-permute-start | bytes 196616 | tf_op jit(solution)/shard_map/ppermute | solution.py:126
  11.0 11.6 %collective-permute-start.4 = (bf16[16,2048]{1,0:T(8,128)(2,1)S(1)}, bf16[16,2048]{1,0:T(8,128)(2,1)S(1)}, u32[]{:S(2)}, u32[]{:S(2)}) collective-permute-start(bf16[16,2048]{1,0:T(8,128)(2,1)S(1)} %get-tuple-element.3), channel_id=1, source_target_pairs={{0,10},{2,12},{4,14},{6,0},{8,2},{10,4},{12,6},{14,8},{1,11},{3,13... | collective-permute-start | bytes 196616 | tf_op jit(solution)/shard_map/ppermute | solution.py:126
  19.8 4.3 %collective-permute-start.5 = (bf16[16,2048]{1,0:T(8,128)(2,1)S(1)}, bf16[16,2048]{1,0:T(8,128)(2,1)S(1)}, u32[]{:S(2)}, u32[]{:S(2)}) collective-permute-start(bf16[16,2048]{1,0:T(8,128)(2,1)S(1)} %get-tuple-element.3), channel_id=1, source_target_pairs={{0,12},{2,14},{4,0},{6,2},{8,4},{10,6},{12,8},{14,10},{1,13},{3,15... | collective-permute-start | bytes 196616 | tf_op jit(solution)/shard_map/ppermute | solution.py:126
  21.1 4.3 %collective-permute-start.6 = (bf16[16,2048]{1,0:T(8,128)(2,1)S(1)}, bf16[16,2048]{1,0:T(8,128)(2,1)S(1)}, u32[]{:S(2)}, u32[]{:S(2)}) collective-permute-start(bf16[16,2048]{1,0:T(8,128)(2,1)S(1)} %get-tuple-element.3), channel_id=1, source_target_pairs={{0,14},{2,0},{4,2},{6,4},{8,6},{10,8},{12,10},{14,12},{1,15},{3,1}... | collective-permute-start | bytes 196616 | tf_op jit(solution)/shard_map/ppermute | solution.py:126
  25.5 2.5 %collective-permute-start.7 = (bf16[8,16,2048]{2,1,0:T(8,128)(2,1)S(1)}, bf16[8,16,2048]{2,1,0:T(8,128)(2,1)S(1)}, u32[]{:S(2)}, u32[]{:S(2)}) collective-permute-start(bf16[8,16,2048]{2,1,0:T(8,128)(2,1)S(1)} %get-tuple-element.19), channel_id=1, source_target_pairs={{0,1},{1,0},{2,3},{3,2},{4,5},{5,4},{6,7},{7,6},{8,9},{9,8},{10,11... | collective-permute-start | bytes 1572872 | tf_op jit(solution)/shard_map/ppermute | solution.py:130
  28.0 1.9 %copy-start.1 = (bf16[1,2048,768]{2,1,0:T(8,128)(2,1)S(1)}, bf16[1,2048,768]{2,1,0:T(8,128)(2,1)}, u32[]{:S(2)}) copy-start(bf16[1,2048,768]{2,1,0:T(8,128)(2,1)} %gate_ref.1) | copy-start | bytes 9437188
  35.7 7.4 %collective-permute-start.8 = (bf16[1,16,2048]{2,1,0:T(8,128)(2,1)S(1)}, bf16[1,16,2048]{2,1,0:T(8,128)(2,1)S(1)}, u32[]{:S(2)}, u32[]{:S(2)}) collective-permute-start(bf16[1,16,2048]{2,1,0:T(8,128)(2,1)S(1)} %get-tuple-element.18), channel_id=1, source_target_pairs={{0,14},{2,0},{4,2},{6,4},{8,6},{10,8},{12,10},{14,12},{1,15},{3,1}... | collective-permute-start | bytes 196616 | tf_op jit(solution)/shard_map/ppermute | solution.py:126
  39.8 5.3 %collective-permute-start.9 = (bf16[1,16,2048]{2,1,0:T(8,128)(2,1)S(1)}, bf16[1,16,2048]{2,1,0:T(8,128)(2,1)S(1)}, u32[]{:S(2)}, u32[]{:S(2)}) collective-permute-start(bf16[1,16,2048]{2,1,0:T(8,128)(2,1)S(1)} %get-tuple-element.17), channel_id=1, source_target_pairs={{0,12},{2,14},{4,0},{6,2},{8,4},{10,6},{12,8},{14,10},{1,13},{3,15... | collective-permute-start | bytes 196616 | tf_op jit(solution)/shard_map/ppermute | solution.py:126
  39.8 6.5 %collective-permute-start.10 = (bf16[1,16,2048]{2,1,0:T(8,128)(2,1)S(1)}, bf16[1,16,2048]{2,1,0:T(8,128)(2,1)S(1)}, u32[]{:S(2)}, u32[]{:S(2)}) collective-permute-start(bf16[1,16,2048]{2,1,0:T(8,128)(2,1)S(1)} %get-tuple-element.16), channel_id=1, source_target_pairs={{0,10},{2,12},{4,14},{6,0},{8,2},{10,4},{12,6},{14,8},{1,11},{3,13... | collective-permute-start | bytes 196616 | tf_op jit(solution)/shard_map/ppermute | solution.py:126
  39.9 8.1 %collective-permute-start.11 = (bf16[1,16,2048]{2,1,0:T(8,128)(2,1)S(1)}, bf16[1,16,2048]{2,1,0:T(8,128)(2,1)S(1)}, u32[]{:S(2)}, u32[]{:S(2)}) collective-permute-start(bf16[1,16,2048]{2,1,0:T(8,128)(2,1)S(1)} %get-tuple-element.15), channel_id=1, source_target_pairs={{0,8},{2,10},{4,12},{6,14},{8,0},{10,2},{12,4},{14,6},{1,9},{3,11}... | collective-permute-start | bytes 196616 | tf_op jit(solution)/shard_map/ppermute | solution.py:126
  42.8 11.7 %collective-permute-start.12 = (bf16[1,16,2048]{2,1,0:T(8,128)(2,1)S(1)}, bf16[1,16,2048]{2,1,0:T(8,128)(2,1)S(1)}, u32[]{:S(2)}, u32[]{:S(2)}) collective-permute-start(bf16[1,16,2048]{2,1,0:T(8,128)(2,1)S(1)} %get-tuple-element.14), channel_id=1, source_target_pairs={{0,6},{2,8},{4,10},{6,12},{8,14},{10,0},{12,2},{14,4},{1,7},{3,9},... | collective-permute-start | bytes 196616 | tf_op jit(solution)/shard_map/ppermute | solution.py:126
  43.1 11.5 %collective-permute-start.13 = (bf16[1,16,2048]{2,1,0:T(8,128)(2,1)S(1)}, bf16[1,16,2048]{2,1,0:T(8,128)(2,1)S(1)}, u32[]{:S(2)}, u32[]{:S(2)}) collective-permute-start(bf16[1,16,2048]{2,1,0:T(8,128)(2,1)S(1)} %get-tuple-element.13), channel_id=1, source_target_pairs={{0,4},{2,6},{4,8},{6,10},{8,12},{10,14},{12,0},{14,2},{1,5},{3,7},... | collective-permute-start | bytes 196616 | tf_op jit(solution)/shard_map/ppermute | solution.py:126
  45.1 11.2 %collective-permute-start.14 = (bf16[1,16,2048]{2,1,0:T(8,128)(2,1)S(1)}, bf16[1,16,2048]{2,1,0:T(8,128)(2,1)S(1)}, u32[]{:S(2)}, u32[]{:S(2)}) collective-permute-start(bf16[1,16,2048]{2,1,0:T(8,128)(2,1)S(1)} %get-tuple-element.12), channel_id=1, source_target_pairs={{0,2},{2,4},{4,6},{6,8},{8,10},{10,12},{12,14},{14,0},{1,3},{3,5},... | collective-permute-start | bytes 196616 | tf_op jit(solution)/shard_map/ppermute | solution.py:126
  46.3 11.0 %collective-permute-start.15 = (bf16[1,16,2048]{2,1,0:T(8,128)(2,1)S(1)}, bf16[1,16,2048]{2,1,0:T(8,128)(2,1)S(1)}, u32[]{:S(2)}, u32[]{:S(2)}) collective-permute-start(bf16[1,16,2048]{2,1,0:T(8,128)(2,1)S(1)} %get-tuple-element.11), channel_id=1, source_target_pairs={{0,1},{1,0},{2,3},{3,2},{4,5},{5,4},{6,7},{7,6},{8,9},{9,8},{10,11... | collective-permute-start | bytes 196616 | tf_op jit(solution)/shard_map/ppermute | solution.py:146
  48.0 9.5 %collective-permute-start.16 = (bf16[1,16,2048]{2,1,0:T(8,128)(2,1)S(1)}, bf16[1,16,2048]{2,1,0:T(8,128)(2,1)S(1)}, u32[]{:S(2)}, u32[]{:S(2)}) collective-permute-start(bf16[1,16,2048]{2,1,0:T(8,128)(2,1)S(1)} %get-tuple-element.10), channel_id=1, source_target_pairs={{0,15},{1,14},{2,1},{3,0},{4,3},{5,2},{6,5},{7,4},{8,7},{9,6},{10,... | collective-permute-start | bytes 196616 | tf_op jit(solution)/shard_map/ppermute | solution.py:146
  54.6 4.7 %collective-permute-start.17 = (bf16[1,16,2048]{2,1,0:T(8,128)(2,1)S(1)}, bf16[1,16,2048]{2,1,0:T(8,128)(2,1)S(1)}, u32[]{:S(2)}, u32[]{:S(2)}) collective-permute-start(bf16[1,16,2048]{2,1,0:T(8,128)(2,1)S(1)} %get-tuple-element.9), channel_id=1, source_target_pairs={{0,13},{1,12},{2,15},{3,14},{4,1},{5,0},{6,3},{7,2},{8,5},{9,4},{1... | collective-permute-start | bytes 196616 | tf_op jit(solution)/shard_map/ppermute | solution.py:146
  54.7 5.9 %collective-permute-start.18 = (bf16[1,16,2048]{2,1,0:T(8,128)(2,1)S(1)}, bf16[1,16,2048]{2,1,0:T(8,128)(2,1)S(1)}, u32[]{:S(2)}, u32[]{:S(2)}) collective-permute-start(bf16[1,16,2048]{2,1,0:T(8,128)(2,1)S(1)} %get-tuple-element.8), channel_id=1, source_target_pairs={{0,11},{1,10},{2,13},{3,12},{4,15},{5,14},{6,1},{7,0},{8,3},{9,2},... | collective-permute-start | bytes 196616 | tf_op jit(solution)/shard_map/ppermute | solution.py:146
  56.3 10.5 %collective-permute-start.19 = (bf16[1,16,2048]{2,1,0:T(8,128)(2,1)S(1)}, bf16[1,16,2048]{2,1,0:T(8,128)(2,1)S(1)}, u32[]{:S(2)}, u32[]{:S(2)}) collective-permute-start(bf16[1,16,2048]{2,1,0:T(8,128)(2,1)S(1)} %get-tuple-element.7), channel_id=1, source_target_pairs={{0,9},{1,8},{2,11},{3,10},{4,13},{5,12},{6,15},{7,14},{8,1},{9,0},... | collective-permute-start | bytes 196616 | tf_op jit(solution)/shard_map/ppermute | solution.py:146
  57.3 11.1 %collective-permute-start.20 = (bf16[1,16,2048]{2,1,0:T(8,128)(2,1)S(1)}, bf16[1,16,2048]{2,1,0:T(8,128)(2,1)S(1)}, u32[]{:S(2)}, u32[]{:S(2)}) collective-permute-start(bf16[1,16,2048]{2,1,0:T(8,128)(2,1)S(1)} %get-tuple-element.6), channel_id=1, source_target_pairs={{0,7},{1,6},{2,9},{3,8},{4,11},{5,10},{6,13},{7,12},{8,15},{9,14},... | collective-permute-start | bytes 196616 | tf_op jit(solution)/shard_map/ppermute | solution.py:146
  57.6 10.9 %collective-permute-start.21 = (bf16[1,16,2048]{2,1,0:T(8,128)(2,1)S(1)}, bf16[1,16,2048]{2,1,0:T(8,128)(2,1)S(1)}, u32[]{:S(2)}, u32[]{:S(2)}) collective-permute-start(bf16[1,16,2048]{2,1,0:T(8,128)(2,1)S(1)} %get-tuple-element.5), channel_id=1, source_target_pairs={{0,5},{1,4},{2,7},{3,6},{4,9},{5,8},{6,11},{7,10},{8,13},{9,12},{1... | collective-permute-start | bytes 196616 | tf_op jit(solution)/shard_map/ppermute | solution.py:146
  59.3 9.2 %collective-permute-start.22 = (bf16[1,16,2048]{2,1,0:T(8,128)(2,1)S(1)}, bf16[1,16,2048]{2,1,0:T(8,128)(2,1)S(1)}, u32[]{:S(2)}, u32[]{:S(2)}) collective-permute-start(bf16[1,16,2048]{2,1,0:T(8,128)(2,1)S(1)} %get-tuple-element.4), channel_id=1, source_target_pairs={{0,3},{1,2},{2,5},{3,4},{4,7},{5,6},{6,9},{7,8},{8,11},{9,10},{10,... | collective-permute-start | bytes 196616 | tf_op jit(solution)/shard_map/ppermute | solution.py:146

commit v5 on v3

--- a/solution.py
+++ b/solution.py
@@ -71,44 +71,58 @@
     return jnp.einsum("tk,tkd->td", shares, gathered.astype(jnp.float32)).astype(jnp.bfloat16)
 
 
-def mlp_kernel(rows_ref, gate_ref, up_ref, down_ref, out_ref, acc_ref):
+def mlp_kernel(core_ref, same_ref, other_ref, gate_ref, up_ref, down_ref, out_ref, acc_ref):
     step = pl.program_id(1)
+    half = same_ref.shape[0]
 
     @pl.when(step == 0)
     def _():
         acc_ref[...] = jnp.zeros_like(acc_ref)
 
-    rows = rows_ref[...]
-    gate_part = jnp.dot(rows, gate_ref[...], preferred_element_type=jnp.float32)
-    up_part = jnp.dot(rows, up_ref[...], preferred_element_type=jnp.float32)
-    inner = (jax.nn.silu(gate_part) * up_part).astype(jnp.bfloat16)
-    acc_ref[...] += jnp.dot(inner, down_ref[...], preferred_element_type=jnp.float32)
+    gate_block = gate_ref[...]
+    up_block = up_ref[...]
+    down_block = down_ref[...]
+    for part, rows_ref in enumerate((same_ref, other_ref)):
+        rows = rows_ref[...]
+        gate_part = jnp.dot(rows, gate_block, preferred_element_type=jnp.float32)
+        up_part = jnp.dot(rows, up_block, preferred_element_type=jnp.float32)
+        inner = (jax.nn.silu(gate_part) * up_part).astype(jnp.bfloat16)
+        acc_ref[part * half : (part + 1) * half, :] += jnp.dot(
+            inner, down_block, preferred_element_type=jnp.float32
+        )
 
     @pl.when(step == pl.num_programs(1) - 1)
     def _():
-        out_ref[...] = acc_ref[...].astype(out_ref.dtype)
-
-
-def expert_mlp(every_row, w_gate, w_up, w_down):
+        core = core_ref[0]
+        out_ref[core] = acc_ref[0:half, :].astype(out_ref.dtype)
+        out_ref[1 - core] = acc_ref[half : 2 * half, :].astype(out_ref.dtype)
+
+
+def expert_mlp(core, same_rows, other_rows, w_gate, w_up, w_down):
     local_experts, features, hidden = w_gate.shape
-    row_count = every_row.shape[0]
+    half = same_rows.shape[0]
     chunk = 256 if hidden % 256 == 0 else hidden
+    grid_spec = pltpu.PrefetchScalarGridSpec(
+        num_scalar_prefetch=1,
+        grid=(local_experts, hidden // chunk),
+        in_specs=[
+            pl.BlockSpec((half, features), lambda e, f, c: (0, 0)),
+            pl.BlockSpec((half, features), lambda e, f, c: (0, 0)),
+            pl.BlockSpec((None, features, chunk), lambda e, f, c: (e, 0, f)),
+            pl.BlockSpec((None, features, chunk), lambda e, f, c: (e, 0, f)),
+            pl.BlockSpec((None, chunk, features), lambda e, f, c: (e, f, 0)),
+        ],
+        out_specs=pl.BlockSpec((None, 2, half, features), lambda e, f, c: (e, 0, 0, 0)),
+        scratch_shapes=[pltpu.VMEM((2 * half, features), jnp.float32)],
+    )
     return pl.pallas_call(
         mlp_kernel,
-        grid=(local_experts, hidden // chunk),
-        in_specs=[
-            pl.BlockSpec((row_count, features), lambda e, f: (0, 0)),
-            pl.BlockSpec((None, features, chunk), lambda e, f: (e, 0, f)),
-            pl.BlockSpec((None, features, chunk), lambda e, f: (e, 0, f)),
-            pl.BlockSpec((None, chunk, features), lambda e, f: (e, f, 0)),
-        ],
-        out_specs=pl.BlockSpec((None, row_count, features), lambda e, f: (e, 0, 0)),
-        out_shape=jax.ShapeDtypeStruct((local_experts, row_count, features), jnp.bfloat16),
-        scratch_shapes=[pltpu.VMEM((row_count, features), jnp.float32)],
+        grid_spec=grid_spec,
+        out_shape=jax.ShapeDtypeStruct((local_experts, 2, half, features), jnp.bfloat16),
         compiler_params=pltpu.CompilerParams(
             dimension_semantics=("arbitrary", "arbitrary"), vmem_limit_bytes=48 * 1024 * 1024
         ),
-    )(every_row, w_gate, w_up, w_down)
+    )(core.reshape(1), same_rows, other_rows, w_gate, w_up, w_down)
 
 
 def spread_block(normed, picks, gate_weights, w_gate, w_up, w_down):
@@ -122,21 +136,28 @@
     spread = jnp.broadcast_to(normed[None], (chips, rows_here, features))
     same_core = lax.all_to_all(spread, "chip", 0, 0, tiled=True)
     other_core = lax.ppermute(same_core, "core", [(i, (i + 1) % cores) for i in range(cores)])
-    both = jnp.stack([same_core, other_core, same_core], axis=1)
-    ordered = lax.dynamic_slice_in_dim(both, core, cores, axis=1)
-    every_row = ordered.reshape(peers * rows_here, features)
-    produced = expert_mlp(every_row, w_gate, w_up, w_down)
+    produced = expert_mlp(
+        core.astype(jnp.int32),
+        same_core.reshape(chips * rows_here, features),
+        other_core.reshape(chips * rows_here, features),
+        w_gate,
+        w_up,
+        w_down,
+    )
     produced = produced.reshape(local_experts, peers, rows_here, features)
     produced = produced.transpose(1, 0, 2, 3)
-    returned = lax.all_to_all(produced, NODE, 0, 0, tiled=True)
+    returned = lax.all_to_all(produced, ("core", "chip"), 0, 0, tiled=True)
+    blocks = jnp.arange(peers, dtype=jnp.int32)
+    source_node = (blocks % chips) * cores + blocks // chips
+    source_expert = (
+        source_node[:, None] * local_experts + jnp.arange(local_experts, dtype=jnp.int32)[None, :]
+    ).reshape(-1)
     returned = returned.reshape(experts_all, rows_here, features)
     shares = gate_weights / jnp.sum(gate_weights, axis=1, keepdims=True)
-    expert_ids = jnp.arange(experts_all, dtype=jnp.int32)
-    chosen = picks[:, :, None] == expert_ids[None, None, :]
-    dense_shares = jnp.sum(jnp.where(chosen, shares[:, :, None], 0.0), axis=1)
-    weighted = dense_shares.T[:, :, None] * returned.astype(jnp.float32)
+    chosen = picks[:, :, None] == source_expert[None, None, :]
+    block_shares = jnp.sum(jnp.where(chosen, shares[:, :, None], 0.0), axis=1)
+    weighted = block_shares.T[:, :, None] * returned.astype(jnp.float32)
     return jnp.sum(weighted, axis=0).astype(jnp.bfloat16)
-
 
 def attend(queries, keys, values, incoming_keys, incoming_values, lengths):
     request_rows = queries.shape[0]

time: 64.5 us -> 66.7 us (1.034)
  the two profiles are of different devices: /device:TPU:11 before, /device:TPU:0 now
where the time goes in v5:
time: 66.7 us; the launch traced here: 66.3 us
  waiting for transfers between devices  25.4 us (38%)
  blocking collectives  21.6 us (32%)
  Pallas kernels  6.98 us (10%)
  other arithmetic  4.01 us (6%)
  starting transfers between devices  3.83 us (6%)
  local copies, waits for them, and re-layouts  2.85 us (4%)
  matrix products  0.91 us (1%)
  between operations  0.75 us (1%)
    all_to_all x1, waiting for transfers between devices, spread_block(): returned = lax.all_to_all(produced, ('core', 'chip'), 0, 0, tiled=True)  24.2 us
    all_to_all x1, blocking collectives, spread_block(): same_core = lax.all_to_all(spread, 'chip', 0, 0, tiled=True)  21.6 us
    pallas_call x1, Pallas kernels, expert_mlp(): pl.pallas_call(mlp_kernel, grid_spec=grid_spec, out_shape=jax.ShapeDtypeS...  6.98 us
    all_to_all x1, starting transfers between devices, spread_block(): returned = lax.all_to_all(produced, ('core', 'chip'), 0, 0, tiled=True)  3.82 us
    unnamed x20, local copies, waits for them, and re-layouts  2.65 us
  transfers between devices with their start and end apart: 2, of which 2 were waited for; matrix products, arithmetic and copies ran while one was open for 4% of the time, Pallas kernels for 0%

profile of v5, /device:TPU:0, one launch (start us, length us, event | category | flops | bytes accessed | tf_op | source)
XLA Modules:
  0.0 66.3 jit_solution(576073735004027246)
XLA Ops:
  0.6 0.0 copy-start
  0.6 1.1 %fusion.8 = f32[16]{0:T(128)S(1)} fusion(bf16[16,2048]{1,0:T(8,128)(2,1)} %param.13), kind=kLoop, calls=%fused_computation.13 | loop fusion | flops 98288 | bytes 65600 | tf_op jit(solution)/shard_map/reduce_sum | solution.py:218
  1.7 0.9 %fusion.10 = bf16[16,2048]{1,0:T(8,128)(2,1)S(1)} fusion(bf16[16,2048]{1,0:T(8,128)(2,1)} %param.13, f32[2048]{0:T(1024)} %param.14, f32[16]{0:T(128)S(1)} %add_sqrt_fusion), kind=kLoop, calls=%fused_computation.15 | loop fusion | flops 131072 | bytes 139328 | tf_op jit(solution)/shard_map/convert_element_type | solution.py:219
  2.7 21.6 %all_to_all.10 = bf16[8,16,2048]{2,1,0:T(8,128)(2,1)S(1)} all-to-all(bf16[8,16,2048]{2,1,0:T(8,128)(2,1)S(1)} %broadcast_in_dim.50), channel_id=1, replica_groups=mesh['group'=2,'chip'=8,'core'=2] {'chip'}, dimensions={0} | all-to-all | bytes 1048576 | tf_op jit(solution)/shard_map/all_to_all | solution.py:137
  24.3 0.0 collective-permute-start
  24.3 0.7 %reduce_sum.45 = f32[16]{0:T(128)S(1)} reduce(f32[16,8]{0,1:T(8,128)} %param.16, f32[]{:T(128)} %constant.44.clone.1), dimensions={1}, to_apply=%region_0.0 | reduce | flops 112 | bytes 580 | tf_op jit(solution)/shard_map/reduce_sum | solution.py:156
  25.0 1.2 %collective-permute-done = bf16[8,16,2048]{2,1,0:T(8,128)(2,1)S(1)} collective-permute-done((bf16[8,16,2048]{2,1,0:T(8,128)(2,1)S(1)}, bf16[8,16,2048]{2,1,0:T(8,128)(2,1)S(1)}, u32[]{:S(2)}, u32[]{:S(2)}) %collective-permute-start) | collective-permute-done | bytes 524320 | tf_op jit(solution)/shard_map/ppermute | solution.py:138
  26.2 0.0 copy-start.1
  26.2 1.9 %copy-done.1 = bf16[1,2048,768]{2,1,0:T(8,128)(2,1)S(1)} copy-done((bf16[1,2048,768]{2,1,0:T(8,128)(2,1)S(1)}, bf16[1,2048,768]{2,1,0:T(8,128)(2,1)}, u32[]{:S(2)}) %copy-start.1) | copy-done | bytes 3145752
  28.1 0.0 copy-start.3
  28.1 0.0 copy-start.4
  28.1 0.0 copy-start.5
  28.1 0.0 copy-start.6
  28.1 0.0 copy-start.8
  28.1 0.0 copy-start.2
  28.2 7.0 %shard_map.140 = bf16[1,2,128,2048]{3,2,1,0:T(8,128)(2,1)} custom-call(s32[1]{0:T(128)} %bitcast.1.core_ref, bf16[128,2048]{1,0:T(8,128)(2,1)S(1)} %bitcast.44, bf16[128,2048]{1,0:T(8,128)(2,1)S(1)} %bitcast.45, bf16[1,2048,768]{2,1,0:T(8,128)(2,1)S(1)} %copy-done.1, bf16[1,2048,768]{2,1,0:T(8,128)(2,1)} %up_ref.1, bf16[1,768,2048]{2,1,0:T(8,128)(2,1)} %down_ref.1), custom_call_target="tpu_custom_call" | custom-call | tf_op jit(solution)/shard_map/pallas_call | solution.py:118
  35.1 0.0 copy-start.7
  35.1 3.8 %all-to-all-start.1 = ((bf16[16,1,16,2048]{3,2,1,0:T(8,128)(2,1)}), bf16[16,1,16,2048]{3,2,1,0:T(8,128)(2,1)S(1)}, u32[]{:S(2)}, u32[]{:S(2)}) async-start(bf16[16,1,16,2048]{3,2,1,0:T(8,128)(2,1)} %bitcast.5), calls=%async_computation.1 | async-start | bytes 2097152 | tf_op jit(solution)/shard_map/all_to_all | solution.py:149
  39.0 0.0 copy-done.3
  39.0 0.1 copy.25
  39.1 0.0 copy-done.4
  39.1 0.1 copy.24
  39.1 0.1 select_reduce_fusion
  39.3 0.1 copy.26
  39.3 0.0 copy-done.5
  39.3 0.0 copy-done.6
  39.4 0.0 copy-done.8
  39.4 0.1 iota_compare_fusion
  39.5 0.0 copy-done.2
  39.5 0.1 fusion.16
  39.6 0.0 copy-done
  39.6 0.5 fusion.26
  40.1 0.2 fusion.11
  40.3 0.0 copy-done.7
  40.3 0.3 fusion.3
  40.6 0.6 copy.57
  41.3 24.2 %all-to-all-done.1 = bf16[16,1,16,2048]{3,2,1,0:T(8,128)(2,1)S(1)} async-done(((bf16[16,1,16,2048]{3,2,1,0:T(8,128)(2,1)}), bf16[16,1,16,2048]{3,2,1,0:T(8,128)(2,1)S(1)}, u32[]{:S(2)}, u32[]{:S(2)}) %all-to-all-start.1) | async-done | bytes 1048608 | tf_op jit(solution)/shard_map/all_to_all | solution.py:149
  65.4 0.9 %fusion = bf16[16,2048]{1,0:T(8,128)(2,1)} fusion(bf16[16,1,16,2048]{3,2,1,0:T(8,128)(2,1)S(1)} %all-to-all-done.1, f32[16,16]{1,0:T(8,128)S(1)} %copy.26), kind=kLoop, calls=%fused_computation.1 | loop fusion | flops 1540096 | bytes 1115136 | tf_op jit(solution)/shard_map/reduce_sum | solution.py:160
  (8 shorter events, 0.1 us)
Async XLA Ops:
  0.6 39.0 %copy-start = (bf16[4,256,512]{2,1,0:T(8,128)(2,1)S(1)}, bf16[4,256,512]{2,1,0:T(8,128)(2,1)}, u32[]{:S(2)}) copy-start(bf16[4,256,512]{2,1,0:T(8,128)(2,1)} %param.21) | copy-start | bytes 3145732
  24.3 1.9 %collective-permute-start = (bf16[8,16,2048]{2,1,0:T(8,128)(2,1)S(1)}, bf16[8,16,2048]{2,1,0:T(8,128)(2,1)S(1)}, u32[]{:S(2)}, u32[]{:S(2)}) collective-permute-start(bf16[8,16,2048]{2,1,0:T(8,128)(2,1)S(1)} %all_to_all.10), channel_id=1, source_target_pairs={{0,1},{1,0},{2,3},{3,2},{4,5},{5,4},{6,7},{7,6},{8,9},{9,8},{10,11... | collective-permute-start | bytes 1572872 | tf_op jit(solution)/shard_map/ppermute | solution.py:138
  26.2 1.9 %copy-start.1 = (bf16[1,2048,768]{2,1,0:T(8,128)(2,1)S(1)}, bf16[1,2048,768]{2,1,0:T(8,128)(2,1)}, u32[]{:S(2)}) copy-start(bf16[1,2048,768]{2,1,0:T(8,128)(2,1)} %gate_ref.1) | copy-start | bytes 9437188
  28.1 10.9 %copy-start.3 = (f32[16,8]{0,1:T(8,128)S(1)}, f32[16,8]{0,1:T(8,128)}, u32[]{:S(2)}) copy-start(f32[16,8]{0,1:T(8,128)} %param.16) | copy-start | bytes 1540
  28.1 10.9 %copy-start.4 = (s32[16,8]{0,1:T(8,128)S(1)}, s32[16,8]{0,1:T(8,128)}, u32[]{:S(2)}) copy-start(s32[16,8]{0,1:T(8,128)} %param.15) | copy-start | bytes 1540
  28.1 11.2 %copy-start.5 = (bf16[4,512]{1,0:T(4,128)(2,1)S(1)}, bf16[4,512]{1,0:T(4,128)(2,1)}, u32[]{:S(2)}) copy-start(bf16[4,512]{1,0:T(4,128)(2,1)} %param.23) | copy-start | bytes 12292
  28.1 11.2 %copy-start.6 = (bf16[4,512]{1,0:T(4,128)(2,1)S(1)}, bf16[4,512]{1,0:T(4,128)(2,1)}, u32[]{:S(2)}) copy-start(bf16[4,512]{1,0:T(4,128)(2,1)} %param.24) | copy-start | bytes 12292
  28.1 11.2 %copy-start.8 = (s32[4]{0:T(128)S(1)}, s32[4]{0:T(128)}, u32[]{:S(2)}) copy-start(s32[4]{0:T(128)} %param.25) | copy-start | bytes 52
  28.1 11.3 %copy-start.2 = (bf16[4,4096]{1,0:T(4,128)(2,1)S(1)}, bf16[4,4096]{1,0:T(4,128)(2,1)}, u32[]{:S(2)}) copy-start(bf16[4,4096]{1,0:T(4,128)(2,1)} %param.20) | copy-start | bytes 98308
  35.1 5.2 %copy-start.7 = (bf16[4,256,512]{2,1,0:T(8,128)(2,1)S(1)}, bf16[4,256,512]{2,1,0:T(8,128)(2,1)}, u32[]{:S(2)}) copy-start(bf16[4,256,512]{2,1,0:T(8,128)(2,1)} %param.22) | copy-start | bytes 3145732
  35.1 30.3 %all-to-all-start.1 = ((bf16[16,1,16,2048]{3,2,1,0:T(8,128)(2,1)}), bf16[16,1,16,2048]{3,2,1,0:T(8,128)(2,1)S(1)}, u32[]{:S(2)}, u32[]{:S(2)}) async-start(bf16[16,1,16,2048]{3,2,1,0:T(8,128)(2,1)} %bitcast.5), calls=%async_computation.1 | async-start | bytes 2097152 | tf_op jit(solution)/shard_map/all_to_all | solution.py:149

commit v6 on v2

--- a/solution.py
+++ b/solution.py
@@ -3,6 +3,8 @@
 import jax
 import jax.numpy as jnp
 from jax import lax
+from jax.experimental import pallas as pl
+from jax.experimental.pallas import tpu as pltpu
 from jax.sharding import Mesh, PartitionSpec as P
 
 QUERY_HEADS = 32
@@ -69,6 +71,89 @@
     return jnp.einsum("tk,tkd->td", shares, gathered.astype(jnp.float32)).astype(jnp.bfloat16)
 
 
+def mlp_kernel(
+    core_ref, same_ref, other_ref, gate_hbm, up_hbm, down_hbm, out_ref,
+    gate_buf, up_buf, down_buf, acc_ref, sems,
+):
+    expert = pl.program_id(0)
+    chunks, _, chunk = gate_buf.shape
+    chips = out_ref.shape[0]
+    half = same_ref.shape[0]
+    rows_here = half // chips
+    copies = []
+    for f in range(chunks):
+        window = pl.ds(f * chunk, chunk)
+        trio = (
+            pltpu.make_async_copy(gate_hbm.at[expert, :, window], gate_buf.at[f], sems.at[0, f]),
+            pltpu.make_async_copy(up_hbm.at[expert, :, window], up_buf.at[f], sems.at[1, f]),
+            pltpu.make_async_copy(down_hbm.at[expert, window, :], down_buf.at[f], sems.at[2, f]),
+        )
+        for copy in trio:
+            copy.start()
+        copies.append(trio)
+    for f in range(chunks):
+        for copy in copies[f]:
+            copy.wait()
+        gate_block = gate_buf[f]
+        up_block = up_buf[f]
+        down_block = down_buf[f]
+        for part, rows_ref in enumerate((same_ref, other_ref)):
+            rows = rows_ref[...]
+            gate_part = jnp.dot(rows, gate_block, preferred_element_type=jnp.float32)
+            up_part = jnp.dot(rows, up_block, preferred_element_type=jnp.float32)
+            inner = (jax.nn.silu(gate_part) * up_part).astype(jnp.bfloat16)
+            produced = jnp.dot(inner, down_block, preferred_element_type=jnp.float32)
+            if f == 0:
+                acc_ref[part] = produced
+            else:
+                acc_ref[part] += produced
+    core = core_ref[0]
+    for part in range(2):
+        target = (core + part) % 2
+        out_ref[:, pl.ds(target, 1)] = (
+            acc_ref[part].reshape(chips, 1, rows_here, -1).astype(out_ref.dtype)
+        )
+
+
+def expert_mlp(core, same_rows, other_rows, w_gate, w_up, w_down, chips):
+    local_experts, features, hidden = w_gate.shape
+    half = same_rows.shape[0]
+    rows_here = half // chips
+    chunk = 256 if hidden % 256 == 0 else hidden
+    chunks = hidden // chunk
+    grid_spec = pltpu.PrefetchScalarGridSpec(
+        num_scalar_prefetch=1,
+        grid=(local_experts,),
+        in_specs=[
+            pl.BlockSpec((half, features), lambda e, c: (0, 0)),
+            pl.BlockSpec((half, features), lambda e, c: (0, 0)),
+            pl.BlockSpec(memory_space=pl.ANY),
+            pl.BlockSpec(memory_space=pl.ANY),
+            pl.BlockSpec(memory_space=pl.ANY),
+        ],
+        out_specs=pl.BlockSpec(
+            (None, chips, 2, rows_here, features), lambda e, c: (e, 0, 0, 0, 0)
+        ),
+        scratch_shapes=[
+            pltpu.VMEM((chunks, features, chunk), jnp.bfloat16),
+            pltpu.VMEM((chunks, features, chunk), jnp.bfloat16),
+            pltpu.VMEM((chunks, chunk, features), jnp.bfloat16),
+            pltpu.VMEM((2, half, features), jnp.float32),
+            pltpu.SemaphoreType.DMA((3, chunks)),
+        ],
+    )
+    return pl.pallas_call(
+        mlp_kernel,
+        grid_spec=grid_spec,
+        out_shape=jax.ShapeDtypeStruct(
+            (local_experts, chips, 2, rows_here, features), jnp.bfloat16
+        ),
+        compiler_params=pltpu.CompilerParams(
+            dimension_semantics=("arbitrary",), vmem_limit_bytes=48 * 1024 * 1024
+        ),
+    )(core.reshape(1), same_rows, other_rows, w_gate, w_up, w_down)
+
+
 def spread_block(normed, picks, gate_weights, w_gate, w_up, w_down):
     chips = lax.axis_size("chip")
     cores = lax.axis_size("core")
@@ -80,18 +165,16 @@
     spread = jnp.broadcast_to(normed[None], (chips, rows_here, features))
     same_core = lax.all_to_all(spread, "chip", 0, 0, tiled=True)
     other_core = lax.ppermute(same_core, "core", [(i, (i + 1) % cores) for i in range(cores)])
-    both = jnp.stack([same_core, other_core, same_core], axis=1)
-    ordered = lax.dynamic_slice_in_dim(both, core, cores, axis=1)
-    every_row = ordered.reshape(peers * rows_here, features)
-    produced = []
-    for expert in range(local_experts):
-        gate_part = jnp.dot(every_row, w_gate[expert], preferred_element_type=jnp.float32)
-        up_part = jnp.dot(every_row, w_up[expert], preferred_element_type=jnp.float32)
-        inner = (jax.nn.silu(gate_part) * up_part).astype(jnp.bfloat16)
-        produced.append(
-            jnp.dot(inner, w_down[expert], preferred_element_type=jnp.float32).astype(jnp.bfloat16)
-        )
-    produced = jnp.stack(produced, axis=0).reshape(local_experts, peers, rows_here, features)
+    produced = expert_mlp(
+        core.astype(jnp.int32),
+        same_core.reshape(chips * rows_here, features),
+        other_core.reshape(chips * rows_here, features),
+        w_gate,
+        w_up,
+        w_down,
+        chips,
+    )
+    produced = produced.reshape(local_experts, peers, rows_here, features)
     produced = produced.transpose(1, 0, 2, 3)
     returned = lax.all_to_all(produced, NODE, 0, 0, tiled=True)
     returned = returned.reshape(experts_all, rows_here, features)
@@ -99,12 +182,8 @@
     expert_ids = jnp.arange(experts_all, dtype=jnp.int32)
     chosen = picks[:, :, None] == expert_ids[None, None, :]
     dense_shares = jnp.sum(jnp.where(chosen, shares[:, :, None], 0.0), axis=1)
-    picked = jnp.any(chosen, axis=1)
-    weighted = jnp.where(
-        picked.T[:, :, None], dense_shares.T[:, :, None] * returned.astype(jnp.float32), 0.0
-    )
+    weighted = dense_shares.T[:, :, None] * returned.astype(jnp.float32)
     return jnp.sum(weighted, axis=0).astype(jnp.bfloat16)
-
 
 def attend(queries, keys, values, incoming_keys, incoming_values, lengths):
     request_rows = queries.shape[0]

time: 70 us -> 63.5 us (0.907)
  matrix products: 12.7 us -> 0.91 us
  Pallas kernels: 0 us -> 6.2 us
  other arithmetic: 7.17 us -> 3.33 us
  waiting for transfers between devices: 21.2 us -> 24.1 us
  local copies, waits for them, and re-layouts: 2.08 us -> 2.86 us
    dot_general x2 -> x0, matrix products: 9.34 us -> none  [the longest x1 5.55 us: spread_block(): jnp.dot(inner, w_down[expert], preferred_element_type=jnp.float32)]
    pallas_call x0 -> x1, Pallas kernels: none -> 6.2 us  [expert_mlp(): pl.pallas_call(mlp_kernel, grid_spec=grid_spec, out_shape=jax.ShapeDtypeS...]
    all_to_all x1, waiting for transfers between devices: 20.1 us -> 22.5 us  [spread_block(): returned = lax.all_to_all(produced, NODE, 0, 0, tiled=True)]
    another operation x1 -> x0, other arithmetic: 1.67 us -> none  [spread_block(): both = jnp.stack([same_core, other_core, same_core], axis=1)]
    reduce_sum x1, other arithmetic: 2.21 us -> 0.89 us  [spread_block(): return jnp.sum(weighted, axis=0).astype(jnp.bfloat16)]
    dot_general x1, matrix products: 1.69 us -> 0.47 us  [attend(): jnp.einsum('rkgd,rlkd->rkgl', query_rows, stored_keys, preferred_element_...]
    dot_general x1, matrix products: 1.53 us -> 0.31 us  [attend(): jnp.einsum('rkgl,rlkd->rkgd', probs, stored_values, preferred_element_typ...]
    unnamed x18 -> x20, local copies, waits for them, and re-layouts: 1.78 us -> 2.65 us
  transfers between devices with their start and end apart: 2 -> 2, of which waited for: 2 -> 2; matrix products, arithmetic and copies ran while one was open for 8% -> 4% of each run, Pallas kernels for 0% -> 0%
where the time goes in v6:
time: 63.5 us; the launch traced here: 63.2 us
  waiting for transfers between devices  24.1 us (38%)
  blocking collectives  18.2 us (29%)
  starting transfers between devices  6.83 us (11%)
  Pallas kernels  6.2 us (10%)
  other arithmetic  3.33 us (5%)
  local copies, waits for them, and re-layouts  2.86 us (5%)
  matrix products  0.91 us (1%)
  between operations  0.75 us (1%)
    all_to_all x1, waiting for transfers between devices, spread_block(): returned = lax.all_to_all(produced, NODE, 0, 0, tiled=True)  22.5 us
    all_to_all x1, blocking collectives, spread_block(): same_core = lax.all_to_all(spread, 'chip', 0, 0, tiled=True)  18.2 us
    pallas_call x1, Pallas kernels, expert_mlp(): pl.pallas_call(mlp_kernel, grid_spec=grid_spec, out_shape=jax.ShapeDtypeS...  6.2 us
    all_to_all x1, starting transfers between devices, spread_block(): returned = lax.all_to_all(produced, NODE, 0, 0, tiled=True)  4.67 us
    unnamed x20, local copies, waits for them, and re-layouts  2.65 us
    ppermute x1, starting transfers between devices, spread_block(): lax.ppermute(same_core, 'core', [(i, (i + 1) % cores) for i in range(core...  2.16 us
    ppermute x1, waiting for transfers between devices, spread_block(): lax.ppermute(same_core, 'core', [(i, (i + 1) % cores) for i in range(core...  1.54 us
  transfers between devices with their start and end apart: 2, of which 2 were waited for; matrix products, arithmetic and copies ran while one was open for 4% of the time, Pallas kernels for 0%

profile of v6, /device:TPU:11, one launch (start us, length us, event | category | flops | bytes accessed | tf_op | source)
XLA Modules:
  0.0 63.2 jit_solution(5019132957898618130)
XLA Ops:
  0.6 0.0 copy-start
  0.6 1.1 %fusion.8 = f32[16]{0:T(128)S(1)} fusion(bf16[16,2048]{1,0:T(8,128)(2,1)} %param.13), kind=kLoop, calls=%fused_computation.13 | loop fusion | flops 98288 | bytes 65600 | tf_op jit(solution)/shard_map/reduce_sum | solution.py:244
  1.7 0.9 %fusion.10 = bf16[16,2048]{1,0:T(8,128)(2,1)S(1)} fusion(bf16[16,2048]{1,0:T(8,128)(2,1)} %param.13, f32[2048]{0:T(1024)} %param.14, f32[16]{0:T(128)S(1)} %add_sqrt_fusion), kind=kLoop, calls=%fused_computation.15 | loop fusion | flops 131072 | bytes 139328 | tf_op jit(solution)/shard_map/convert_element_type | solution.py:245
  2.7 18.2 %all_to_all.10 = bf16[8,16,2048]{2,1,0:T(8,128)(2,1)S(1)} all-to-all(bf16[8,16,2048]{2,1,0:T(8,128)(2,1)S(1)} %broadcast_in_dim.51), channel_id=1, replica_groups=mesh['group'=2,'chip'=8,'core'=2] {'chip'}, dimensions={0} | all-to-all | bytes 1048576 | tf_op jit(solution)/shard_map/all_to_all | solution.py:166
  20.9 2.2 %collective-permute-start = (bf16[8,16,2048]{2,1,0:T(8,128)(2,1)S(1)}, bf16[8,16,2048]{2,1,0:T(8,128)(2,1)S(1)}, u32[]{:S(2)}, u32[]{:S(2)}) collective-permute-start(bf16[8,16,2048]{2,1,0:T(8,128)(2,1)S(1)} %all_to_all.10), channel_id=1, source_target_pairs={{0,1},{1,0},{2,3},{3,2},{4,5},{5,4},{6,7},{7,6},{8,9},{9,8},{10,11... | collective-permute-start | bytes 1572872 | tf_op jit(solution)/shard_map/ppermute | solution.py:167
  23.1 1.5 %collective-permute-done = bf16[8,16,2048]{2,1,0:T(8,128)(2,1)S(1)} collective-permute-done((bf16[8,16,2048]{2,1,0:T(8,128)(2,1)S(1)}, bf16[8,16,2048]{2,1,0:T(8,128)(2,1)S(1)}, u32[]{:S(2)}, u32[]{:S(2)}) %collective-permute-start) | collective-permute-done | bytes 524320 | tf_op jit(solution)/shard_map/ppermute | solution.py:167
  24.6 0.0 copy-start.1
  24.6 1.9 %copy-done.1 = bf16[1,2048,768]{2,1,0:T(8,128)(2,1)S(1)} copy-done((bf16[1,2048,768]{2,1,0:T(8,128)(2,1)S(1)}, bf16[1,2048,768]{2,1,0:T(8,128)(2,1)}, u32[]{:S(2)}) %copy-start.1) | copy-done | bytes 3145752
  26.5 0.0 copy-start.3
  26.5 0.0 copy-start.4
  26.5 0.0 copy-start.5
  26.5 0.0 copy-start.6
  26.5 0.0 copy-start.8
  26.5 0.0 copy-start.2
  26.5 6.2 %shard_map.140 = bf16[1,8,2,16,2048]{4,3,2,1,0:T(8,128)(2,1)} custom-call(s32[1]{0:T(128)} %bitcast.1.core_ref, bf16[128,2048]{1,0:T(8,128)(2,1)S(1)} %bitcast.44, bf16[128,2048]{1,0:T(8,128)(2,1)S(1)} %bitcast.45, bf16[1,2048,768]{2,1,0:T(8,128)(2,1)S(1)} %copy-done.1, bf16[1,2048,768]{2,1,0:T(8,128)(2,1)} %up_hbm.1, bf16[1,768,2048]{2,1,0:T(8,128)(2,1)} %down_hbm.1), custom_call_target="tpu_custom_call" | custom-call | tf_op jit(solution)/shard_map/pallas_call | solution.py:145
  32.8 0.0 copy-start.7
  32.8 4.7 %all-to-all-start.1 = ((bf16[16,1,16,2048]{3,2,1,0:T(8,128)(2,1)}), bf16[16,1,16,2048]{3,2,1,0:T(8,128)(2,1)S(1)}, u32[]{:S(2)}, u32[]{:S(2)}) async-start(bf16[16,1,16,2048]{3,2,1,0:T(8,128)(2,1)} %bitcast.5), calls=%async_computation.1 | async-start | bytes 2097152 | tf_op jit(solution)/shard_map/all_to_all | solution.py:179
  37.4 0.0 copy-done.3
  37.5 0.1 copy.25
  37.5 0.0 copy-done.4
  37.5 0.1 copy.24
  37.6 0.1 select_reduce_fusion
  37.7 0.1 copy.26
  37.8 0.0 copy-done.5
  37.8 0.0 copy-done.6
  37.8 0.0 copy-done.8
  37.9 0.1 iota_compare_fusion.1
  37.9 0.0 copy-done.2
  37.9 0.1 fusion.16
  38.1 0.0 copy-done
  38.1 0.5 fusion.24
  38.5 0.2 fusion.11
  38.8 0.0 copy-done.7
  38.8 0.3 fusion.3
  39.1 0.6 %copy.57 = bf16[1,4,32,128]{3,1,2,0:T(4,128)(2,1)} copy(bf16[1,4,32,128]{3,2,1,0:T(8,128)(2,1)S(1)} %fusion.3) | data formatting | bytes 65536
  39.7 22.5 %all-to-all-done.1 = bf16[16,1,16,2048]{3,2,1,0:T(8,128)(2,1)S(1)} async-done(((bf16[16,1,16,2048]{3,2,1,0:T(8,128)(2,1)}), bf16[16,1,16,2048]{3,2,1,0:T(8,128)(2,1)S(1)}, u32[]{:S(2)}, u32[]{:S(2)}) %all-to-all-start.1) | async-done | bytes 1048608 | tf_op jit(solution)/shard_map/all_to_all | solution.py:179
  62.3 0.9 %fusion = bf16[16,2048]{1,0:T(8,128)(2,1)} fusion(bf16[16,1,16,2048]{3,2,1,0:T(8,128)(2,1)S(1)} %all-to-all-done.1, f32[16,16]{1,0:T(8,128)S(1)} %copy.26), kind=kLoop, calls=%fused_computation.1 | loop fusion | flops 1540096 | bytes 1115136 | tf_op jit(solution)/shard_map/reduce_sum | solution.py:186
  (8 shorter events, 0.1 us)
Async XLA Ops:
  0.6 37.4 %copy-start = (bf16[4,256,512]{2,1,0:T(8,128)(2,1)S(1)}, bf16[4,256,512]{2,1,0:T(8,128)(2,1)}, u32[]{:S(2)}) copy-start(bf16[4,256,512]{2,1,0:T(8,128)(2,1)} %param.21) | copy-start | bytes 3145732
  20.9 3.7 %collective-permute-start = (bf16[8,16,2048]{2,1,0:T(8,128)(2,1)S(1)}, bf16[8,16,2048]{2,1,0:T(8,128)(2,1)S(1)}, u32[]{:S(2)}, u32[]{:S(2)}) collective-permute-start(bf16[8,16,2048]{2,1,0:T(8,128)(2,1)S(1)} %all_to_all.10), channel_id=1, source_target_pairs={{0,1},{1,0},{2,3},{3,2},{4,5},{5,4},{6,7},{7,6},{8,9},{9,8},{10,11... | collective-permute-start | bytes 1572872 | tf_op jit(solution)/shard_map/ppermute | solution.py:167
  24.6 1.9 %copy-start.1 = (bf16[1,2048,768]{2,1,0:T(8,128)(2,1)S(1)}, bf16[1,2048,768]{2,1,0:T(8,128)(2,1)}, u32[]{:S(2)}) copy-start(bf16[1,2048,768]{2,1,0:T(8,128)(2,1)} %gate_hbm.1) | copy-start | bytes 9437188
  26.5 10.9 %copy-start.3 = (f32[16,8]{0,1:T(8,128)S(1)}, f32[16,8]{0,1:T(8,128)}, u32[]{:S(2)}) copy-start(f32[16,8]{0,1:T(8,128)} %param.16) | copy-start | bytes 1540
  26.5 11.0 %copy-start.4 = (s32[16,8]{0,1:T(8,128)S(1)}, s32[16,8]{0,1:T(8,128)}, u32[]{:S(2)}) copy-start(s32[16,8]{0,1:T(8,128)} %param.15) | copy-start | bytes 1540
  26.5 11.3 %copy-start.5 = (bf16[4,512]{1,0:T(4,128)(2,1)S(1)}, bf16[4,512]{1,0:T(4,128)(2,1)}, u32[]{:S(2)}) copy-start(bf16[4,512]{1,0:T(4,128)(2,1)} %param.23) | copy-start | bytes 12292
  26.5 11.3 %copy-start.6 = (bf16[4,512]{1,0:T(4,128)(2,1)S(1)}, bf16[4,512]{1,0:T(4,128)(2,1)}, u32[]{:S(2)}) copy-start(bf16[4,512]{1,0:T(4,128)(2,1)} %param.24) | copy-start | bytes 12292
  26.5 11.3 %copy-start.8 = (s32[4]{0:T(128)S(1)}, s32[4]{0:T(128)}, u32[]{:S(2)}) copy-start(s32[4]{0:T(128)} %param.25) | copy-start | bytes 52
  26.5 11.4 %copy-start.2 = (bf16[4,4096]{1,0:T(4,128)(2,1)S(1)}, bf16[4,4096]{1,0:T(4,128)(2,1)}, u32[]{:S(2)}) copy-start(bf16[4,4096]{1,0:T(4,128)(2,1)} %param.20) | copy-start | bytes 98308
  32.8 6.0 %copy-start.7 = (bf16[4,256,512]{2,1,0:T(8,128)(2,1)S(1)}, bf16[4,256,512]{2,1,0:T(8,128)(2,1)}, u32[]{:S(2)}) copy-start(bf16[4,256,512]{2,1,0:T(8,128)(2,1)} %param.22) | copy-start | bytes 3145732
  32.8 29.5 %all-to-all-start.1 = ((bf16[16,1,16,2048]{3,2,1,0:T(8,128)(2,1)}), bf16[16,1,16,2048]{3,2,1,0:T(8,128)(2,1)S(1)}, u32[]{:S(2)}, u32[]{:S(2)}) async-start(bf16[16,1,16,2048]{3,2,1,0:T(8,128)(2,1)} %bitcast.5), calls=%async_computation.1 | async-start | bytes 2097152 | tf_op jit(solution)/shard_map/all_to_all | solution.py:179

commit v7 on v6

--- a/solution.py
+++ b/solution.py
@@ -73,7 +73,7 @@
 
 def mlp_kernel(
     core_ref, same_ref, other_ref, gate_hbm, up_hbm, down_hbm, out_ref,
-    gate_buf, up_buf, down_buf, acc_ref, sems,
+    gate_buf, up_buf, down_buf, inner_buf, sems,
 ):
     expert = pl.program_id(0)
     chunks, _, chunk = gate_buf.shape
@@ -83,35 +83,35 @@
     copies = []
     for f in range(chunks):
         window = pl.ds(f * chunk, chunk)
-        trio = (
+        pair = (
             pltpu.make_async_copy(gate_hbm.at[expert, :, window], gate_buf.at[f], sems.at[0, f]),
             pltpu.make_async_copy(up_hbm.at[expert, :, window], up_buf.at[f], sems.at[1, f]),
-            pltpu.make_async_copy(down_hbm.at[expert, window, :], down_buf.at[f], sems.at[2, f]),
         )
-        for copy in trio:
+        for copy in pair:
             copy.start()
-        copies.append(trio)
+        copies.append(pair)
+    down_copy = pltpu.make_async_copy(down_hbm.at[expert], down_buf, sems.at[2, 0])
+    down_copy.start()
     for f in range(chunks):
         for copy in copies[f]:
             copy.wait()
         gate_block = gate_buf[f]
         up_block = up_buf[f]
-        down_block = down_buf[f]
         for part, rows_ref in enumerate((same_ref, other_ref)):
             rows = rows_ref[...]
             gate_part = jnp.dot(rows, gate_block, preferred_element_type=jnp.float32)
             up_part = jnp.dot(rows, up_block, preferred_element_type=jnp.float32)
-            inner = (jax.nn.silu(gate_part) * up_part).astype(jnp.bfloat16)
-            produced = jnp.dot(inner, down_block, preferred_element_type=jnp.float32)
-            if f == 0:
-                acc_ref[part] = produced
-            else:
-                acc_ref[part] += produced
+            inner_buf[part, :, f * chunk : (f + 1) * chunk] = (
+                jax.nn.silu(gate_part) * up_part
+            ).astype(jnp.bfloat16)
+    down_copy.wait()
+    down_block = down_buf[...]
     core = core_ref[0]
     for part in range(2):
+        produced = jnp.dot(inner_buf[part], down_block, preferred_element_type=jnp.float32)
         target = (core + part) % 2
         out_ref[:, pl.ds(target, 1)] = (
-            acc_ref[part].reshape(chips, 1, rows_here, -1).astype(out_ref.dtype)
+            produced.reshape(chips, 1, rows_here, -1).astype(out_ref.dtype)
         )
 
 
@@ -127,9 +127,9 @@
         in_specs=[
             pl.BlockSpec((half, features), lambda e, c: (0, 0)),
             pl.BlockSpec((half, features), lambda e, c: (0, 0)),
-            pl.BlockSpec(memory_space=pl.ANY),
-            pl.BlockSpec(memory_space=pl.ANY),
-            pl.BlockSpec(memory_space=pl.ANY),
+            pl.BlockSpec(memory_space=pltpu.HBM),
+            pl.BlockSpec(memory_space=pltpu.HBM),
+            pl.BlockSpec(memory_space=pltpu.HBM),
         ],
         out_specs=pl.BlockSpec(
             (None, chips, 2, rows_here, features), lambda e, c: (e, 0, 0, 0, 0)
@@ -137,8 +137,8 @@
         scratch_shapes=[
             pltpu.VMEM((chunks, features, chunk), jnp.bfloat16),
             pltpu.VMEM((chunks, features, chunk), jnp.bfloat16),
-            pltpu.VMEM((chunks, chunk, features), jnp.bfloat16),
-            pltpu.VMEM((2, half, features), jnp.float32),
+            pltpu.VMEM((hidden, features), jnp.bfloat16),
+            pltpu.VMEM((2, half, hidden), jnp.bfloat16),
             pltpu.SemaphoreType.DMA((3, chunks)),
         ],
     )

time: 63.5 us -> 62.9 us (level)
  Pallas kernels: 6.2 us -> 5.54 us
    pallas_call x1, Pallas kernels: 6.2 us -> 5.54 us  [expert_mlp(): pl.pallas_call(mlp_kernel, grid_spec=grid_spec, out_shape=jax.ShapeDtypeS...]
where the time goes in v7:
time: 62.9 us; the launch traced here: 62.5 us
  waiting for transfers between devices  24.1 us (38%)
  blocking collectives  18.2 us (29%)
  starting transfers between devices  6.84 us (11%)
  Pallas kernels  5.54 us (9%)
  other arithmetic  3.33 us (5%)
  local copies, waits for them, and re-layouts  2.86 us (5%)
  matrix products  0.91 us (1%)
  between operations  0.75 us (1%)
    all_to_all x1, waiting for transfers between devices, spread_block(): returned = lax.all_to_all(produced, NODE, 0, 0, tiled=True)  22.5 us
    all_to_all x1, blocking collectives, spread_block(): same_core = lax.all_to_all(spread, 'chip', 0, 0, tiled=True)  18.2 us
    pallas_call x1, Pallas kernels, expert_mlp(): pl.pallas_call(mlp_kernel, grid_spec=grid_spec, out_shape=jax.ShapeDtypeS...  5.54 us
    all_to_all x1, starting transfers between devices, spread_block(): returned = lax.all_to_all(produced, NODE, 0, 0, tiled=True)  4.68 us
    unnamed x20, local copies, waits for them, and re-layouts  2.65 us
    ppermute x1, starting transfers between devices, spread_block(): lax.ppermute(same_core, 'core', [(i, (i + 1) % cores) for i in range(core...  2.16 us
    ppermute x1, waiting for transfers between devices, spread_block(): lax.ppermute(same_core, 'core', [(i, (i + 1) % cores) for i in range(core...  1.54 us
  transfers between devices with their start and end apart: 2, of which 2 were waited for; matrix products, arithmetic and copies ran while one was open for 4% of the time, Pallas kernels for 0%

profile of v7, /device:TPU:11, one launch (start us, length us, event | category | flops | bytes accessed | tf_op | source)
XLA Modules:
  0.0 62.5 jit_solution(3464872200335588431)
XLA Ops:
  0.6 0.0 copy-start
  0.6 1.1 %fusion.8 = f32[16]{0:T(128)S(1)} fusion(bf16[16,2048]{1,0:T(8,128)(2,1)} %param.13), kind=kLoop, calls=%fused_computation.13 | loop fusion | flops 98288 | bytes 65600 | tf_op jit(solution)/shard_map/reduce_sum | solution.py:244
  1.7 0.9 %fusion.10 = bf16[16,2048]{1,0:T(8,128)(2,1)S(1)} fusion(bf16[16,2048]{1,0:T(8,128)(2,1)} %param.13, f32[2048]{0:T(1024)} %param.14, f32[16]{0:T(128)S(1)} %add_sqrt_fusion), kind=kLoop, calls=%fused_computation.15 | loop fusion | flops 131072 | bytes 139328 | tf_op jit(solution)/shard_map/convert_element_type | solution.py:245
  2.7 18.2 %all_to_all.10 = bf16[8,16,2048]{2,1,0:T(8,128)(2,1)S(1)} all-to-all(bf16[8,16,2048]{2,1,0:T(8,128)(2,1)S(1)} %broadcast_in_dim.51), channel_id=1, replica_groups=mesh['group'=2,'chip'=8,'core'=2] {'chip'}, dimensions={0} | all-to-all | bytes 1048576 | tf_op jit(solution)/shard_map/all_to_all | solution.py:166
  20.9 2.2 %collective-permute-start = (bf16[8,16,2048]{2,1,0:T(8,128)(2,1)S(1)}, bf16[8,16,2048]{2,1,0:T(8,128)(2,1)S(1)}, u32[]{:S(2)}, u32[]{:S(2)}) collective-permute-start(bf16[8,16,2048]{2,1,0:T(8,128)(2,1)S(1)} %all_to_all.10), channel_id=1, source_target_pairs={{0,1},{1,0},{2,3},{3,2},{4,5},{5,4},{6,7},{7,6},{8,9},{9,8},{10,11... | collective-permute-start | bytes 1572872 | tf_op jit(solution)/shard_map/ppermute | solution.py:167
  23.1 1.5 %collective-permute-done = bf16[8,16,2048]{2,1,0:T(8,128)(2,1)S(1)} collective-permute-done((bf16[8,16,2048]{2,1,0:T(8,128)(2,1)S(1)}, bf16[8,16,2048]{2,1,0:T(8,128)(2,1)S(1)}, u32[]{:S(2)}, u32[]{:S(2)}) %collective-permute-start) | collective-permute-done | bytes 524320 | tf_op jit(solution)/shard_map/ppermute | solution.py:167
  24.6 0.0 copy-start.1
  24.6 1.9 %copy-done.1 = bf16[1,2048,768]{2,1,0:T(8,128)(2,1)S(1)} copy-done((bf16[1,2048,768]{2,1,0:T(8,128)(2,1)S(1)}, bf16[1,2048,768]{2,1,0:T(8,128)(2,1)}, u32[]{:S(2)}) %copy-start.1) | copy-done | bytes 3145752
  26.5 0.0 copy-start.3
  26.5 0.0 copy-start.4
  26.5 0.0 copy-start.5
  26.5 0.0 copy-start.6
  26.5 0.0 copy-start.8
  26.5 0.0 copy-start.2
  26.5 5.5 %shard_map.140 = bf16[1,8,2,16,2048]{4,3,2,1,0:T(8,128)(2,1)} custom-call(s32[1]{0:T(128)} %bitcast.1.core_ref, bf16[128,2048]{1,0:T(8,128)(2,1)S(1)} %bitcast.44, bf16[128,2048]{1,0:T(8,128)(2,1)S(1)} %bitcast.45, bf16[1,2048,768]{2,1,0:T(8,128)(2,1)S(1)} %copy-done.1, bf16[1,2048,768]{2,1,0:T(8,128)(2,1)} %up_hbm.1, bf16[1,768,2048]{2,1,0:T(8,128)(2,1)} %down_hbm.1), custom_call_target="tpu_custom_call" | custom-call | tf_op jit(solution)/shard_map/pallas_call | solution.py:145
  32.1 0.0 copy-start.7
  32.1 4.7 %all-to-all-start.1 = ((bf16[16,1,16,2048]{3,2,1,0:T(8,128)(2,1)}), bf16[16,1,16,2048]{3,2,1,0:T(8,128)(2,1)S(1)}, u32[]{:S(2)}, u32[]{:S(2)}) async-start(bf16[16,1,16,2048]{3,2,1,0:T(8,128)(2,1)} %bitcast.5), calls=%async_computation.1 | async-start | bytes 2097152 | tf_op jit(solution)/shard_map/all_to_all | solution.py:179
  36.8 0.0 copy-done.3
  36.8 0.1 copy.25
  36.9 0.0 copy-done.4
  36.9 0.1 copy.24
  37.0 0.1 select_reduce_fusion
  37.1 0.1 copy.26
  37.2 0.0 copy-done.5
  37.2 0.0 copy-done.6
  37.2 0.0 copy-done.8
  37.2 0.1 iota_compare_fusion.1
  37.3 0.0 copy-done.2
  37.3 0.1 fusion.16
  37.4 0.0 copy-done
  37.4 0.5 fusion.24
  37.9 0.2 fusion.11
  38.1 0.0 copy-done.7
  38.1 0.3 fusion.3
  38.4 0.6 %copy.57 = bf16[1,4,32,128]{3,1,2,0:T(4,128)(2,1)} copy(bf16[1,4,32,128]{3,2,1,0:T(8,128)(2,1)S(1)} %fusion.3) | data formatting | bytes 65536
  39.1 22.5 %all-to-all-done.1 = bf16[16,1,16,2048]{3,2,1,0:T(8,128)(2,1)S(1)} async-done(((bf16[16,1,16,2048]{3,2,1,0:T(8,128)(2,1)}), bf16[16,1,16,2048]{3,2,1,0:T(8,128)(2,1)S(1)}, u32[]{:S(2)}, u32[]{:S(2)}) %all-to-all-start.1) | async-done | bytes 1048608 | tf_op jit(solution)/shard_map/all_to_all | solution.py:179
  61.6 0.9 %fusion = bf16[16,2048]{1,0:T(8,128)(2,1)} fusion(bf16[16,1,16,2048]{3,2,1,0:T(8,128)(2,1)S(1)} %all-to-all-done.1, f32[16,16]{1,0:T(8,128)S(1)} %copy.26), kind=kLoop, calls=%fused_computation.1 | loop fusion | flops 1540096 | bytes 1115136 | tf_op jit(solution)/shard_map/reduce_sum | solution.py:186
  (8 shorter events, 0.1 us)
Async XLA Ops:
  0.6 36.8 %copy-start = (bf16[4,256,512]{2,1,0:T(8,128)(2,1)S(1)}, bf16[4,256,512]{2,1,0:T(8,128)(2,1)}, u32[]{:S(2)}) copy-start(bf16[4,256,512]{2,1,0:T(8,128)(2,1)} %param.21) | copy-start | bytes 3145732
  20.9 3.7 %collective-permute-start = (bf16[8,16,2048]{2,1,0:T(8,128)(2,1)S(1)}, bf16[8,16,2048]{2,1,0:T(8,128)(2,1)S(1)}, u32[]{:S(2)}, u32[]{:S(2)}) collective-permute-start(bf16[8,16,2048]{2,1,0:T(8,128)(2,1)S(1)} %all_to_all.10), channel_id=1, source_target_pairs={{0,1},{1,0},{2,3},{3,2},{4,5},{5,4},{6,7},{7,6},{8,9},{9,8},{10,11... | collective-permute-start | bytes 1572872 | tf_op jit(solution)/shard_map/ppermute | solution.py:167
  24.6 1.9 %copy-start.1 = (bf16[1,2048,768]{2,1,0:T(8,128)(2,1)S(1)}, bf16[1,2048,768]{2,1,0:T(8,128)(2,1)}, u32[]{:S(2)}) copy-start(bf16[1,2048,768]{2,1,0:T(8,128)(2,1)} %gate_hbm.1) | copy-start | bytes 9437188
  26.5 10.3 %copy-start.3 = (f32[16,8]{0,1:T(8,128)S(1)}, f32[16,8]{0,1:T(8,128)}, u32[]{:S(2)}) copy-start(f32[16,8]{0,1:T(8,128)} %param.16) | copy-start | bytes 1540
  26.5 10.4 %copy-start.4 = (s32[16,8]{0,1:T(8,128)S(1)}, s32[16,8]{0,1:T(8,128)}, u32[]{:S(2)}) copy-start(s32[16,8]{0,1:T(8,128)} %param.15) | copy-start | bytes 1540
  26.5 10.7 %copy-start.5 = (bf16[4,512]{1,0:T(4,128)(2,1)S(1)}, bf16[4,512]{1,0:T(4,128)(2,1)}, u32[]{:S(2)}) copy-start(bf16[4,512]{1,0:T(4,128)(2,1)} %param.23) | copy-start | bytes 12292
  26.5 10.7 %copy-start.6 = (bf16[4,512]{1,0:T(4,128)(2,1)S(1)}, bf16[4,512]{1,0:T(4,128)(2,1)}, u32[]{:S(2)}) copy-start(bf16[4,512]{1,0:T(4,128)(2,1)} %param.24) | copy-start | bytes 12292
  26.5 10.7 %copy-start.8 = (s32[4]{0:T(128)S(1)}, s32[4]{0:T(128)}, u32[]{:S(2)}) copy-start(s32[4]{0:T(128)} %param.25) | copy-start | bytes 52
  26.5 10.8 %copy-start.2 = (bf16[4,4096]{1,0:T(4,128)(2,1)S(1)}, bf16[4,4096]{1,0:T(4,128)(2,1)}, u32[]{:S(2)}) copy-start(bf16[4,4096]{1,0:T(4,128)(2,1)} %param.20) | copy-start | bytes 98308
  32.1 6.0 %copy-start.7 = (bf16[4,256,512]{2,1,0:T(8,128)(2,1)S(1)}, bf16[4,256,512]{2,1,0:T(8,128)(2,1)}, u32[]{:S(2)}) copy-start(bf16[4,256,512]{2,1,0:T(8,128)(2,1)} %param.22) | copy-start | bytes 3145732
  32.1 29.5 %all-to-all-start.1 = ((bf16[16,1,16,2048]{3,2,1,0:T(8,128)(2,1)}), bf16[16,1,16,2048]{3,2,1,0:T(8,128)(2,1)S(1)}, u32[]{:S(2)}, u32[]{:S(2)}) async-start(bf16[16,1,16,2048]{3,2,1,0:T(8,128)(2,1)} %bitcast.5), calls=%async_computation.1 | async-start | bytes 2097152 | tf_op jit(solution)/shard_map/all_to_all | solution.py:179

commit v8 on v7

--- a/solution.py
+++ b/solution.py
@@ -149,7 +149,7 @@
             (local_experts, chips, 2, rows_here, features), jnp.bfloat16
         ),
         compiler_params=pltpu.CompilerParams(
-            dimension_semantics=("arbitrary",), vmem_limit_bytes=48 * 1024 * 1024
+            dimension_semantics=("arbitrary",), vmem_limit_bytes=50 * 1024 * 1024
         ),
     )(core.reshape(1), same_rows, other_rows, w_gate, w_up, w_down)
 

time: 62.9 us -> 61.4 us (0.976)
  local copies, waits for them, and re-layouts: 2.86 us -> 0.97 us
    unnamed x20 -> x18, local copies, waits for them, and re-layouts: 2.65 us -> 0.76 us
where the time goes in v8:
time: 61.4 us; the launch traced here: 61.1 us
  waiting for transfers between devices  24.1 us (39%)
  blocking collectives  18.2 us (30%)
  starting transfers between devices  6.83 us (11%)
  Pallas kernels  6.01 us (10%)
  other arithmetic  3.33 us (5%)
  local copies, waits for them, and re-layouts  0.97 us (2%)
  matrix products  0.91 us (1%)
  between operations  0.74 us (1%)
    all_to_all x1, waiting for transfers between devices, spread_block(): returned = lax.all_to_all(produced, NODE, 0, 0, tiled=True)  22.5 us
    all_to_all x1, blocking collectives, spread_block(): same_core = lax.all_to_all(spread, 'chip', 0, 0, tiled=True)  18.2 us
    pallas_call x1, Pallas kernels, expert_mlp(): pl.pallas_call(mlp_kernel, grid_spec=grid_spec, out_shape=jax.ShapeDtypeS...  6.01 us
    all_to_all x1, starting transfers between devices, spread_block(): returned = lax.all_to_all(produced, NODE, 0, 0, tiled=True)  4.67 us
    ppermute x1, starting transfers between devices, spread_block(): lax.ppermute(same_core, 'core', [(i, (i + 1) % cores) for i in range(core...  2.16 us
    ppermute x1, waiting for transfers between devices, spread_block(): lax.ppermute(same_core, 'core', [(i, (i + 1) % cores) for i in range(core...  1.54 us
  transfers between devices with their start and end apart: 2, of which 2 were waited for; matrix products, arithmetic and copies ran while one was open for 4% of the time, Pallas kernels for 0%

profile of v8, /device:TPU:11, one launch (start us, length us, event | category | flops | bytes accessed | tf_op | source)
XLA Modules:
  0.0 61.1 jit_solution(9026258722678509181)
XLA Ops:
  0.6 0.0 copy-start
  0.6 1.1 %fusion.8 = f32[16]{0:T(128)S(1)} fusion(bf16[16,2048]{1,0:T(8,128)(2,1)} %param.13), kind=kLoop, calls=%fused_computation.13 | loop fusion | flops 98288 | bytes 65600 | tf_op jit(solution)/shard_map/reduce_sum | solution.py:244
  1.7 0.9 %fusion.10 = bf16[16,2048]{1,0:T(8,128)(2,1)S(1)} fusion(bf16[16,2048]{1,0:T(8,128)(2,1)} %param.13, f32[2048]{0:T(1024)} %param.14, f32[16]{0:T(128)S(1)} %add_sqrt_fusion), kind=kLoop, calls=%fused_computation.15 | loop fusion | flops 131072 | bytes 139328 | tf_op jit(solution)/shard_map/convert_element_type | solution.py:245
  2.7 18.2 %all_to_all.10 = bf16[8,16,2048]{2,1,0:T(8,128)(2,1)S(1)} all-to-all(bf16[8,16,2048]{2,1,0:T(8,128)(2,1)S(1)} %broadcast_in_dim.51), channel_id=1, replica_groups=mesh['group'=2,'chip'=8,'core'=2] {'chip'}, dimensions={0} | all-to-all | bytes 1048576 | tf_op jit(solution)/shard_map/all_to_all | solution.py:166
  20.9 2.2 %collective-permute-start = (bf16[8,16,2048]{2,1,0:T(8,128)(2,1)S(1)}, bf16[8,16,2048]{2,1,0:T(8,128)(2,1)S(1)}, u32[]{:S(2)}, u32[]{:S(2)}) collective-permute-start(bf16[8,16,2048]{2,1,0:T(8,128)(2,1)S(1)} %all_to_all.10), channel_id=1, source_target_pairs={{0,1},{1,0},{2,3},{3,2},{4,5},{5,4},{6,7},{7,6},{8,9},{9,8},{10,11... | collective-permute-start | bytes 1572872 | tf_op jit(solution)/shard_map/ppermute | solution.py:167
  23.1 1.5 %collective-permute-done = bf16[8,16,2048]{2,1,0:T(8,128)(2,1)S(1)} collective-permute-done((bf16[8,16,2048]{2,1,0:T(8,128)(2,1)S(1)}, bf16[8,16,2048]{2,1,0:T(8,128)(2,1)S(1)}, u32[]{:S(2)}, u32[]{:S(2)}) %collective-permute-start) | collective-permute-done | bytes 524320 | tf_op jit(solution)/shard_map/ppermute | solution.py:167
  24.6 0.0 copy-start.2
  24.6 0.0 copy-start.3
  24.6 0.0 copy-start.4
  24.6 0.0 copy-start.5
  24.6 0.0 copy-start.7
  24.6 0.0 copy-start.1
  24.6 6.0 %shard_map.140 = bf16[1,8,2,16,2048]{4,3,2,1,0:T(8,128)(2,1)} custom-call(s32[1]{0:T(128)} %bitcast.1.core_ref, bf16[128,2048]{1,0:T(8,128)(2,1)S(1)} %bitcast.44, bf16[128,2048]{1,0:T(8,128)(2,1)S(1)} %bitcast.45, bf16[1,2048,768]{2,1,0:T(8,128)(2,1)} %gate_hbm.1, bf16[1,2048,768]{2,1,0:T(8,128)(2,1)} %up_hbm.1, bf16[1,768,2048]{2,1,0:T(8,128)(2,1)} %down_hbm.1), custom_call_target="tpu_custom_call" | custom-call | tf_op jit(solution)/shard_map/pallas_call | solution.py:145
  30.7 0.0 copy-start.6
  30.7 4.7 %all-to-all-start.1 = ((bf16[16,1,16,2048]{3,2,1,0:T(8,128)(2,1)}), bf16[16,1,16,2048]{3,2,1,0:T(8,128)(2,1)S(1)}, u32[]{:S(2)}, u32[]{:S(2)}) async-start(bf16[16,1,16,2048]{3,2,1,0:T(8,128)(2,1)} %bitcast.5), calls=%async_computation.1 | async-start | bytes 2097152 | tf_op jit(solution)/shard_map/all_to_all | solution.py:179
  35.3 0.0 copy-done.2
  35.4 0.1 copy.25
  35.5 0.0 copy-done.3
  35.5 0.1 copy.24
  35.5 0.1 select_reduce_fusion
  35.7 0.1 copy.26
  35.7 0.0 copy-done.4
  35.7 0.0 copy-done.5
  35.8 0.0 copy-done.7
  35.8 0.1 iota_compare_fusion.1
  35.8 0.0 copy-done.1
  35.8 0.1 fusion.16
  36.0 0.0 copy-done
  36.0 0.5 fusion.24
  36.5 0.2 fusion.11
  36.7 0.0 copy-done.6
  36.7 0.3 fusion.3
  37.0 0.6 %copy.57 = bf16[1,4,32,128]{3,1,2,0:T(4,128)(2,1)} copy(bf16[1,4,32,128]{3,2,1,0:T(8,128)(2,1)S(1)} %fusion.3) | data formatting | bytes 65536
  37.7 22.5 %all-to-all-done.1 = bf16[16,1,16,2048]{3,2,1,0:T(8,128)(2,1)S(1)} async-done(((bf16[16,1,16,2048]{3,2,1,0:T(8,128)(2,1)}), bf16[16,1,16,2048]{3,2,1,0:T(8,128)(2,1)S(1)}, u32[]{:S(2)}, u32[]{:S(2)}) %all-to-all-start.1) | async-done | bytes 1048608 | tf_op jit(solution)/shard_map/all_to_all | solution.py:179
  60.2 0.9 %fusion = bf16[16,2048]{1,0:T(8,128)(2,1)} fusion(bf16[16,1,16,2048]{3,2,1,0:T(8,128)(2,1)S(1)} %all-to-all-done.1, f32[16,16]{1,0:T(8,128)S(1)} %copy.26), kind=kLoop, calls=%fused_computation.1 | loop fusion | flops 1540096 | bytes 1115136 | tf_op jit(solution)/shard_map/reduce_sum | solution.py:186
  (8 shorter events, 0.1 us)
Async XLA Ops:
  0.6 35.3 %copy-start = (bf16[4,256,512]{2,1,0:T(8,128)(2,1)S(1)}, bf16[4,256,512]{2,1,0:T(8,128)(2,1)}, u32[]{:S(2)}) copy-start(bf16[4,256,512]{2,1,0:T(8,128)(2,1)} %param.21) | copy-start | bytes 3145732
  20.9 3.7 %collective-permute-start = (bf16[8,16,2048]{2,1,0:T(8,128)(2,1)S(1)}, bf16[8,16,2048]{2,1,0:T(8,128)(2,1)S(1)}, u32[]{:S(2)}, u32[]{:S(2)}) collective-permute-start(bf16[8,16,2048]{2,1,0:T(8,128)(2,1)S(1)} %all_to_all.10), channel_id=1, source_target_pairs={{0,1},{1,0},{2,3},{3,2},{4,5},{5,4},{6,7},{7,6},{8,9},{9,8},{10,11... | collective-permute-start | bytes 1572872 | tf_op jit(solution)/shard_map/ppermute | solution.py:167
  24.6 10.7 %copy-start.2 = (f32[16,8]{0,1:T(8,128)S(1)}, f32[16,8]{0,1:T(8,128)}, u32[]{:S(2)}) copy-start(f32[16,8]{0,1:T(8,128)} %param.16) | copy-start | bytes 1540
  24.6 10.8 %copy-start.3 = (s32[16,8]{0,1:T(8,128)S(1)}, s32[16,8]{0,1:T(8,128)}, u32[]{:S(2)}) copy-start(s32[16,8]{0,1:T(8,128)} %param.15) | copy-start | bytes 1540
  24.6 11.1 %copy-start.4 = (bf16[4,512]{1,0:T(4,128)(2,1)S(1)}, bf16[4,512]{1,0:T(4,128)(2,1)}, u32[]{:S(2)}) copy-start(bf16[4,512]{1,0:T(4,128)(2,1)} %param.23) | copy-start | bytes 12292
  24.6 11.1 %copy-start.5 = (bf16[4,512]{1,0:T(4,128)(2,1)S(1)}, bf16[4,512]{1,0:T(4,128)(2,1)}, u32[]{:S(2)}) copy-start(bf16[4,512]{1,0:T(4,128)(2,1)} %param.24) | copy-start | bytes 12292
  24.6 11.1 %copy-start.7 = (s32[4]{0:T(128)S(1)}, s32[4]{0:T(128)}, u32[]{:S(2)}) copy-start(s32[4]{0:T(128)} %param.25) | copy-start | bytes 52
  24.6 11.2 %copy-start.1 = (bf16[4,4096]{1,0:T(4,128)(2,1)S(1)}, bf16[4,4096]{1,0:T(4,128)(2,1)}, u32[]{:S(2)}) copy-start(bf16[4,4096]{1,0:T(4,128)(2,1)} %param.20) | copy-start | bytes 98308
  30.7 6.0 %copy-start.6 = (bf16[4,256,512]{2,1,0:T(8,128)(2,1)S(1)}, bf16[4,256,512]{2,1,0:T(8,128)(2,1)}, u32[]{:S(2)}) copy-start(bf16[4,256,512]{2,1,0:T(8,128)(2,1)} %param.22) | copy-start | bytes 3145732
  30.7 29.5 %all-to-all-start.1 = ((bf16[16,1,16,2048]{3,2,1,0:T(8,128)(2,1)}), bf16[16,1,16,2048]{3,2,1,0:T(8,128)(2,1)S(1)}, u32[]{:S(2)}, u32[]{:S(2)}) async-start(bf16[16,1,16,2048]{3,2,1,0:T(8,128)(2,1)} %bitcast.5), calls=%async_computation.1 | async-start | bytes 2097152 | tf_op jit(solution)/shard_map/all_to_all | solution.py:179

commit v9 on v8

--- a/solution.py
+++ b/solution.py
@@ -72,8 +72,8 @@
 
 
 def mlp_kernel(
-    core_ref, same_ref, other_ref, gate_hbm, up_hbm, down_hbm, out_ref,
-    gate_buf, up_buf, down_buf, inner_buf, sems,
+    core_ref, gain_ref, same_ref, other_ref, gate_hbm, up_hbm, down_hbm, out_ref,
+    gate_buf, up_buf, down_buf, inner_buf, normed_buf, sems,
 ):
     expert = pl.program_id(0)
     chunks, _, chunk = gate_buf.shape
@@ -92,13 +92,18 @@
         copies.append(pair)
     down_copy = pltpu.make_async_copy(down_hbm.at[expert], down_buf, sems.at[2, 0])
     down_copy.start()
+    gain = gain_ref[...]
+    for part, rows_ref in enumerate((same_ref, other_ref)):
+        widened = rows_ref[...].astype(jnp.float32)
+        meansq = jnp.mean(widened * widened, axis=1, keepdims=True) + 1e-06
+        normed_buf[part] = (widened / jnp.sqrt(meansq) * gain).astype(jnp.bfloat16)
     for f in range(chunks):
         for copy in copies[f]:
             copy.wait()
         gate_block = gate_buf[f]
         up_block = up_buf[f]
-        for part, rows_ref in enumerate((same_ref, other_ref)):
-            rows = rows_ref[...]
+        for part in range(2):
+            rows = normed_buf[part]
             gate_part = jnp.dot(rows, gate_block, preferred_element_type=jnp.float32)
             up_part = jnp.dot(rows, up_block, preferred_element_type=jnp.float32)
             inner_buf[part, :, f * chunk : (f + 1) * chunk] = (
@@ -115,7 +120,7 @@
         )
 
 
-def expert_mlp(core, same_rows, other_rows, w_gate, w_up, w_down, chips):
+def expert_mlp(core, norm_gain, same_rows, other_rows, w_gate, w_up, w_down, chips):
     local_experts, features, hidden = w_gate.shape
     half = same_rows.shape[0]
     rows_here = half // chips
@@ -125,6 +130,7 @@
         num_scalar_prefetch=1,
         grid=(local_experts,),
         in_specs=[
+            pl.BlockSpec((1, features), lambda e, c: (0, 0)),
             pl.BlockSpec((half, features), lambda e, c: (0, 0)),
             pl.BlockSpec((half, features), lambda e, c: (0, 0)),
             pl.BlockSpec(memory_space=pltpu.HBM),
@@ -139,6 +145,7 @@
             pltpu.VMEM((chunks, features, chunk), jnp.bfloat16),
             pltpu.VMEM((hidden, features), jnp.bfloat16),
             pltpu.VMEM((2, half, hidden), jnp.bfloat16),
+            pltpu.VMEM((2, half, features), jnp.bfloat16),
             pltpu.SemaphoreType.DMA((3, chunks)),
         ],
     )
@@ -151,22 +158,23 @@
         compiler_params=pltpu.CompilerParams(
             dimension_semantics=("arbitrary",), vmem_limit_bytes=50 * 1024 * 1024
         ),
-    )(core.reshape(1), same_rows, other_rows, w_gate, w_up, w_down)
-
-
-def spread_block(normed, picks, gate_weights, w_gate, w_up, w_down):
+    )(core.reshape(1), norm_gain.reshape(1, -1), same_rows, other_rows, w_gate, w_up, w_down)
+
+
+def spread_block(states, norm_gain, picks, gate_weights, w_gate, w_up, w_down):
     chips = lax.axis_size("chip")
     cores = lax.axis_size("core")
     core = lax.axis_index("core")
-    rows_here, features = normed.shape
+    rows_here, features = states.shape
     local_experts = w_gate.shape[0]
     peers = chips * cores
     experts_all = local_experts * peers
-    spread = jnp.broadcast_to(normed[None], (chips, rows_here, features))
+    spread = jnp.broadcast_to(states[None], (chips, rows_here, features))
     same_core = lax.all_to_all(spread, "chip", 0, 0, tiled=True)
     other_core = lax.ppermute(same_core, "core", [(i, (i + 1) % cores) for i in range(cores)])
     produced = expert_mlp(
         core.astype(jnp.int32),
+        norm_gain,
         same_core.reshape(chips * rows_here, features),
         other_core.reshape(chips * rows_here, features),
         w_gate,
@@ -247,7 +255,7 @@
     capacity = min(TOK_DEV, max(2, 2 * TOK_DEV * TOPK // experts_all))
     gathered_rows = normed.shape[0] * node_size()
     if gathered_rows <= experts_all * capacity and lax.axis_size("core") == 2:
-        moe_output = spread_block(normed, picks, gate_weights, w_gate, w_up, w_down)
+        moe_output = spread_block(states, norm_gain, picks, gate_weights, w_gate, w_up, w_down)
     else:
         moe_output = route_block(normed, picks, gate_weights, w_gate, w_up, w_down, capacity)
     attention_output = attend(queries, keys, values, incoming_keys, incoming_values, lengths)

time: 61.4 us -> 61.1 us (level)
  other arithmetic: 3.33 us -> 1.33 us
  local copies, waits for them, and re-layouts: 0.97 us -> 2.59 us
    reduce_sum x1 -> x0, other arithmetic: 1.06 us -> none  [on_device(): meansq = jnp.mean(widened * widened, axis=1, keepdims=True) + 1e-06]
    convert_element_type x1 -> x0, other arithmetic: 0.93 us -> none  [on_device(): (widened / jnp.sqrt(meansq) * norm_gain[None, :]).astype(jnp.bfloat16)]
    broadcast_in_dim x1, local copies, waits for them, and re-layouts: 0.04 us -> 0.97 us  [spread_block(): spread = jnp.broadcast_to(states[None], (chips, rows_here, features))]
    unnamed x18 -> x20, local copies, waits for them, and re-layouts: 0.76 us -> 1.46 us
where the time goes in v9:
time: 61.1 us; the launch traced here: 60.7 us
  waiting for transfers between devices  24.1 us (39%)
  blocking collectives  18.2 us (30%)
  starting transfers between devices  6.83 us (11%)
  Pallas kernels  6.05 us (10%)
  local copies, waits for them, and re-layouts  2.59 us (4%)
  other arithmetic  1.33 us (2%)
  matrix products  0.91 us (1%)
  between operations  0.74 us (1%)
    all_to_all x1, waiting for transfers between devices, spread_block(): returned = lax.all_to_all(produced, NODE, 0, 0, tiled=True)  22.5 us
    all_to_all x1, blocking collectives, spread_block(): same_core = lax.all_to_all(spread, 'chip', 0, 0, tiled=True)  18.2 us
    pallas_call x1, Pallas kernels, expert_mlp(): pl.pallas_call(mlp_kernel, grid_spec=grid_spec, out_shape=jax.ShapeDtypeS...  6.05 us
    all_to_all x1, starting transfers between devices, spread_block(): returned = lax.all_to_all(produced, NODE, 0, 0, tiled=True)  4.68 us
    ppermute x1, starting transfers between devices, spread_block(): lax.ppermute(same_core, 'core', [(i, (i + 1) % cores) for i in range(core...  2.16 us
    ppermute x1, waiting for transfers between devices, spread_block(): lax.ppermute(same_core, 'core', [(i, (i + 1) % cores) for i in range(core...  1.54 us
    unnamed x20, local copies, waits for them, and re-layouts  1.46 us
  transfers between devices with their start and end apart: 2, of which 2 were waited for; matrix products, arithmetic and copies ran while one was open for 4% of the time, Pallas kernels for 0%

profile of v9, /device:TPU:11, one launch (start us, length us, event | category | flops | bytes accessed | tf_op | source)
XLA Modules:
  0.0 60.7 jit_solution(18018746090057115357)
XLA Ops:
  0.6 0.0 copy-start
  0.6 1.0 %broadcast_in_dim.49 = bf16[8,16,2048]{2,1,0:T(8,128)(2,1)S(1)} broadcast(bf16[16,2048]{1,0:T(8,128)(2,1)} %param.13), dimensions={1,2} | broadcast | bytes 589824 | tf_op jit(solution)/shard_map/broadcast_in_dim | solution.py:172
  1.6 18.2 %all_to_all.10 = bf16[8,16,2048]{2,1,0:T(8,128)(2,1)S(1)} all-to-all(bf16[8,16,2048]{2,1,0:T(8,128)(2,1)S(1)} %broadcast_in_dim.49), channel_id=1, replica_groups=mesh['group'=2,'chip'=8,'core'=2] {'chip'}, dimensions={0} | all-to-all | bytes 1048576 | tf_op jit(solution)/shard_map/all_to_all | solution.py:173
  19.8 2.2 %collective-permute-start = (bf16[8,16,2048]{2,1,0:T(8,128)(2,1)S(1)}, bf16[8,16,2048]{2,1,0:T(8,128)(2,1)S(1)}, u32[]{:S(2)}, u32[]{:S(2)}) collective-permute-start(bf16[8,16,2048]{2,1,0:T(8,128)(2,1)S(1)} %all_to_all.10), channel_id=1, source_target_pairs={{0,1},{1,0},{2,3},{3,2},{4,5},{5,4},{6,7},{7,6},{8,9},{9,8},{10,11... | collective-permute-start | bytes 1572872 | tf_op jit(solution)/shard_map/ppermute | solution.py:174
  22.0 1.5 %collective-permute-done = bf16[8,16,2048]{2,1,0:T(8,128)(2,1)S(1)} collective-permute-done((bf16[8,16,2048]{2,1,0:T(8,128)(2,1)S(1)}, bf16[8,16,2048]{2,1,0:T(8,128)(2,1)S(1)}, u32[]{:S(2)}, u32[]{:S(2)}) %collective-permute-start) | collective-permute-done | bytes 524320 | tf_op jit(solution)/shard_map/ppermute | solution.py:174
  23.5 0.0 copy-start.1
  23.5 0.7 %copy-done.1 = f32[2048]{0:T(1024)S(1)} copy-done((f32[2048]{0:T(1024)S(1)}, f32[2048]{0:T(1024)}, u32[]{:S(2)}) %copy-start.1) | copy-done | bytes 8216
  24.2 0.0 copy-start.3
  24.2 0.0 copy-start.4
  24.2 0.0 copy-start.5
  24.2 0.0 copy-start.6
  24.2 0.0 copy-start.8
  24.3 0.0 copy-start.2
  24.3 6.0 %shard_map.140 = bf16[1,8,2,16,2048]{4,3,2,1,0:T(8,128)(2,1)} custom-call(s32[1]{0:T(128)} %bitcast.1.core_ref, f32[1,2048]{1,0:T(1,128)S(1)} %bitcast.47, bf16[128,2048]{1,0:T(8,128)(2,1)S(1)} %bitcast.45, bf16[128,2048]{1,0:T(8,128)(2,1)S(1)} %bitcast.46, bf16[1,2048,768]{2,1,0:T(8,128)(2,1)} %gate_hbm.1, bf16[1,2048,768]{2,1,0:T(8,128)(2,1)} %up_hbm.1, ...), custom_call_target="tpu_custom_call" | custom-call | tf_op jit(solution)/shard_map/pallas_call | solution.py:152
  30.3 0.0 copy-start.7
  30.3 4.7 %all-to-all-start.1 = ((bf16[16,1,16,2048]{3,2,1,0:T(8,128)(2,1)}), bf16[16,1,16,2048]{3,2,1,0:T(8,128)(2,1)S(1)}, u32[]{:S(2)}, u32[]{:S(2)}) async-start(bf16[16,1,16,2048]{3,2,1,0:T(8,128)(2,1)} %bitcast.6), calls=%async_computation.1 | async-start | bytes 2097152 | tf_op jit(solution)/shard_map/all_to_all | solution.py:187
  35.0 0.0 copy-done.3
  35.0 0.1 copy.25
  35.1 0.0 copy-done.4
  35.1 0.1 copy.24
  35.2 0.1 select_reduce_fusion
  35.3 0.1 copy.26
  35.4 0.0 copy-done.5
  35.4 0.0 copy-done.6
  35.4 0.0 copy-done.8
  35.4 0.1 iota_compare_fusion.1
  35.5 0.0 copy-done.2
  35.5 0.1 fusion.13
  35.6 0.0 copy-done
  35.6 0.5 fusion.21
  36.1 0.2 fusion.8
  36.3 0.0 copy-done.7
  36.4 0.3 fusion.3
  36.7 0.6 %copy.57 = bf16[1,4,32,128]{3,1,2,0:T(4,128)(2,1)} copy(bf16[1,4,32,128]{3,2,1,0:T(8,128)(2,1)S(1)} %fusion.3) | data formatting | bytes 65536
  37.3 22.5 %all-to-all-done.1 = bf16[16,1,16,2048]{3,2,1,0:T(8,128)(2,1)S(1)} async-done(((bf16[16,1,16,2048]{3,2,1,0:T(8,128)(2,1)}), bf16[16,1,16,2048]{3,2,1,0:T(8,128)(2,1)S(1)}, u32[]{:S(2)}, u32[]{:S(2)}) %all-to-all-start.1) | async-done | bytes 1048608 | tf_op jit(solution)/shard_map/all_to_all | solution.py:187
  59.9 0.9 %fusion = bf16[16,2048]{1,0:T(8,128)(2,1)} fusion(bf16[16,1,16,2048]{3,2,1,0:T(8,128)(2,1)S(1)} %all-to-all-done.1, f32[16,16]{1,0:T(8,128)S(1)} %copy.26), kind=kLoop, calls=%fused_computation.1 | loop fusion | flops 1540096 | bytes 1115136 | tf_op jit(solution)/shard_map/reduce_sum | solution.py:194
  (6 shorter events, 0.1 us)
Async XLA Ops:
  0.6 35.0 %copy-start = (bf16[4,256,512]{2,1,0:T(8,128)(2,1)S(1)}, bf16[4,256,512]{2,1,0:T(8,128)(2,1)}, u32[]{:S(2)}) copy-start(bf16[4,256,512]{2,1,0:T(8,128)(2,1)} %param.21) | copy-start | bytes 3145732
  19.8 3.7 %collective-permute-start = (bf16[8,16,2048]{2,1,0:T(8,128)(2,1)S(1)}, bf16[8,16,2048]{2,1,0:T(8,128)(2,1)S(1)}, u32[]{:S(2)}, u32[]{:S(2)}) collective-permute-start(bf16[8,16,2048]{2,1,0:T(8,128)(2,1)S(1)} %all_to_all.10), channel_id=1, source_target_pairs={{0,1},{1,0},{2,3},{3,2},{4,5},{5,4},{6,7},{7,6},{8,9},{9,8},{10,11... | collective-permute-start | bytes 1572872 | tf_op jit(solution)/shard_map/ppermute | solution.py:174
  23.5 0.7 %copy-start.1 = (f32[2048]{0:T(1024)S(1)}, f32[2048]{0:T(1024)}, u32[]{:S(2)}) copy-start(f32[2048]{0:T(1024)} %param.14) | copy-start | bytes 24580
  24.2 10.8 %copy-start.3 = (f32[16,8]{0,1:T(8,128)S(1)}, f32[16,8]{0,1:T(8,128)}, u32[]{:S(2)}) copy-start(f32[16,8]{0,1:T(8,128)} %param.16) | copy-start | bytes 1540
  24.2 10.9 %copy-start.4 = (s32[16,8]{0,1:T(8,128)S(1)}, s32[16,8]{0,1:T(8,128)}, u32[]{:S(2)}) copy-start(s32[16,8]{0,1:T(8,128)} %param.15) | copy-start | bytes 1540
  24.2 11.2 %copy-start.5 = (bf16[4,512]{1,0:T(4,128)(2,1)S(1)}, bf16[4,512]{1,0:T(4,128)(2,1)}, u32[]{:S(2)}) copy-start(bf16[4,512]{1,0:T(4,128)(2,1)} %param.23) | copy-start | bytes 12292
  24.2 11.2 %copy-start.6 = (bf16[4,512]{1,0:T(4,128)(2,1)S(1)}, bf16[4,512]{1,0:T(4,128)(2,1)}, u32[]{:S(2)}) copy-start(bf16[4,512]{1,0:T(4,128)(2,1)} %param.24) | copy-start | bytes 12292
  24.2 11.2 %copy-start.8 = (s32[4]{0:T(128)S(1)}, s32[4]{0:T(128)}, u32[]{:S(2)}) copy-start(s32[4]{0:T(128)} %param.25) | copy-start | bytes 52
  24.3 11.3 %copy-start.2 = (bf16[4,4096]{1,0:T(4,128)(2,1)S(1)}, bf16[4,4096]{1,0:T(4,128)(2,1)}, u32[]{:S(2)}) copy-start(bf16[4,4096]{1,0:T(4,128)(2,1)} %param.20) | copy-start | bytes 98308
  30.3 6.0 %copy-start.7 = (bf16[4,256,512]{2,1,0:T(8,128)(2,1)S(1)}, bf16[4,256,512]{2,1,0:T(8,128)(2,1)}, u32[]{:S(2)}) copy-start(bf16[4,256,512]{2,1,0:T(8,128)(2,1)} %param.22) | copy-start | bytes 3145732
  30.3 29.5 %all-to-all-start.1 = ((bf16[16,1,16,2048]{3,2,1,0:T(8,128)(2,1)}), bf16[16,1,16,2048]{3,2,1,0:T(8,128)(2,1)S(1)}, u32[]{:S(2)}, u32[]{:S(2)}) async-start(bf16[16,1,16,2048]{3,2,1,0:T(8,128)(2,1)} %bitcast.6), calls=%async_computation.1 | async-start | bytes 2097152 | tf_op jit(solution)/shard_map/all_to_all | solution.py:187

commit v10 on v9

--- a/solution.py
+++ b/solution.py
@@ -73,13 +73,15 @@
 
 def mlp_kernel(
     core_ref, gain_ref, same_ref, other_ref, gate_hbm, up_hbm, down_hbm, out_ref,
-    gate_buf, up_buf, down_buf, inner_buf, normed_buf, sems,
+    gate_buf, up_buf, down_buf, inner_buf, normed_buf, gain_buf, sems,
 ):
     expert = pl.program_id(0)
     chunks, _, chunk = gate_buf.shape
     chips = out_ref.shape[0]
     half = same_ref.shape[0]
     rows_here = half // chips
+    gain_copy = pltpu.make_async_copy(gain_ref, gain_buf, sems.at[2, 1])
+    gain_copy.start()
     copies = []
     for f in range(chunks):
         window = pl.ds(f * chunk, chunk)
@@ -92,7 +94,8 @@
         copies.append(pair)
     down_copy = pltpu.make_async_copy(down_hbm.at[expert], down_buf, sems.at[2, 0])
     down_copy.start()
-    gain = gain_ref[...]
+    gain_copy.wait()
+    gain = gain_buf[...]
     for part, rows_ref in enumerate((same_ref, other_ref)):
         widened = rows_ref[...].astype(jnp.float32)
         meansq = jnp.mean(widened * widened, axis=1, keepdims=True) + 1e-06
@@ -130,7 +133,7 @@
         num_scalar_prefetch=1,
         grid=(local_experts,),
         in_specs=[
-            pl.BlockSpec((1, features), lambda e, c: (0, 0)),
+            pl.BlockSpec(memory_space=pltpu.HBM),
             pl.BlockSpec((half, features), lambda e, c: (0, 0)),
             pl.BlockSpec((half, features), lambda e, c: (0, 0)),
             pl.BlockSpec(memory_space=pltpu.HBM),
@@ -146,7 +149,8 @@
             pltpu.VMEM((hidden, features), jnp.bfloat16),
             pltpu.VMEM((2, half, hidden), jnp.bfloat16),
             pltpu.VMEM((2, half, features), jnp.bfloat16),
-            pltpu.SemaphoreType.DMA((3, chunks)),
+            pltpu.VMEM((1, features), jnp.float32),
+            pltpu.SemaphoreType.DMA((3, max(chunks, 2))),
         ],
     )
     return pl.pallas_call(

time: 61.1 us -> 61 us (level)
  no operation moved by 1% of the time
where the time goes in v10:
time: 61 us; the launch traced here: 60.7 us
  waiting for transfers between devices  24.1 us (40%)
  blocking collectives  18.2 us (30%)
  starting transfers between devices  6.84 us (11%)
  Pallas kernels  6 us (10%)
  local copies, waits for them, and re-layouts  2.59 us (4%)
  other arithmetic  1.33 us (2%)
  matrix products  0.91 us (1%)
  between operations  0.74 us (1%)
    all_to_all x1, waiting for transfers between devices, spread_block(): returned = lax.all_to_all(produced, NODE, 0, 0, tiled=True)  22.5 us
    all_to_all x1, blocking collectives, spread_block(): same_core = lax.all_to_all(spread, 'chip', 0, 0, tiled=True)  18.2 us
    pallas_call x1, Pallas kernels, expert_mlp(): pl.pallas_call(mlp_kernel, grid_spec=grid_spec, out_shape=jax.ShapeDtypeS...  6 us
    all_to_all x1, starting transfers between devices, spread_block(): returned = lax.all_to_all(produced, NODE, 0, 0, tiled=True)  4.68 us
    ppermute x1, starting transfers between devices, spread_block(): lax.ppermute(same_core, 'core', [(i, (i + 1) % cores) for i in range(core...  2.16 us
    ppermute x1, waiting for transfers between devices, spread_block(): lax.ppermute(same_core, 'core', [(i, (i + 1) % cores) for i in range(core...  1.54 us
    unnamed x20, local copies, waits for them, and re-layouts  1.46 us
  transfers between devices with their start and end apart: 2, of which 2 were waited for; matrix products, arithmetic and copies ran while one was open for 4% of the time, Pallas kernels for 0%

profile of v10, /device:TPU:11, one launch (start us, length us, event | category | flops | bytes accessed | tf_op | source)
XLA Modules:
  0.0 60.7 jit_solution(1911830242850650243)
XLA Ops:
  0.6 0.0 copy-start
  0.6 1.0 %broadcast_in_dim.49 = bf16[8,16,2048]{2,1,0:T(8,128)(2,1)S(1)} broadcast(bf16[16,2048]{1,0:T(8,128)(2,1)} %param.13), dimensions={1,2} | broadcast | bytes 589824 | tf_op jit(solution)/shard_map/broadcast_in_dim | solution.py:176
  1.6 18.2 %all_to_all.10 = bf16[8,16,2048]{2,1,0:T(8,128)(2,1)S(1)} all-to-all(bf16[8,16,2048]{2,1,0:T(8,128)(2,1)S(1)} %broadcast_in_dim.49), channel_id=1, replica_groups=mesh['group'=2,'chip'=8,'core'=2] {'chip'}, dimensions={0} | all-to-all | bytes 1048576 | tf_op jit(solution)/shard_map/all_to_all | solution.py:177
  19.8 2.2 %collective-permute-start = (bf16[8,16,2048]{2,1,0:T(8,128)(2,1)S(1)}, bf16[8,16,2048]{2,1,0:T(8,128)(2,1)S(1)}, u32[]{:S(2)}, u32[]{:S(2)}) collective-permute-start(bf16[8,16,2048]{2,1,0:T(8,128)(2,1)S(1)} %all_to_all.10), channel_id=1, source_target_pairs={{0,1},{1,0},{2,3},{3,2},{4,5},{5,4},{6,7},{7,6},{8,9},{9,8},{10,11... | collective-permute-start | bytes 1572872 | tf_op jit(solution)/shard_map/ppermute | solution.py:178
  22.0 1.5 %collective-permute-done = bf16[8,16,2048]{2,1,0:T(8,128)(2,1)S(1)} collective-permute-done((bf16[8,16,2048]{2,1,0:T(8,128)(2,1)S(1)}, bf16[8,16,2048]{2,1,0:T(8,128)(2,1)S(1)}, u32[]{:S(2)}, u32[]{:S(2)}) %collective-permute-start) | collective-permute-done | bytes 524320 | tf_op jit(solution)/shard_map/ppermute | solution.py:178
  23.5 0.0 copy-start.1
  23.5 0.7 %copy-done.1 = f32[2048]{0:T(1024)S(1)} copy-done((f32[2048]{0:T(1024)S(1)}, f32[2048]{0:T(1024)}, u32[]{:S(2)}) %copy-start.1) | copy-done | bytes 8216
  24.2 0.0 copy-start.3
  24.2 0.0 copy-start.4
  24.2 0.0 copy-start.5
  24.2 0.0 copy-start.6
  24.2 0.0 copy-start.8
  24.3 0.0 copy-start.2
  24.3 6.0 %shard_map.140 = bf16[1,8,2,16,2048]{4,3,2,1,0:T(8,128)(2,1)} custom-call(s32[1]{0:T(128)} %bitcast.1.core_ref, f32[1,2048]{1,0:T(1,128)S(1)} %bitcast.47, bf16[128,2048]{1,0:T(8,128)(2,1)S(1)} %bitcast.45, bf16[128,2048]{1,0:T(8,128)(2,1)S(1)} %bitcast.46, bf16[1,2048,768]{2,1,0:T(8,128)(2,1)} %gate_hbm.1, bf16[1,2048,768]{2,1,0:T(8,128)(2,1)} %up_hbm.1, ...), custom_call_target="tpu_custom_call" | custom-call | tf_op jit(solution)/shard_map/pallas_call | solution.py:156
  30.3 0.0 copy-start.7
  30.3 4.7 %all-to-all-start.1 = ((bf16[16,1,16,2048]{3,2,1,0:T(8,128)(2,1)}), bf16[16,1,16,2048]{3,2,1,0:T(8,128)(2,1)S(1)}, u32[]{:S(2)}, u32[]{:S(2)}) async-start(bf16[16,1,16,2048]{3,2,1,0:T(8,128)(2,1)} %bitcast.6), calls=%async_computation.1 | async-start | bytes 2097152 | tf_op jit(solution)/shard_map/all_to_all | solution.py:191
  35.0 0.0 copy-done.3
  35.0 0.1 copy.25
  35.1 0.0 copy-done.4
  35.1 0.1 copy.24
  35.1 0.1 select_reduce_fusion
  35.3 0.1 copy.26
  35.3 0.0 copy-done.5
  35.4 0.0 copy-done.6
  35.4 0.0 copy-done.8
  35.4 0.1 iota_compare_fusion.1
  35.5 0.0 copy-done.2
  35.5 0.1 fusion.13
  35.6 0.0 copy-done
  35.6 0.5 fusion.21
  36.1 0.2 fusion.8
  36.3 0.0 copy-done.7
  36.3 0.3 fusion.3
  36.6 0.6 %copy.57 = bf16[1,4,32,128]{3,1,2,0:T(4,128)(2,1)} copy(bf16[1,4,32,128]{3,2,1,0:T(8,128)(2,1)S(1)} %fusion.3) | data formatting | bytes 65536
  37.3 22.5 %all-to-all-done.1 = bf16[16,1,16,2048]{3,2,1,0:T(8,128)(2,1)S(1)} async-done(((bf16[16,1,16,2048]{3,2,1,0:T(8,128)(2,1)}), bf16[16,1,16,2048]{3,2,1,0:T(8,128)(2,1)S(1)}, u32[]{:S(2)}, u32[]{:S(2)}) %all-to-all-start.1) | async-done | bytes 1048608 | tf_op jit(solution)/shard_map/all_to_all | solution.py:191
  59.8 0.9 %fusion = bf16[16,2048]{1,0:T(8,128)(2,1)} fusion(bf16[16,1,16,2048]{3,2,1,0:T(8,128)(2,1)S(1)} %all-to-all-done.1, f32[16,16]{1,0:T(8,128)S(1)} %copy.26), kind=kLoop, calls=%fused_computation.1 | loop fusion | flops 1540096 | bytes 1115136 | tf_op jit(solution)/shard_map/reduce_sum | solution.py:198
  (6 shorter events, 0.1 us)
Async XLA Ops:
  0.6 35.0 %copy-start = (bf16[4,256,512]{2,1,0:T(8,128)(2,1)S(1)}, bf16[4,256,512]{2,1,0:T(8,128)(2,1)}, u32[]{:S(2)}) copy-start(bf16[4,256,512]{2,1,0:T(8,128)(2,1)} %param.21) | copy-start | bytes 3145732
  19.8 3.7 %collective-permute-start = (bf16[8,16,2048]{2,1,0:T(8,128)(2,1)S(1)}, bf16[8,16,2048]{2,1,0:T(8,128)(2,1)S(1)}, u32[]{:S(2)}, u32[]{:S(2)}) collective-permute-start(bf16[8,16,2048]{2,1,0:T(8,128)(2,1)S(1)} %all_to_all.10), channel_id=1, source_target_pairs={{0,1},{1,0},{2,3},{3,2},{4,5},{5,4},{6,7},{7,6},{8,9},{9,8},{10,11... | collective-permute-start | bytes 1572872 | tf_op jit(solution)/shard_map/ppermute | solution.py:178
  23.5 0.7 %copy-start.1 = (f32[2048]{0:T(1024)S(1)}, f32[2048]{0:T(1024)}, u32[]{:S(2)}) copy-start(f32[2048]{0:T(1024)} %param.14) | copy-start | bytes 24580
  24.2 10.7 %copy-start.3 = (f32[16,8]{0,1:T(8,128)S(1)}, f32[16,8]{0,1:T(8,128)}, u32[]{:S(2)}) copy-start(f32[16,8]{0,1:T(8,128)} %param.16) | copy-start | bytes 1540
  24.2 10.8 %copy-start.4 = (s32[16,8]{0,1:T(8,128)S(1)}, s32[16,8]{0,1:T(8,128)}, u32[]{:S(2)}) copy-start(s32[16,8]{0,1:T(8,128)} %param.15) | copy-start | bytes 1540
  24.2 11.1 %copy-start.5 = (bf16[4,512]{1,0:T(4,128)(2,1)S(1)}, bf16[4,512]{1,0:T(4,128)(2,1)}, u32[]{:S(2)}) copy-start(bf16[4,512]{1,0:T(4,128)(2,1)} %param.23) | copy-start | bytes 12292
  24.2 11.1 %copy-start.6 = (bf16[4,512]{1,0:T(4,128)(2,1)S(1)}, bf16[4,512]{1,0:T(4,128)(2,1)}, u32[]{:S(2)}) copy-start(bf16[4,512]{1,0:T(4,128)(2,1)} %param.24) | copy-start | bytes 12292
  24.2 11.1 %copy-start.8 = (s32[4]{0:T(128)S(1)}, s32[4]{0:T(128)}, u32[]{:S(2)}) copy-start(s32[4]{0:T(128)} %param.25) | copy-start | bytes 52
  24.3 11.2 %copy-start.2 = (bf16[4,4096]{1,0:T(4,128)(2,1)S(1)}, bf16[4,4096]{1,0:T(4,128)(2,1)}, u32[]{:S(2)}) copy-start(bf16[4,4096]{1,0:T(4,128)(2,1)} %param.20) | copy-start | bytes 98308
  30.3 6.0 %copy-start.7 = (bf16[4,256,512]{2,1,0:T(8,128)(2,1)S(1)}, bf16[4,256,512]{2,1,0:T(8,128)(2,1)}, u32[]{:S(2)}) copy-start(bf16[4,256,512]{2,1,0:T(8,128)(2,1)} %param.22) | copy-start | bytes 3145732
  30.3 29.5 %all-to-all-start.1 = ((bf16[16,1,16,2048]{3,2,1,0:T(8,128)(2,1)}), bf16[16,1,16,2048]{3,2,1,0:T(8,128)(2,1)S(1)}, u32[]{:S(2)}, u32[]{:S(2)}) async-start(bf16[16,1,16,2048]{3,2,1,0:T(8,128)(2,1)} %bitcast.6), calls=%async_computation.1 | async-start | bytes 2097152 | tf_op jit(solution)/shard_map/all_to_all | solution.py:191

commit v11 on v10

--- a/solution.py
+++ b/solution.py
@@ -95,7 +95,7 @@
     down_copy = pltpu.make_async_copy(down_hbm.at[expert], down_buf, sems.at[2, 0])
     down_copy.start()
     gain_copy.wait()
-    gain = gain_buf[...]
+    gain = gain_buf[0:1, :]
     for part, rows_ref in enumerate((same_ref, other_ref)):
         widened = rows_ref[...].astype(jnp.float32)
         meansq = jnp.mean(widened * widened, axis=1, keepdims=True) + 1e-06
@@ -149,7 +149,7 @@
             pltpu.VMEM((hidden, features), jnp.bfloat16),
             pltpu.VMEM((2, half, hidden), jnp.bfloat16),
             pltpu.VMEM((2, half, features), jnp.bfloat16),
-            pltpu.VMEM((1, features), jnp.float32),
+            pltpu.VMEM((8, features), jnp.float32),
             pltpu.SemaphoreType.DMA((3, max(chunks, 2))),
         ],
     )
@@ -162,7 +162,7 @@
         compiler_params=pltpu.CompilerParams(
             dimension_semantics=("arbitrary",), vmem_limit_bytes=50 * 1024 * 1024
         ),
-    )(core.reshape(1), norm_gain.reshape(1, -1), same_rows, other_rows, w_gate, w_up, w_down)
+    )(core.reshape(1), norm_gain, same_rows, other_rows, w_gate, w_up, w_down)
 
 
 def spread_block(states, norm_gain, picks, gate_weights, w_gate, w_up, w_down):
@@ -176,9 +176,10 @@
     spread = jnp.broadcast_to(states[None], (chips, rows_here, features))
     same_core = lax.all_to_all(spread, "chip", 0, 0, tiled=True)
     other_core = lax.ppermute(same_core, "core", [(i, (i + 1) % cores) for i in range(cores)])
+    gain_rows = jnp.broadcast_to(norm_gain[None, :], (8, features))
     produced = expert_mlp(
         core.astype(jnp.int32),
-        norm_gain,
+        gain_rows,
         same_core.reshape(chips * rows_here, features),
         other_core.reshape(chips * rows_here, features),
         w_gate,

time: 61 us -> 61.1 us (level)
    broadcast_in_dim x0 -> x1, local copies, waits for them, and re-layouts: none -> 0.7 us  [spread_block(): gain_rows = jnp.broadcast_to(norm_gain[None, :], (8, features))]
    unnamed x20 -> x18, local copies, waits for them, and re-layouts: 1.46 us -> 0.77 us
where the time goes in v11:
time: 61.1 us; the launch traced here: 60.8 us
  waiting for transfers between devices  24.1 us (39%)
  blocking collectives  18.2 us (30%)
  starting transfers between devices  6.84 us (11%)
  Pallas kernels  6.05 us (10%)
  local copies, waits for them, and re-layouts  2.6 us (4%)
  other arithmetic  1.33 us (2%)
  matrix products  0.91 us (1%)
  between operations  0.76 us (1%)
    all_to_all x1, waiting for transfers between devices, spread_block(): returned = lax.all_to_all(produced, NODE, 0, 0, tiled=True)  22.5 us
    all_to_all x1, blocking collectives, spread_block(): same_core = lax.all_to_all(spread, 'chip', 0, 0, tiled=True)  18.2 us
    pallas_call x1, Pallas kernels, expert_mlp(): pl.pallas_call(mlp_kernel, grid_spec=grid_spec, out_shape=jax.ShapeDtypeS...  6.05 us
    all_to_all x1, starting transfers between devices, spread_block(): returned = lax.all_to_all(produced, NODE, 0, 0, tiled=True)  4.68 us
    ppermute x1, starting transfers between devices, spread_block(): lax.ppermute(same_core, 'core', [(i, (i + 1) % cores) for i in range(core...  2.16 us
    ppermute x1, waiting for transfers between devices, spread_block(): lax.ppermute(same_core, 'core', [(i, (i + 1) % cores) for i in range(core...  1.54 us
  transfers between devices with their start and end apart: 2, of which 2 were waited for; matrix products, arithmetic and copies ran while one was open for 4% of the time, Pallas kernels for 0%

profile of v11, /device:TPU:11, one launch (start us, length us, event | category | flops | bytes accessed | tf_op | source)
XLA Modules:
  0.0 60.8 jit_solution(13468771640753157201)
XLA Ops:
  0.6 0.0 copy-start
  0.6 1.0 %broadcast_in_dim.56 = bf16[8,16,2048]{2,1,0:T(8,128)(2,1)S(1)} broadcast(bf16[16,2048]{1,0:T(8,128)(2,1)} %param.13), dimensions={1,2} | broadcast | bytes 589824 | tf_op jit(solution)/shard_map/broadcast_in_dim | solution.py:176
  1.6 18.2 %all_to_all.10 = bf16[8,16,2048]{2,1,0:T(8,128)(2,1)S(1)} all-to-all(bf16[8,16,2048]{2,1,0:T(8,128)(2,1)S(1)} %broadcast_in_dim.56), channel_id=1, replica_groups=mesh['group'=2,'chip'=8,'core'=2] {'chip'}, dimensions={0} | all-to-all | bytes 1048576 | tf_op jit(solution)/shard_map/all_to_all | solution.py:177
  19.8 2.2 %collective-permute-start = (bf16[8,16,2048]{2,1,0:T(8,128)(2,1)S(1)}, bf16[8,16,2048]{2,1,0:T(8,128)(2,1)S(1)}, u32[]{:S(2)}, u32[]{:S(2)}) collective-permute-start(bf16[8,16,2048]{2,1,0:T(8,128)(2,1)S(1)} %all_to_all.10), channel_id=1, source_target_pairs={{0,1},{1,0},{2,3},{3,2},{4,5},{5,4},{6,7},{7,6},{8,9},{9,8},{10,11... | collective-permute-start | bytes 1572872 | tf_op jit(solution)/shard_map/ppermute | solution.py:178
  22.0 1.5 %collective-permute-done = bf16[8,16,2048]{2,1,0:T(8,128)(2,1)S(1)} collective-permute-done((bf16[8,16,2048]{2,1,0:T(8,128)(2,1)S(1)}, bf16[8,16,2048]{2,1,0:T(8,128)(2,1)S(1)}, u32[]{:S(2)}, u32[]{:S(2)}) %collective-permute-start) | collective-permute-done | bytes 524320 | tf_op jit(solution)/shard_map/ppermute | solution.py:178
  23.5 0.7 %broadcast_in_dim.55.gain_ref = f32[8,2048]{1,0:T(8,128)S(1)} broadcast(f32[2048]{0:T(1024)} %param.14), dimensions={1} | broadcast | bytes 73728 | tf_op jit(solution)/shard_map/broadcast_in_dim | solution.py:179
  24.2 0.0 copy-start.2
  24.2 0.0 copy-start.3
  24.2 0.0 copy-start.4
  24.3 0.0 copy-start.5
  24.3 0.0 copy-start.7
  24.3 0.0 copy-start.1
  24.3 6.0 %shard_map.140 = bf16[1,8,2,16,2048]{4,3,2,1,0:T(8,128)(2,1)} custom-call(s32[1]{0:T(128)} %bitcast.1.core_ref, f32[8,2048]{1,0:T(8,128)S(1)} %broadcast_in_dim.55.gain_ref, bf16[128,2048]{1,0:T(8,128)(2,1)S(1)} %bitcast.44, bf16[128,2048]{1,0:T(8,128)(2,1)S(1)} %bitcast.45, bf16[1,2048,768]{2,1,0:T(8,128)(2,1)} %gate_hbm.1, bf16[1,2048,768]{2,1,0:T(8,128)(2,1)} %up_hbm.1, ...), custom_call_target="tpu_custom_call" | custom-call | tf_op jit(solution)/shard_map/pallas_call | solution.py:156
  30.3 0.0 copy-start.6
  30.4 4.7 %all-to-all-start.1 = ((bf16[16,1,16,2048]{3,2,1,0:T(8,128)(2,1)}), bf16[16,1,16,2048]{3,2,1,0:T(8,128)(2,1)S(1)}, u32[]{:S(2)}, u32[]{:S(2)}) async-start(bf16[16,1,16,2048]{3,2,1,0:T(8,128)(2,1)} %bitcast.5), calls=%async_computation.1 | async-start | bytes 2097152 | tf_op jit(solution)/shard_map/all_to_all | solution.py:192
  35.0 0.0 copy-done.2
  35.1 0.1 copy.25
  35.1 0.0 copy-done.3
  35.1 0.1 copy.24
  35.2 0.1 select_reduce_fusion
  35.3 0.1 copy.26
  35.4 0.0 copy-done.4
  35.4 0.0 copy-done.5
  35.4 0.0 copy-done.7
  35.5 0.1 iota_compare_fusion.1
  35.5 0.0 copy-done.1
  35.5 0.1 fusion.13
  35.7 0.0 copy-done
  35.7 0.5 fusion.21
  36.1 0.2 fusion.8
  36.4 0.0 copy-done.6
  36.4 0.3 fusion.3
  36.7 0.6 %copy.57 = bf16[1,4,32,128]{3,1,2,0:T(4,128)(2,1)} copy(bf16[1,4,32,128]{3,2,1,0:T(8,128)(2,1)S(1)} %fusion.3) | data formatting | bytes 65536
  37.3 22.5 %all-to-all-done.1 = bf16[16,1,16,2048]{3,2,1,0:T(8,128)(2,1)S(1)} async-done(((bf16[16,1,16,2048]{3,2,1,0:T(8,128)(2,1)}), bf16[16,1,16,2048]{3,2,1,0:T(8,128)(2,1)S(1)}, u32[]{:S(2)}, u32[]{:S(2)}) %all-to-all-start.1) | async-done | bytes 1048608 | tf_op jit(solution)/shard_map/all_to_all | solution.py:192
  59.9 0.9 %fusion = bf16[16,2048]{1,0:T(8,128)(2,1)} fusion(bf16[16,1,16,2048]{3,2,1,0:T(8,128)(2,1)S(1)} %all-to-all-done.1, f32[16,16]{1,0:T(8,128)S(1)} %copy.26), kind=kLoop, calls=%fused_computation.1 | loop fusion | flops 1540096 | bytes 1115136 | tf_op jit(solution)/shard_map/reduce_sum | solution.py:199
  (6 shorter events, 0.1 us)
Async XLA Ops:
  0.6 35.0 %copy-start = (bf16[4,256,512]{2,1,0:T(8,128)(2,1)S(1)}, bf16[4,256,512]{2,1,0:T(8,128)(2,1)}, u32[]{:S(2)}) copy-start(bf16[4,256,512]{2,1,0:T(8,128)(2,1)} %param.21) | copy-start | bytes 3145732
  19.8 3.7 %collective-permute-start = (bf16[8,16,2048]{2,1,0:T(8,128)(2,1)S(1)}, bf16[8,16,2048]{2,1,0:T(8,128)(2,1)S(1)}, u32[]{:S(2)}, u32[]{:S(2)}) collective-permute-start(bf16[8,16,2048]{2,1,0:T(8,128)(2,1)S(1)} %all_to_all.10), channel_id=1, source_target_pairs={{0,1},{1,0},{2,3},{3,2},{4,5},{5,4},{6,7},{7,6},{8,9},{9,8},{10,11... | collective-permute-start | bytes 1572872 | tf_op jit(solution)/shard_map/ppermute | solution.py:178
  24.2 10.8 %copy-start.2 = (f32[16,8]{0,1:T(8,128)S(1)}, f32[16,8]{0,1:T(8,128)}, u32[]{:S(2)}) copy-start(f32[16,8]{0,1:T(8,128)} %param.16) | copy-start | bytes 1540
  24.2 10.9 %copy-start.3 = (s32[16,8]{0,1:T(8,128)S(1)}, s32[16,8]{0,1:T(8,128)}, u32[]{:S(2)}) copy-start(s32[16,8]{0,1:T(8,128)} %param.15) | copy-start | bytes 1540
  24.2 11.2 %copy-start.4 = (bf16[4,512]{1,0:T(4,128)(2,1)S(1)}, bf16[4,512]{1,0:T(4,128)(2,1)}, u32[]{:S(2)}) copy-start(bf16[4,512]{1,0:T(4,128)(2,1)} %param.23) | copy-start | bytes 12292
  24.3 11.2 %copy-start.5 = (bf16[4,512]{1,0:T(4,128)(2,1)S(1)}, bf16[4,512]{1,0:T(4,128)(2,1)}, u32[]{:S(2)}) copy-start(bf16[4,512]{1,0:T(4,128)(2,1)} %param.24) | copy-start | bytes 12292
  24.3 11.2 %copy-start.7 = (s32[4]{0:T(128)S(1)}, s32[4]{0:T(128)}, u32[]{:S(2)}) copy-start(s32[4]{0:T(128)} %param.25) | copy-start | bytes 52
  24.3 11.3 %copy-start.1 = (bf16[4,4096]{1,0:T(4,128)(2,1)S(1)}, bf16[4,4096]{1,0:T(4,128)(2,1)}, u32[]{:S(2)}) copy-start(bf16[4,4096]{1,0:T(4,128)(2,1)} %param.20) | copy-start | bytes 98308
  30.3 6.0 %copy-start.6 = (bf16[4,256,512]{2,1,0:T(8,128)(2,1)S(1)}, bf16[4,256,512]{2,1,0:T(8,128)(2,1)}, u32[]{:S(2)}) copy-start(bf16[4,256,512]{2,1,0:T(8,128)(2,1)} %param.22) | copy-start | bytes 3145732
  30.4 29.5 %all-to-all-start.1 = ((bf16[16,1,16,2048]{3,2,1,0:T(8,128)(2,1)}), bf16[16,1,16,2048]{3,2,1,0:T(8,128)(2,1)S(1)}, u32[]{:S(2)}, u32[]{:S(2)}) async-start(bf16[16,1,16,2048]{3,2,1,0:T(8,128)(2,1)} %bitcast.5), calls=%async_computation.1 | async-start | bytes 2097152 | tf_op jit(solution)/shard_map/all_to_all | solution.py:192

commit v12 on v11

--- a/solution.py
+++ b/solution.py
@@ -76,51 +76,60 @@
     gate_buf, up_buf, down_buf, inner_buf, normed_buf, gain_buf, sems,
 ):
     expert = pl.program_id(0)
+    gain_copy = pltpu.make_async_copy(gain_ref, gain_buf, sems.at[3, 0])
+    gain_copy.start()
     chunks, _, chunk = gate_buf.shape
+    columns, _, width = down_buf.shape
     chips = out_ref.shape[0]
     half = same_ref.shape[0]
     rows_here = half // chips
-    gain_copy = pltpu.make_async_copy(gain_ref, gain_buf, sems.at[2, 1])
-    gain_copy.start()
-    copies = []
+    stages = []
     for f in range(chunks):
         window = pl.ds(f * chunk, chunk)
-        pair = (
+        stages.append((
             pltpu.make_async_copy(gate_hbm.at[expert, :, window], gate_buf.at[f], sems.at[0, f]),
             pltpu.make_async_copy(up_hbm.at[expert, :, window], up_buf.at[f], sems.at[1, f]),
+        ))
+    for j in range(columns):
+        window = pl.ds(j * width, width)
+        stages.append(
+            (pltpu.make_async_copy(down_hbm.at[expert, :, window], down_buf.at[j], sems.at[2, j]),)
         )
-        for copy in pair:
+    for stage in stages[:2]:
+        for copy in stage:
             copy.start()
-        copies.append(pair)
-    down_copy = pltpu.make_async_copy(down_hbm.at[expert], down_buf, sems.at[2, 0])
-    down_copy.start()
     gain_copy.wait()
     gain = gain_buf[0:1, :]
     for part, rows_ref in enumerate((same_ref, other_ref)):
         widened = rows_ref[...].astype(jnp.float32)
         meansq = jnp.mean(widened * widened, axis=1, keepdims=True) + 1e-06
         normed_buf[part] = (widened / jnp.sqrt(meansq) * gain).astype(jnp.bfloat16)
-    for f in range(chunks):
-        for copy in copies[f]:
+    core = core_ref[0]
+    for index, stage in enumerate(stages):
+        for copy in stage:
             copy.wait()
-        gate_block = gate_buf[f]
-        up_block = up_buf[f]
-        for part in range(2):
-            rows = normed_buf[part]
-            gate_part = jnp.dot(rows, gate_block, preferred_element_type=jnp.float32)
-            up_part = jnp.dot(rows, up_block, preferred_element_type=jnp.float32)
-            inner_buf[part, :, f * chunk : (f + 1) * chunk] = (
-                jax.nn.silu(gate_part) * up_part
-            ).astype(jnp.bfloat16)
-    down_copy.wait()
-    down_block = down_buf[...]
-    core = core_ref[0]
-    for part in range(2):
-        produced = jnp.dot(inner_buf[part], down_block, preferred_element_type=jnp.float32)
-        target = (core + part) % 2
-        out_ref[:, pl.ds(target, 1)] = (
-            produced.reshape(chips, 1, rows_here, -1).astype(out_ref.dtype)
-        )
+        if index + 2 < len(stages):
+            for copy in stages[index + 2]:
+                copy.start()
+        if index < chunks:
+            gate_block = gate_buf[index]
+            up_block = up_buf[index]
+            for part in range(2):
+                rows = normed_buf[part]
+                gate_part = jnp.dot(rows, gate_block, preferred_element_type=jnp.float32)
+                up_part = jnp.dot(rows, up_block, preferred_element_type=jnp.float32)
+                inner_buf[part, :, index * chunk : (index + 1) * chunk] = (
+                    jax.nn.silu(gate_part) * up_part
+                ).astype(jnp.bfloat16)
+        else:
+            j = index - chunks
+            down_block = down_buf[j]
+            for part in range(2):
+                produced = jnp.dot(inner_buf[part], down_block, preferred_element_type=jnp.float32)
+                target = (core + part) % 2
+                out_ref[:, pl.ds(target, 1), :, j * width : (j + 1) * width] = (
+                    produced.reshape(chips, 1, rows_here, width).astype(out_ref.dtype)
+                )
 
 
 def expert_mlp(core, norm_gain, same_rows, other_rows, w_gate, w_up, w_down, chips):
@@ -129,6 +138,7 @@
     rows_here = half // chips
     chunk = 256 if hidden % 256 == 0 else hidden
     chunks = hidden // chunk
+    columns = 4 if features % 512 == 0 else 1
     grid_spec = pltpu.PrefetchScalarGridSpec(
         num_scalar_prefetch=1,
         grid=(local_experts,),
@@ -146,11 +156,11 @@
         scratch_shapes=[
             pltpu.VMEM((chunks, features, chunk), jnp.bfloat16),
             pltpu.VMEM((chunks, features, chunk), jnp.bfloat16),
-            pltpu.VMEM((hidden, features), jnp.bfloat16),
+            pltpu.VMEM((columns, hidden, features // columns), jnp.bfloat16),
             pltpu.VMEM((2, half, hidden), jnp.bfloat16),
             pltpu.VMEM((2, half, features), jnp.bfloat16),
             pltpu.VMEM((8, features), jnp.float32),
-            pltpu.SemaphoreType.DMA((3, max(chunks, 2))),
+            pltpu.SemaphoreType.DMA((4, max(chunks, columns))),
         ],
     )
     return pl.pallas_call(

time: 61.1 us -> 62.4 us (1.021)
  Pallas kernels: 6.05 us -> 7.26 us
    pallas_call x1, Pallas kernels: 6.05 us -> 7.26 us  [expert_mlp(): pl.pallas_call(mlp_kernel, grid_spec=grid_spec, out_shape=jax.ShapeDtypeS...]
where the time goes in v12:
time: 62.4 us; the launch traced here: 62 us
  waiting for transfers between devices  24.1 us (39%)
  blocking collectives  18.2 us (29%)
  Pallas kernels  7.26 us (12%)
  starting transfers between devices  6.84 us (11%)
  local copies, waits for them, and re-layouts  2.6 us (4%)
  other arithmetic  1.33 us (2%)
  matrix products  0.91 us (1%)
  between operations  0.76 us (1%)
    all_to_all x1, waiting for transfers between devices, spread_block(): returned = lax.all_to_all(produced, NODE, 0, 0, tiled=True)  22.5 us
    all_to_all x1, blocking collectives, spread_block(): same_core = lax.all_to_all(spread, 'chip', 0, 0, tiled=True)  18.2 us
    pallas_call x1, Pallas kernels, expert_mlp(): pl.pallas_call(mlp_kernel, grid_spec=grid_spec, out_shape=jax.ShapeDtypeS...  7.26 us
    all_to_all x1, starting transfers between devices, spread_block(): returned = lax.all_to_all(produced, NODE, 0, 0, tiled=True)  4.68 us
    ppermute x1, starting transfers between devices, spread_block(): lax.ppermute(same_core, 'core', [(i, (i + 1) % cores) for i in range(core...  2.16 us
    ppermute x1, waiting for transfers between devices, spread_block(): lax.ppermute(same_core, 'core', [(i, (i + 1) % cores) for i in range(core...  1.54 us
  transfers between devices with their start and end apart: 2, of which 2 were waited for; matrix products, arithmetic and copies ran while one was open for 4% of the time, Pallas kernels for 0%

profile of v12, /device:TPU:11, one launch (start us, length us, event | category | flops | bytes accessed | tf_op | source)
XLA Modules:
  0.0 62.0 jit_solution(2491445417018403582)
XLA Ops:
  0.6 0.0 copy-start
  0.6 1.0 %broadcast_in_dim.56 = bf16[8,16,2048]{2,1,0:T(8,128)(2,1)S(1)} broadcast(bf16[16,2048]{1,0:T(8,128)(2,1)} %param.13), dimensions={1,2} | broadcast | bytes 589824 | tf_op jit(solution)/shard_map/broadcast_in_dim | solution.py:186
  1.6 18.2 %all_to_all.10 = bf16[8,16,2048]{2,1,0:T(8,128)(2,1)S(1)} all-to-all(bf16[8,16,2048]{2,1,0:T(8,128)(2,1)S(1)} %broadcast_in_dim.56), channel_id=1, replica_groups=mesh['group'=2,'chip'=8,'core'=2] {'chip'}, dimensions={0} | all-to-all | bytes 1048576 | tf_op jit(solution)/shard_map/all_to_all | solution.py:187
  19.8 2.2 %collective-permute-start = (bf16[8,16,2048]{2,1,0:T(8,128)(2,1)S(1)}, bf16[8,16,2048]{2,1,0:T(8,128)(2,1)S(1)}, u32[]{:S(2)}, u32[]{:S(2)}) collective-permute-start(bf16[8,16,2048]{2,1,0:T(8,128)(2,1)S(1)} %all_to_all.10), channel_id=1, source_target_pairs={{0,1},{1,0},{2,3},{3,2},{4,5},{5,4},{6,7},{7,6},{8,9},{9,8},{10,11... | collective-permute-start | bytes 1572872 | tf_op jit(solution)/shard_map/ppermute | solution.py:188
  22.0 1.5 %collective-permute-done = bf16[8,16,2048]{2,1,0:T(8,128)(2,1)S(1)} collective-permute-done((bf16[8,16,2048]{2,1,0:T(8,128)(2,1)S(1)}, bf16[8,16,2048]{2,1,0:T(8,128)(2,1)S(1)}, u32[]{:S(2)}, u32[]{:S(2)}) %collective-permute-start) | collective-permute-done | bytes 524320 | tf_op jit(solution)/shard_map/ppermute | solution.py:188
  23.5 0.7 %broadcast_in_dim.55.gain_ref = f32[8,2048]{1,0:T(8,128)S(1)} broadcast(f32[2048]{0:T(1024)} %param.14), dimensions={1} | broadcast | bytes 73728 | tf_op jit(solution)/shard_map/broadcast_in_dim | solution.py:189
  24.2 0.0 copy-start.2
  24.2 0.0 copy-start.3
  24.2 0.0 copy-start.4
  24.3 0.0 copy-start.5
  24.3 0.0 copy-start.7
  24.3 0.0 copy-start.1
  24.3 7.3 %shard_map.140 = bf16[1,8,2,16,2048]{4,3,2,1,0:T(8,128)(2,1)} custom-call(s32[1]{0:T(128)} %bitcast.1.core_ref, f32[8,2048]{1,0:T(8,128)S(1)} %broadcast_in_dim.55.gain_ref, bf16[128,2048]{1,0:T(8,128)(2,1)S(1)} %bitcast.44, bf16[128,2048]{1,0:T(8,128)(2,1)S(1)} %bitcast.45, bf16[1,2048,768]{2,1,0:T(8,128)(2,1)} %gate_hbm.1, bf16[1,2048,768]{2,1,0:T(8,128)(2,1)} %up_hbm.1, ...), custom_call_target="tpu_custom_call" | custom-call | tf_op jit(solution)/shard_map/pallas_call | solution.py:166
  31.6 0.0 copy-start.6
  31.6 4.7 %all-to-all-start.1 = ((bf16[16,1,16,2048]{3,2,1,0:T(8,128)(2,1)}), bf16[16,1,16,2048]{3,2,1,0:T(8,128)(2,1)S(1)}, u32[]{:S(2)}, u32[]{:S(2)}) async-start(bf16[16,1,16,2048]{3,2,1,0:T(8,128)(2,1)} %bitcast.5), calls=%async_computation.1 | async-start | bytes 2097152 | tf_op jit(solution)/shard_map/all_to_all | solution.py:202
  36.2 0.0 copy-done.2
  36.3 0.1 copy.25
  36.4 0.0 copy-done.3
  36.4 0.1 copy.24
  36.4 0.1 select_reduce_fusion
  36.5 0.1 copy.26
  36.6 0.0 copy-done.4
  36.6 0.0 copy-done.5
  36.7 0.0 copy-done.7
  36.7 0.1 iota_compare_fusion.1
  36.7 0.0 copy-done.1
  36.7 0.1 fusion.13
  36.9 0.0 copy-done
  36.9 0.5 fusion.21
  37.4 0.2 fusion.8
  37.6 0.0 copy-done.6
  37.6 0.3 fusion.3
  37.9 0.6 %copy.57 = bf16[1,4,32,128]{3,1,2,0:T(4,128)(2,1)} copy(bf16[1,4,32,128]{3,2,1,0:T(8,128)(2,1)S(1)} %fusion.3) | data formatting | bytes 65536
  38.5 22.5 %all-to-all-done.1 = bf16[16,1,16,2048]{3,2,1,0:T(8,128)(2,1)S(1)} async-done(((bf16[16,1,16,2048]{3,2,1,0:T(8,128)(2,1)}), bf16[16,1,16,2048]{3,2,1,0:T(8,128)(2,1)S(1)}, u32[]{:S(2)}, u32[]{:S(2)}) %all-to-all-start.1) | async-done | bytes 1048608 | tf_op jit(solution)/shard_map/all_to_all | solution.py:202
  61.1 0.9 %fusion = bf16[16,2048]{1,0:T(8,128)(2,1)} fusion(bf16[16,1,16,2048]{3,2,1,0:T(8,128)(2,1)S(1)} %all-to-all-done.1, f32[16,16]{1,0:T(8,128)S(1)} %copy.26), kind=kLoop, calls=%fused_computation.1 | loop fusion | flops 1540096 | bytes 1115136 | tf_op jit(solution)/shard_map/reduce_sum | solution.py:209
  (6 shorter events, 0.1 us)
Async XLA Ops:
  0.6 36.2 %copy-start = (bf16[4,256,512]{2,1,0:T(8,128)(2,1)S(1)}, bf16[4,256,512]{2,1,0:T(8,128)(2,1)}, u32[]{:S(2)}) copy-start(bf16[4,256,512]{2,1,0:T(8,128)(2,1)} %param.21) | copy-start | bytes 3145732
  19.8 3.7 %collective-permute-start = (bf16[8,16,2048]{2,1,0:T(8,128)(2,1)S(1)}, bf16[8,16,2048]{2,1,0:T(8,128)(2,1)S(1)}, u32[]{:S(2)}, u32[]{:S(2)}) collective-permute-start(bf16[8,16,2048]{2,1,0:T(8,128)(2,1)S(1)} %all_to_all.10), channel_id=1, source_target_pairs={{0,1},{1,0},{2,3},{3,2},{4,5},{5,4},{6,7},{7,6},{8,9},{9,8},{10,11... | collective-permute-start | bytes 1572872 | tf_op jit(solution)/shard_map/ppermute | solution.py:188
  24.2 12.0 %copy-start.2 = (f32[16,8]{0,1:T(8,128)S(1)}, f32[16,8]{0,1:T(8,128)}, u32[]{:S(2)}) copy-start(f32[16,8]{0,1:T(8,128)} %param.16) | copy-start | bytes 1540
  24.2 12.1 %copy-start.3 = (s32[16,8]{0,1:T(8,128)S(1)}, s32[16,8]{0,1:T(8,128)}, u32[]{:S(2)}) copy-start(s32[16,8]{0,1:T(8,128)} %param.15) | copy-start | bytes 1540
  24.2 12.4 %copy-start.4 = (bf16[4,512]{1,0:T(4,128)(2,1)S(1)}, bf16[4,512]{1,0:T(4,128)(2,1)}, u32[]{:S(2)}) copy-start(bf16[4,512]{1,0:T(4,128)(2,1)} %param.23) | copy-start | bytes 12292
  24.3 12.4 %copy-start.5 = (bf16[4,512]{1,0:T(4,128)(2,1)S(1)}, bf16[4,512]{1,0:T(4,128)(2,1)}, u32[]{:S(2)}) copy-start(bf16[4,512]{1,0:T(4,128)(2,1)} %param.24) | copy-start | bytes 12292
  24.3 12.4 %copy-start.7 = (s32[4]{0:T(128)S(1)}, s32[4]{0:T(128)}, u32[]{:S(2)}) copy-start(s32[4]{0:T(128)} %param.25) | copy-start | bytes 52
  24.3 12.5 %copy-start.1 = (bf16[4,4096]{1,0:T(4,128)(2,1)S(1)}, bf16[4,4096]{1,0:T(4,128)(2,1)}, u32[]{:S(2)}) copy-start(bf16[4,4096]{1,0:T(4,128)(2,1)} %param.20) | copy-start | bytes 98308
  31.6 6.0 %copy-start.6 = (bf16[4,256,512]{2,1,0:T(8,128)(2,1)S(1)}, bf16[4,256,512]{2,1,0:T(8,128)(2,1)}, u32[]{:S(2)}) copy-start(bf16[4,256,512]{2,1,0:T(8,128)(2,1)} %param.22) | copy-start | bytes 3145732
  31.6 29.5 %all-to-all-start.1 = ((bf16[16,1,16,2048]{3,2,1,0:T(8,128)(2,1)}), bf16[16,1,16,2048]{3,2,1,0:T(8,128)(2,1)S(1)}, u32[]{:S(2)}, u32[]{:S(2)}) async-start(bf16[16,1,16,2048]{3,2,1,0:T(8,128)(2,1)} %bitcast.5), calls=%async_computation.1 | async-start | bytes 2097152 | tf_op jit(solution)/shard_map/all_to_all | solution.py:202

commit v13 on v12

--- a/solution.py
+++ b/solution.py
@@ -95,7 +95,7 @@
         stages.append(
             (pltpu.make_async_copy(down_hbm.at[expert, :, window], down_buf.at[j], sems.at[2, j]),)
         )
-    for stage in stages[:2]:
+    for stage in stages:
         for copy in stage:
             copy.start()
     gain_copy.wait()
@@ -108,9 +108,6 @@
     for index, stage in enumerate(stages):
         for copy in stage:
             copy.wait()
-        if index + 2 < len(stages):
-            for copy in stages[index + 2]:
-                copy.start()
         if index < chunks:
             gate_block = gate_buf[index]
             up_block = up_buf[index]

time: 62.4 us -> 61.5 us (0.986)
  Pallas kernels: 7.26 us -> 6.48 us
    pallas_call x1, Pallas kernels: 7.26 us -> 6.48 us  [expert_mlp(): pl.pallas_call(mlp_kernel, grid_spec=grid_spec, out_shape=jax.ShapeDtypeS...]
where the time goes in v13:
time: 61.5 us; the launch traced here: 61.2 us
  waiting for transfers between devices  24.1 us (39%)
  blocking collectives  18.2 us (30%)
  starting transfers between devices  6.83 us (11%)
  Pallas kernels  6.48 us (11%)
  local copies, waits for them, and re-layouts  2.6 us (4%)
  other arithmetic  1.33 us (2%)
  matrix products  0.91 us (1%)
  between operations  0.76 us (1%)
    all_to_all x1, waiting for transfers between devices, spread_block(): returned = lax.all_to_all(produced, NODE, 0, 0, tiled=True)  22.5 us
    all_to_all x1, blocking collectives, spread_block(): same_core = lax.all_to_all(spread, 'chip', 0, 0, tiled=True)  18.2 us
    pallas_call x1, Pallas kernels, expert_mlp(): pl.pallas_call(mlp_kernel, grid_spec=grid_spec, out_shape=jax.ShapeDtypeS...  6.48 us
    all_to_all x1, starting transfers between devices, spread_block(): returned = lax.all_to_all(produced, NODE, 0, 0, tiled=True)  4.67 us
    ppermute x1, starting transfers between devices, spread_block(): lax.ppermute(same_core, 'core', [(i, (i + 1) % cores) for i in range(core...  2.16 us
    ppermute x1, waiting for transfers between devices, spread_block(): lax.ppermute(same_core, 'core', [(i, (i + 1) % cores) for i in range(core...  1.54 us
  transfers between devices with their start and end apart: 2, of which 2 were waited for; matrix products, arithmetic and copies ran while one was open for 4% of the time, Pallas kernels for 0%

profile of v13, /device:TPU:11, one launch (start us, length us, event | category | flops | bytes accessed | tf_op | source)
XLA Modules:
  0.0 61.2 jit_solution(12816772003274695614)
XLA Ops:
  0.6 0.0 copy-start
  0.6 1.0 %broadcast_in_dim.56 = bf16[8,16,2048]{2,1,0:T(8,128)(2,1)S(1)} broadcast(bf16[16,2048]{1,0:T(8,128)(2,1)} %param.13), dimensions={1,2} | broadcast | bytes 589824 | tf_op jit(solution)/shard_map/broadcast_in_dim | solution.py:183
  1.6 18.2 %all_to_all.10 = bf16[8,16,2048]{2,1,0:T(8,128)(2,1)S(1)} all-to-all(bf16[8,16,2048]{2,1,0:T(8,128)(2,1)S(1)} %broadcast_in_dim.56), channel_id=1, replica_groups=mesh['group'=2,'chip'=8,'core'=2] {'chip'}, dimensions={0} | all-to-all | bytes 1048576 | tf_op jit(solution)/shard_map/all_to_all | solution.py:184
  19.8 2.2 %collective-permute-start = (bf16[8,16,2048]{2,1,0:T(8,128)(2,1)S(1)}, bf16[8,16,2048]{2,1,0:T(8,128)(2,1)S(1)}, u32[]{:S(2)}, u32[]{:S(2)}) collective-permute-start(bf16[8,16,2048]{2,1,0:T(8,128)(2,1)S(1)} %all_to_all.10), channel_id=1, source_target_pairs={{0,1},{1,0},{2,3},{3,2},{4,5},{5,4},{6,7},{7,6},{8,9},{9,8},{10,11... | collective-permute-start | bytes 1572872 | tf_op jit(solution)/shard_map/ppermute | solution.py:185
  22.0 1.5 %collective-permute-done = bf16[8,16,2048]{2,1,0:T(8,128)(2,1)S(1)} collective-permute-done((bf16[8,16,2048]{2,1,0:T(8,128)(2,1)S(1)}, bf16[8,16,2048]{2,1,0:T(8,128)(2,1)S(1)}, u32[]{:S(2)}, u32[]{:S(2)}) %collective-permute-start) | collective-permute-done | bytes 524320 | tf_op jit(solution)/shard_map/ppermute | solution.py:185
  23.5 0.7 %broadcast_in_dim.55.gain_ref = f32[8,2048]{1,0:T(8,128)S(1)} broadcast(f32[2048]{0:T(1024)} %param.14), dimensions={1} | broadcast | bytes 73728 | tf_op jit(solution)/shard_map/broadcast_in_dim | solution.py:186
  24.2 0.0 copy-start.2
  24.2 0.0 copy-start.3
  24.2 0.0 copy-start.4
  24.3 0.0 copy-start.5
  24.3 0.0 copy-start.7
  24.3 0.0 copy-start.1
  24.3 6.5 %shard_map.140 = bf16[1,8,2,16,2048]{4,3,2,1,0:T(8,128)(2,1)} custom-call(s32[1]{0:T(128)} %bitcast.1.core_ref, f32[8,2048]{1,0:T(8,128)S(1)} %broadcast_in_dim.55.gain_ref, bf16[128,2048]{1,0:T(8,128)(2,1)S(1)} %bitcast.44, bf16[128,2048]{1,0:T(8,128)(2,1)S(1)} %bitcast.45, bf16[1,2048,768]{2,1,0:T(8,128)(2,1)} %gate_hbm.1, bf16[1,2048,768]{2,1,0:T(8,128)(2,1)} %up_hbm.1, ...), custom_call_target="tpu_custom_call" | custom-call | tf_op jit(solution)/shard_map/pallas_call | solution.py:163
  30.8 0.0 copy-start.6
  30.8 4.7 %all-to-all-start.1 = ((bf16[16,1,16,2048]{3,2,1,0:T(8,128)(2,1)}), bf16[16,1,16,2048]{3,2,1,0:T(8,128)(2,1)S(1)}, u32[]{:S(2)}, u32[]{:S(2)}) async-start(bf16[16,1,16,2048]{3,2,1,0:T(8,128)(2,1)} %bitcast.5), calls=%async_computation.1 | async-start | bytes 2097152 | tf_op jit(solution)/shard_map/all_to_all | solution.py:199
  35.5 0.0 copy-done.2
  35.5 0.1 copy.25
  35.6 0.0 copy-done.3
  35.6 0.1 copy.24
  35.6 0.1 select_reduce_fusion
  35.8 0.1 copy.26
  35.8 0.0 copy-done.4
  35.9 0.0 copy-done.5
  35.9 0.0 copy-done.7
  35.9 0.1 iota_compare_fusion.1
  36.0 0.0 copy-done.1
  36.0 0.1 fusion.13
  36.1 0.0 copy-done
  36.1 0.5 fusion.21
  36.6 0.2 fusion.8
  36.8 0.0 copy-done.6
  36.8 0.3 fusion.3
  37.1 0.6 %copy.57 = bf16[1,4,32,128]{3,1,2,0:T(4,128)(2,1)} copy(bf16[1,4,32,128]{3,2,1,0:T(8,128)(2,1)S(1)} %fusion.3) | data formatting | bytes 65536
  37.8 22.5 %all-to-all-done.1 = bf16[16,1,16,2048]{3,2,1,0:T(8,128)(2,1)S(1)} async-done(((bf16[16,1,16,2048]{3,2,1,0:T(8,128)(2,1)}), bf16[16,1,16,2048]{3,2,1,0:T(8,128)(2,1)S(1)}, u32[]{:S(2)}, u32[]{:S(2)}) %all-to-all-start.1) | async-done | bytes 1048608 | tf_op jit(solution)/shard_map/all_to_all | solution.py:199
  60.3 0.9 %fusion = bf16[16,2048]{1,0:T(8,128)(2,1)} fusion(bf16[16,1,16,2048]{3,2,1,0:T(8,128)(2,1)S(1)} %all-to-all-done.1, f32[16,16]{1,0:T(8,128)S(1)} %copy.26), kind=kLoop, calls=%fused_computation.1 | loop fusion | flops 1540096 | bytes 1115136 | tf_op jit(solution)/shard_map/reduce_sum | solution.py:206
  (6 shorter events, 0.1 us)
Async XLA Ops:
  0.6 35.5 %copy-start = (bf16[4,256,512]{2,1,0:T(8,128)(2,1)S(1)}, bf16[4,256,512]{2,1,0:T(8,128)(2,1)}, u32[]{:S(2)}) copy-start(bf16[4,256,512]{2,1,0:T(8,128)(2,1)} %param.21) | copy-start | bytes 3145732
  19.8 3.7 %collective-permute-start = (bf16[8,16,2048]{2,1,0:T(8,128)(2,1)S(1)}, bf16[8,16,2048]{2,1,0:T(8,128)(2,1)S(1)}, u32[]{:S(2)}, u32[]{:S(2)}) collective-permute-start(bf16[8,16,2048]{2,1,0:T(8,128)(2,1)S(1)} %all_to_all.10), channel_id=1, source_target_pairs={{0,1},{1,0},{2,3},{3,2},{4,5},{5,4},{6,7},{7,6},{8,9},{9,8},{10,11... | collective-permute-start | bytes 1572872 | tf_op jit(solution)/shard_map/ppermute | solution.py:185
  24.2 11.2 %copy-start.2 = (f32[16,8]{0,1:T(8,128)S(1)}, f32[16,8]{0,1:T(8,128)}, u32[]{:S(2)}) copy-start(f32[16,8]{0,1:T(8,128)} %param.16) | copy-start | bytes 1540
  24.2 11.3 %copy-start.3 = (s32[16,8]{0,1:T(8,128)S(1)}, s32[16,8]{0,1:T(8,128)}, u32[]{:S(2)}) copy-start(s32[16,8]{0,1:T(8,128)} %param.15) | copy-start | bytes 1540
  24.2 11.6 %copy-start.4 = (bf16[4,512]{1,0:T(4,128)(2,1)S(1)}, bf16[4,512]{1,0:T(4,128)(2,1)}, u32[]{:S(2)}) copy-start(bf16[4,512]{1,0:T(4,128)(2,1)} %param.23) | copy-start | bytes 12292
  24.3 11.6 %copy-start.5 = (bf16[4,512]{1,0:T(4,128)(2,1)S(1)}, bf16[4,512]{1,0:T(4,128)(2,1)}, u32[]{:S(2)}) copy-start(bf16[4,512]{1,0:T(4,128)(2,1)} %param.24) | copy-start | bytes 12292
  24.3 11.6 %copy-start.7 = (s32[4]{0:T(128)S(1)}, s32[4]{0:T(128)}, u32[]{:S(2)}) copy-start(s32[4]{0:T(128)} %param.25) | copy-start | bytes 52
  24.3 11.7 %copy-start.1 = (bf16[4,4096]{1,0:T(4,128)(2,1)S(1)}, bf16[4,4096]{1,0:T(4,128)(2,1)}, u32[]{:S(2)}) copy-start(bf16[4,4096]{1,0:T(4,128)(2,1)} %param.20) | copy-start | bytes 98308
  30.8 6.0 %copy-start.6 = (bf16[4,256,512]{2,1,0:T(8,128)(2,1)S(1)}, bf16[4,256,512]{2,1,0:T(8,128)(2,1)}, u32[]{:S(2)}) copy-start(bf16[4,256,512]{2,1,0:T(8,128)(2,1)} %param.22) | copy-start | bytes 3145732
  30.8 29.5 %all-to-all-start.1 = ((bf16[16,1,16,2048]{3,2,1,0:T(8,128)(2,1)}), bf16[16,1,16,2048]{3,2,1,0:T(8,128)(2,1)S(1)}, u32[]{:S(2)}, u32[]{:S(2)}) async-start(bf16[16,1,16,2048]{3,2,1,0:T(8,128)(2,1)} %bitcast.5), calls=%async_computation.1 | async-start | bytes 2097152 | tf_op jit(solution)/shard_map/all_to_all | solution.py:199

commit v14 on v11

--- a/solution.py
+++ b/solution.py
@@ -187,8 +187,11 @@
         w_down,
         chips,
     )
-    produced = produced.reshape(local_experts, peers, rows_here, features)
-    produced = produced.transpose(1, 0, 2, 3)
+    if local_experts == 1:
+        produced = produced.reshape(peers, rows_here, features)
+    else:
+        produced = produced.reshape(local_experts, peers, rows_here, features)
+        produced = produced.transpose(1, 0, 2, 3)
     returned = lax.all_to_all(produced, NODE, 0, 0, tiled=True)
     returned = returned.reshape(experts_all, rows_here, features)
     shares = gate_weights / jnp.sum(gate_weights, axis=1, keepdims=True)

time: 61.1 us -> 61.1 us (level)
  no operation moved by 1% of the time
where the time goes in v14:
time: 61.1 us; the launch traced here: 60.8 us
  waiting for transfers between devices  24.1 us (39%)
  blocking collectives  18.2 us (30%)
  starting transfers between devices  6.84 us (11%)
  Pallas kernels  6.05 us (10%)
  local copies, waits for them, and re-layouts  2.6 us (4%)
  other arithmetic  1.33 us (2%)
  matrix products  0.91 us (1%)
  between operations  0.76 us (1%)
    all_to_all x1, waiting for transfers between devices, spread_block(): returned = lax.all_to_all(produced, NODE, 0, 0, tiled=True)  22.5 us
    all_to_all x1, blocking collectives, spread_block(): same_core = lax.all_to_all(spread, 'chip', 0, 0, tiled=True)  18.2 us
    pallas_call x1, Pallas kernels, expert_mlp(): pl.pallas_call(mlp_kernel, grid_spec=grid_spec, out_shape=jax.ShapeDtypeS...  6.05 us
    all_to_all x1, starting transfers between devices, spread_block(): returned = lax.all_to_all(produced, NODE, 0, 0, tiled=True)  4.68 us
    ppermute x1, starting transfers between devices, spread_block(): lax.ppermute(same_core, 'core', [(i, (i + 1) % cores) for i in range(core...  2.16 us
    ppermute x1, waiting for transfers between devices, spread_block(): lax.ppermute(same_core, 'core', [(i, (i + 1) % cores) for i in range(core...  1.54 us
  transfers between devices with their start and end apart: 2, of which 2 were waited for; matrix products, arithmetic and copies ran while one was open for 4% of the time, Pallas kernels for 0%

profile of v14, /device:TPU:11, one launch (start us, length us, event | category | flops | bytes accessed | tf_op | source)
XLA Modules:
  0.0 60.8 jit_solution(13468771640753157201)
XLA Ops:
  0.6 0.0 copy-start
  0.6 1.0 %broadcast_in_dim.56 = bf16[8,16,2048]{2,1,0:T(8,128)(2,1)S(1)} broadcast(bf16[16,2048]{1,0:T(8,128)(2,1)} %param.13), dimensions={1,2} | broadcast | bytes 589824 | tf_op jit(solution)/shard_map/broadcast_in_dim | solution.py:176
  1.6 18.2 %all_to_all.10 = bf16[8,16,2048]{2,1,0:T(8,128)(2,1)S(1)} all-to-all(bf16[8,16,2048]{2,1,0:T(8,128)(2,1)S(1)} %broadcast_in_dim.56), channel_id=1, replica_groups=mesh['group'=2,'chip'=8,'core'=2] {'chip'}, dimensions={0} | all-to-all | bytes 1048576 | tf_op jit(solution)/shard_map/all_to_all | solution.py:177
  19.8 2.2 %collective-permute-start = (bf16[8,16,2048]{2,1,0:T(8,128)(2,1)S(1)}, bf16[8,16,2048]{2,1,0:T(8,128)(2,1)S(1)}, u32[]{:S(2)}, u32[]{:S(2)}) collective-permute-start(bf16[8,16,2048]{2,1,0:T(8,128)(2,1)S(1)} %all_to_all.10), channel_id=1, source_target_pairs={{0,1},{1,0},{2,3},{3,2},{4,5},{5,4},{6,7},{7,6},{8,9},{9,8},{10,11... | collective-permute-start | bytes 1572872 | tf_op jit(solution)/shard_map/ppermute | solution.py:178
  22.0 1.5 %collective-permute-done = bf16[8,16,2048]{2,1,0:T(8,128)(2,1)S(1)} collective-permute-done((bf16[8,16,2048]{2,1,0:T(8,128)(2,1)S(1)}, bf16[8,16,2048]{2,1,0:T(8,128)(2,1)S(1)}, u32[]{:S(2)}, u32[]{:S(2)}) %collective-permute-start) | collective-permute-done | bytes 524320 | tf_op jit(solution)/shard_map/ppermute | solution.py:178
  23.5 0.7 %broadcast_in_dim.55.gain_ref = f32[8,2048]{1,0:T(8,128)S(1)} broadcast(f32[2048]{0:T(1024)} %param.14), dimensions={1} | broadcast | bytes 73728 | tf_op jit(solution)/shard_map/broadcast_in_dim | solution.py:179
  24.2 0.0 copy-start.2
  24.2 0.0 copy-start.3
  24.2 0.0 copy-start.4
  24.3 0.0 copy-start.5
  24.3 0.0 copy-start.7
  24.3 0.0 copy-start.1
  24.3 6.0 %shard_map.140 = bf16[1,8,2,16,2048]{4,3,2,1,0:T(8,128)(2,1)} custom-call(s32[1]{0:T(128)} %bitcast.1.core_ref, f32[8,2048]{1,0:T(8,128)S(1)} %broadcast_in_dim.55.gain_ref, bf16[128,2048]{1,0:T(8,128)(2,1)S(1)} %bitcast.39, bf16[128,2048]{1,0:T(8,128)(2,1)S(1)} %bitcast.40, bf16[1,2048,768]{2,1,0:T(8,128)(2,1)} %gate_hbm.1, bf16[1,2048,768]{2,1,0:T(8,128)(2,1)} %up_hbm.1, ...), custom_call_target="tpu_custom_call" | custom-call | tf_op jit(solution)/shard_map/pallas_call | solution.py:156
  30.3 0.0 copy-start.6
  30.4 4.7 %all-to-all-start.1 = ((bf16[16,16,2048]{2,1,0:T(8,128)(2,1)}), bf16[16,16,2048]{2,1,0:T(8,128)(2,1)S(1)}, u32[]{:S(2)}, u32[]{:S(2)}) async-start(bf16[16,16,2048]{2,1,0:T(8,128)(2,1)} %bitcast.4), calls=%async_computation.1 | async-start | bytes 2097152 | tf_op jit(solution)/shard_map/all_to_all | solution.py:195
  35.0 0.0 copy-done.2
  35.1 0.1 copy.20
  35.1 0.0 copy-done.3
  35.1 0.1 copy.19
  35.2 0.1 select_reduce_fusion
  35.3 0.1 copy.21
  35.4 0.0 copy-done.4
  35.4 0.0 copy-done.5
  35.4 0.0 copy-done.7
  35.5 0.1 iota_compare_fusion.1
  35.5 0.0 copy-done.1
  35.5 0.1 fusion.12
  35.7 0.0 copy-done
  35.7 0.5 fusion.20
  36.1 0.2 fusion.7
  36.4 0.0 copy-done.6
  36.4 0.3 fusion.2
  36.7 0.6 %copy.51 = bf16[1,4,32,128]{3,1,2,0:T(4,128)(2,1)} copy(bf16[1,4,32,128]{3,2,1,0:T(8,128)(2,1)S(1)} %fusion.2) | data formatting | bytes 65536
  37.3 22.5 %all-to-all-done.1 = bf16[16,16,2048]{2,1,0:T(8,128)(2,1)S(1)} async-done(((bf16[16,16,2048]{2,1,0:T(8,128)(2,1)}), bf16[16,16,2048]{2,1,0:T(8,128)(2,1)S(1)}, u32[]{:S(2)}, u32[]{:S(2)}) %all-to-all-start.1) | async-done | bytes 1048608 | tf_op jit(solution)/shard_map/all_to_all | solution.py:195
  59.9 0.9 %multiply_reduce_fusion = bf16[16,2048]{1,0:T(8,128)(2,1)} fusion(bf16[16,16,2048]{2,1,0:T(8,128)(2,1)S(1)} %all-to-all-done.1, f32[16,16]{1,0:T(8,128)S(1)} %copy.21), kind=kLoop, calls=%fused_computation | loop fusion | flops 1540096 | bytes 1115136 | tf_op jit(solution)/shard_map/reduce_sum | solution.py:202
  (6 shorter events, 0.1 us)
Async XLA Ops:
  0.6 35.0 %copy-start = (bf16[4,256,512]{2,1,0:T(8,128)(2,1)S(1)}, bf16[4,256,512]{2,1,0:T(8,128)(2,1)}, u32[]{:S(2)}) copy-start(bf16[4,256,512]{2,1,0:T(8,128)(2,1)} %param.21) | copy-start | bytes 3145732
  19.8 3.7 %collective-permute-start = (bf16[8,16,2048]{2,1,0:T(8,128)(2,1)S(1)}, bf16[8,16,2048]{2,1,0:T(8,128)(2,1)S(1)}, u32[]{:S(2)}, u32[]{:S(2)}) collective-permute-start(bf16[8,16,2048]{2,1,0:T(8,128)(2,1)S(1)} %all_to_all.10), channel_id=1, source_target_pairs={{0,1},{1,0},{2,3},{3,2},{4,5},{5,4},{6,7},{7,6},{8,9},{9,8},{10,11... | collective-permute-start | bytes 1572872 | tf_op jit(solution)/shard_map/ppermute | solution.py:178
  24.2 10.8 %copy-start.2 = (f32[16,8]{0,1:T(8,128)S(1)}, f32[16,8]{0,1:T(8,128)}, u32[]{:S(2)}) copy-start(f32[16,8]{0,1:T(8,128)} %param.16) | copy-start | bytes 1540
  24.2 10.9 %copy-start.3 = (s32[16,8]{0,1:T(8,128)S(1)}, s32[16,8]{0,1:T(8,128)}, u32[]{:S(2)}) copy-start(s32[16,8]{0,1:T(8,128)} %param.15) | copy-start | bytes 1540
  24.2 11.2 %copy-start.4 = (bf16[4,512]{1,0:T(4,128)(2,1)S(1)}, bf16[4,512]{1,0:T(4,128)(2,1)}, u32[]{:S(2)}) copy-start(bf16[4,512]{1,0:T(4,128)(2,1)} %param.23) | copy-start | bytes 12292
  24.3 11.2 %copy-start.5 = (bf16[4,512]{1,0:T(4,128)(2,1)S(1)}, bf16[4,512]{1,0:T(4,128)(2,1)}, u32[]{:S(2)}) copy-start(bf16[4,512]{1,0:T(4,128)(2,1)} %param.24) | copy-start | bytes 12292
  24.3 11.2 %copy-start.7 = (s32[4]{0:T(128)S(1)}, s32[4]{0:T(128)}, u32[]{:S(2)}) copy-start(s32[4]{0:T(128)} %param.25) | copy-start | bytes 52
  24.3 11.3 %copy-start.1 = (bf16[4,4096]{1,0:T(4,128)(2,1)S(1)}, bf16[4,4096]{1,0:T(4,128)(2,1)}, u32[]{:S(2)}) copy-start(bf16[4,4096]{1,0:T(4,128)(2,1)} %param.20) | copy-start | bytes 98308
  30.3 6.0 %copy-start.6 = (bf16[4,256,512]{2,1,0:T(8,128)(2,1)S(1)}, bf16[4,256,512]{2,1,0:T(8,128)(2,1)}, u32[]{:S(2)}) copy-start(bf16[4,256,512]{2,1,0:T(8,128)(2,1)} %param.22) | copy-start | bytes 3145732
  30.4 29.5 %all-to-all-start.1 = ((bf16[16,16,2048]{2,1,0:T(8,128)(2,1)}), bf16[16,16,2048]{2,1,0:T(8,128)(2,1)S(1)}, u32[]{:S(2)}, u32[]{:S(2)}) async-start(bf16[16,16,2048]{2,1,0:T(8,128)(2,1)} %bitcast.4), calls=%async_computation.1 | async-start | bytes 2097152 | tf_op jit(solution)/shard_map/all_to_all | solution.py:195

commit v15 on v14

--- a/solution.py
+++ b/solution.py
@@ -130,18 +130,17 @@
     chunk = 256 if hidden % 256 == 0 else hidden
     chunks = hidden // chunk
     grid_spec = pltpu.PrefetchScalarGridSpec(
-        num_scalar_prefetch=1,
+        num_scalar_prefetch=2,
         grid=(local_experts,),
         in_specs=[
-            pl.BlockSpec(memory_space=pltpu.HBM),
-            pl.BlockSpec((half, features), lambda e, c: (0, 0)),
-            pl.BlockSpec((half, features), lambda e, c: (0, 0)),
+            pl.BlockSpec((half, features), lambda e, c, g: (0, 0)),
+            pl.BlockSpec((half, features), lambda e, c, g: (0, 0)),
             pl.BlockSpec(memory_space=pltpu.HBM),
             pl.BlockSpec(memory_space=pltpu.HBM),
             pl.BlockSpec(memory_space=pltpu.HBM),
         ],
         out_specs=pl.BlockSpec(
-            (None, chips, 2, rows_here, features), lambda e, c: (e, 0, 0, 0, 0)
+            (None, chips, 2, rows_here, features), lambda e, c, g: (e, 0, 0, 0, 0)
         ),
         scratch_shapes=[
             pltpu.VMEM((chunks, features, chunk), jnp.bfloat16),
@@ -149,7 +148,7 @@
             pltpu.VMEM((hidden, features), jnp.bfloat16),
             pltpu.VMEM((2, half, hidden), jnp.bfloat16),
             pltpu.VMEM((2, half, features), jnp.bfloat16),
-            pltpu.VMEM((8, features), jnp.float32),
+            pltpu.VMEM((1, features), jnp.float32),
             pltpu.SemaphoreType.DMA((3, max(chunks, 2))),
         ],
     )
@@ -176,7 +175,7 @@
     spread = jnp.broadcast_to(states[None], (chips, rows_here, features))
     same_core = lax.all_to_all(spread, "chip", 0, 0, tiled=True)
     other_core = lax.ppermute(same_core, "core", [(i, (i + 1) % cores) for i in range(cores)])
-    gain_rows = jnp.broadcast_to(norm_gain[None, :], (8, features))
+    gain_rows = norm_gain.reshape(1, features)
     produced = expert_mlp(
         core.astype(jnp.int32),
         gain_rows,

time: 61.1 us -> 61.6 us (level)
    broadcast_in_dim x1 -> x0, local copies, waits for them, and re-layouts: 0.7 us -> none  [spread_block(): gain_rows = jnp.broadcast_to(norm_gain[None, :], (8, features))]
    unnamed x18 -> x20, local copies, waits for them, and re-layouts: 0.77 us -> 1.46 us
where the time goes in v15:
time: 61.6 us; the launch traced here: 61.3 us
  waiting for transfers between devices  24.1 us (39%)
  blocking collectives  18.2 us (30%)
  starting transfers between devices  6.84 us (11%)
  Pallas kernels  6.62 us (11%)
  local copies, waits for them, and re-layouts  2.59 us (4%)
  other arithmetic  1.33 us (2%)
  matrix products  0.91 us (1%)
  between operations  0.74 us (1%)
    all_to_all x1, waiting for transfers between devices, spread_block(): returned = lax.all_to_all(produced, NODE, 0, 0, tiled=True)  22.5 us
    all_to_all x1, blocking collectives, spread_block(): same_core = lax.all_to_all(spread, 'chip', 0, 0, tiled=True)  18.2 us
    pallas_call x1, Pallas kernels, expert_mlp(): pl.pallas_call(mlp_kernel, grid_spec=grid_spec, out_shape=jax.ShapeDtypeS...  6.62 us
    all_to_all x1, starting transfers between devices, spread_block(): returned = lax.all_to_all(produced, NODE, 0, 0, tiled=True)  4.68 us
    ppermute x1, starting transfers between devices, spread_block(): lax.ppermute(same_core, 'core', [(i, (i + 1) % cores) for i in range(core...  2.16 us
    ppermute x1, waiting for transfers between devices, spread_block(): lax.ppermute(same_core, 'core', [(i, (i + 1) % cores) for i in range(core...  1.54 us
    unnamed x20, local copies, waits for them, and re-layouts  1.46 us
  transfers between devices with their start and end apart: 2, of which 2 were waited for; matrix products, arithmetic and copies ran while one was open for 4% of the time, Pallas kernels for 0%

profile of v15, /device:TPU:11, one launch (start us, length us, event | category | flops | bytes accessed | tf_op | source)
XLA Modules:
  0.0 61.3 jit_solution(4183917902715374428)
XLA Ops:
  0.6 0.0 copy-start
  0.6 1.0 %broadcast_in_dim.49 = bf16[8,16,2048]{2,1,0:T(8,128)(2,1)S(1)} broadcast(bf16[16,2048]{1,0:T(8,128)(2,1)} %param.13), dimensions={1,2} | broadcast | bytes 589824 | tf_op jit(solution)/shard_map/broadcast_in_dim | solution.py:175
  1.6 18.2 %all_to_all.10 = bf16[8,16,2048]{2,1,0:T(8,128)(2,1)S(1)} all-to-all(bf16[8,16,2048]{2,1,0:T(8,128)(2,1)S(1)} %broadcast_in_dim.49), channel_id=1, replica_groups=mesh['group'=2,'chip'=8,'core'=2] {'chip'}, dimensions={0} | all-to-all | bytes 1048576 | tf_op jit(solution)/shard_map/all_to_all | solution.py:176
  19.8 2.2 %collective-permute-start = (bf16[8,16,2048]{2,1,0:T(8,128)(2,1)S(1)}, bf16[8,16,2048]{2,1,0:T(8,128)(2,1)S(1)}, u32[]{:S(2)}, u32[]{:S(2)}) collective-permute-start(bf16[8,16,2048]{2,1,0:T(8,128)(2,1)S(1)} %all_to_all.10), channel_id=1, source_target_pairs={{0,1},{1,0},{2,3},{3,2},{4,5},{5,4},{6,7},{7,6},{8,9},{9,8},{10,11... | collective-permute-start | bytes 1572872 | tf_op jit(solution)/shard_map/ppermute | solution.py:177
  22.0 1.5 %collective-permute-done = bf16[8,16,2048]{2,1,0:T(8,128)(2,1)S(1)} collective-permute-done((bf16[8,16,2048]{2,1,0:T(8,128)(2,1)S(1)}, bf16[8,16,2048]{2,1,0:T(8,128)(2,1)S(1)}, u32[]{:S(2)}, u32[]{:S(2)}) %collective-permute-start) | collective-permute-done | bytes 524320 | tf_op jit(solution)/shard_map/ppermute | solution.py:177
  23.5 0.0 copy-start.1
  23.5 0.7 %copy-done.1 = f32[2048]{0:T(1024)S(1)} copy-done((f32[2048]{0:T(1024)S(1)}, f32[2048]{0:T(1024)}, u32[]{:S(2)}) %copy-start.1) | copy-done | bytes 8216
  24.2 0.0 copy-start.3
  24.2 0.0 copy-start.4
  24.2 0.0 copy-start.5
  24.2 0.0 copy-start.6
  24.2 0.0 copy-start.8
  24.3 0.0 copy-start.2
  24.3 6.6 %shard_map.140 = bf16[1,8,2,16,2048]{4,3,2,1,0:T(8,128)(2,1)} custom-call(s32[1]{0:T(128)} %bitcast.1.core_ref, f32[1,2048]{1,0:T(1,128)S(1)} %bitcast.42, bf16[128,2048]{1,0:T(8,128)(2,1)S(1)} %bitcast.40, bf16[128,2048]{1,0:T(8,128)(2,1)S(1)} %bitcast.41, bf16[1,2048,768]{2,1,0:T(8,128)(2,1)} %gate_hbm.1, bf16[1,2048,768]{2,1,0:T(8,128)(2,1)} %up_hbm.1, ...), custom_call_target="tpu_custom_call" | custom-call | tf_op jit(solution)/shard_map/pallas_call | solution.py:155
  30.9 0.0 copy-start.7
  30.9 4.7 %all-to-all-start.1 = ((bf16[16,16,2048]{2,1,0:T(8,128)(2,1)}), bf16[16,16,2048]{2,1,0:T(8,128)(2,1)S(1)}, u32[]{:S(2)}, u32[]{:S(2)}) async-start(bf16[16,16,2048]{2,1,0:T(8,128)(2,1)} %bitcast.5), calls=%async_computation.1 | async-start | bytes 2097152 | tf_op jit(solution)/shard_map/all_to_all | solution.py:194
  35.6 0.0 copy-done.3
  35.6 0.1 copy.20
  35.7 0.0 copy-done.4
  35.7 0.1 copy.19
  35.8 0.1 select_reduce_fusion
  35.9 0.1 copy.21
  36.0 0.0 copy-done.5
  36.0 0.0 copy-done.6
  36.0 0.0 copy-done.8
  36.0 0.1 iota_compare_fusion.1
  36.1 0.0 copy-done.2
  36.1 0.1 fusion.12
  36.2 0.0 copy-done
  36.2 0.5 fusion.20
  36.7 0.2 fusion.7
  36.9 0.0 copy-done.7
  36.9 0.3 fusion.2
  37.2 0.6 %copy.51 = bf16[1,4,32,128]{3,1,2,0:T(4,128)(2,1)} copy(bf16[1,4,32,128]{3,2,1,0:T(8,128)(2,1)S(1)} %fusion.2) | data formatting | bytes 65536
  37.9 22.5 %all-to-all-done.1 = bf16[16,16,2048]{2,1,0:T(8,128)(2,1)S(1)} async-done(((bf16[16,16,2048]{2,1,0:T(8,128)(2,1)}), bf16[16,16,2048]{2,1,0:T(8,128)(2,1)S(1)}, u32[]{:S(2)}, u32[]{:S(2)}) %all-to-all-start.1) | async-done | bytes 1048608 | tf_op jit(solution)/shard_map/all_to_all | solution.py:194
  60.4 0.9 %multiply_reduce_fusion = bf16[16,2048]{1,0:T(8,128)(2,1)} fusion(bf16[16,16,2048]{2,1,0:T(8,128)(2,1)S(1)} %all-to-all-done.1, f32[16,16]{1,0:T(8,128)S(1)} %copy.21), kind=kLoop, calls=%fused_computation | loop fusion | flops 1540096 | bytes 1115136 | tf_op jit(solution)/shard_map/reduce_sum | solution.py:201
  (6 shorter events, 0.1 us)
Async XLA Ops:
  0.6 35.6 %copy-start = (bf16[4,256,512]{2,1,0:T(8,128)(2,1)S(1)}, bf16[4,256,512]{2,1,0:T(8,128)(2,1)}, u32[]{:S(2)}) copy-start(bf16[4,256,512]{2,1,0:T(8,128)(2,1)} %param.21) | copy-start | bytes 3145732
  19.8 3.7 %collective-permute-start = (bf16[8,16,2048]{2,1,0:T(8,128)(2,1)S(1)}, bf16[8,16,2048]{2,1,0:T(8,128)(2,1)S(1)}, u32[]{:S(2)}, u32[]{:S(2)}) collective-permute-start(bf16[8,16,2048]{2,1,0:T(8,128)(2,1)S(1)} %all_to_all.10), channel_id=1, source_target_pairs={{0,1},{1,0},{2,3},{3,2},{4,5},{5,4},{6,7},{7,6},{8,9},{9,8},{10,11... | collective-permute-start | bytes 1572872 | tf_op jit(solution)/shard_map/ppermute | solution.py:177
  23.5 0.7 %copy-start.1 = (f32[2048]{0:T(1024)S(1)}, f32[2048]{0:T(1024)}, u32[]{:S(2)}) copy-start(f32[2048]{0:T(1024)} %param.14) | copy-start | bytes 24580
  24.2 11.4 %copy-start.3 = (f32[16,8]{0,1:T(8,128)S(1)}, f32[16,8]{0,1:T(8,128)}, u32[]{:S(2)}) copy-start(f32[16,8]{0,1:T(8,128)} %param.16) | copy-start | bytes 1540
  24.2 11.5 %copy-start.4 = (s32[16,8]{0,1:T(8,128)S(1)}, s32[16,8]{0,1:T(8,128)}, u32[]{:S(2)}) copy-start(s32[16,8]{0,1:T(8,128)} %param.15) | copy-start | bytes 1540
  24.2 11.7 %copy-start.5 = (bf16[4,512]{1,0:T(4,128)(2,1)S(1)}, bf16[4,512]{1,0:T(4,128)(2,1)}, u32[]{:S(2)}) copy-start(bf16[4,512]{1,0:T(4,128)(2,1)} %param.23) | copy-start | bytes 12292
  24.2 11.7 %copy-start.6 = (bf16[4,512]{1,0:T(4,128)(2,1)S(1)}, bf16[4,512]{1,0:T(4,128)(2,1)}, u32[]{:S(2)}) copy-start(bf16[4,512]{1,0:T(4,128)(2,1)} %param.24) | copy-start | bytes 12292
  24.2 11.8 %copy-start.8 = (s32[4]{0:T(128)S(1)}, s32[4]{0:T(128)}, u32[]{:S(2)}) copy-start(s32[4]{0:T(128)} %param.25) | copy-start | bytes 52
  24.3 11.8 %copy-start.2 = (bf16[4,4096]{1,0:T(4,128)(2,1)S(1)}, bf16[4,4096]{1,0:T(4,128)(2,1)}, u32[]{:S(2)}) copy-start(bf16[4,4096]{1,0:T(4,128)(2,1)} %param.20) | copy-start | bytes 98308
  30.9 6.0 %copy-start.7 = (bf16[4,256,512]{2,1,0:T(8,128)(2,1)S(1)}, bf16[4,256,512]{2,1,0:T(8,128)(2,1)}, u32[]{:S(2)}) copy-start(bf16[4,256,512]{2,1,0:T(8,128)(2,1)} %param.22) | copy-start | bytes 3145732
  30.9 29.5 %all-to-all-start.1 = ((bf16[16,16,2048]{2,1,0:T(8,128)(2,1)}), bf16[16,16,2048]{2,1,0:T(8,128)(2,1)S(1)}, u32[]{:S(2)}, u32[]{:S(2)}) async-start(bf16[16,16,2048]{2,1,0:T(8,128)(2,1)} %bitcast.5), calls=%async_computation.1 | async-start | bytes 2097152 | tf_op jit(solution)/shard_map/all_to_all | solution.py:194

commit v16 on v11

--- a/solution.py
+++ b/solution.py
@@ -73,11 +73,11 @@
 
 def mlp_kernel(
     core_ref, gain_ref, same_ref, other_ref, gate_hbm, up_hbm, down_hbm, out_ref,
-    gate_buf, up_buf, down_buf, inner_buf, normed_buf, gain_buf, sems,
+    gate_buf, up_buf, down_buf, inner_buf, normed_buf, gain_buf, out_buf, sems,
 ):
     expert = pl.program_id(0)
     chunks, _, chunk = gate_buf.shape
-    chips = out_ref.shape[0]
+    chips = out_buf.shape[1]
     half = same_ref.shape[0]
     rows_here = half // chips
     gain_copy = pltpu.make_async_copy(gain_ref, gain_buf, sems.at[2, 1])
@@ -115,12 +115,18 @@
     down_copy.wait()
     down_block = down_buf[...]
     core = core_ref[0]
+    stores = []
     for part in range(2):
         produced = jnp.dot(inner_buf[part], down_block, preferred_element_type=jnp.float32)
+        out_buf[part] = produced.reshape(chips, 1, rows_here, -1).astype(out_buf.dtype)
         target = (core + part) % 2
-        out_ref[:, pl.ds(target, 1)] = (
-            produced.reshape(chips, 1, rows_here, -1).astype(out_ref.dtype)
+        store = pltpu.make_async_copy(
+            out_buf.at[part], out_ref.at[expert, :, pl.ds(target, 1)], sems.at[2, 2 + part]
         )
+        store.start()
+        stores.append(store)
+    for store in stores:
+        store.wait()
 
 
 def expert_mlp(core, norm_gain, same_rows, other_rows, w_gate, w_up, w_down, chips):
@@ -140,9 +146,7 @@
             pl.BlockSpec(memory_space=pltpu.HBM),
             pl.BlockSpec(memory_space=pltpu.HBM),
         ],
-        out_specs=pl.BlockSpec(
-            (None, chips, 2, rows_here, features), lambda e, c: (e, 0, 0, 0, 0)
-        ),
+        out_specs=pl.BlockSpec(memory_space=pltpu.HBM),
         scratch_shapes=[
             pltpu.VMEM((chunks, features, chunk), jnp.bfloat16),
             pltpu.VMEM((chunks, features, chunk), jnp.bfloat16),
@@ -150,7 +154,8 @@
             pltpu.VMEM((2, half, hidden), jnp.bfloat16),
             pltpu.VMEM((2, half, features), jnp.bfloat16),
             pltpu.VMEM((8, features), jnp.float32),
-            pltpu.SemaphoreType.DMA((3, max(chunks, 2))),
+            pltpu.VMEM((2, chips, 1, rows_here, features), jnp.bfloat16),
+            pltpu.SemaphoreType.DMA((3, max(chunks, 4))),
         ],
     )
     return pl.pallas_call(

time: 61.1 us -> 60.9 us (level)
  no operation moved by 1% of the time
where the time goes in v16:
time: 60.9 us; the launch traced here: 60.6 us
  waiting for transfers between devices  24.1 us (40%)
  blocking collectives  18.2 us (30%)
  starting transfers between devices  6.86 us (11%)
  Pallas kernels  5.88 us (10%)
  local copies, waits for them, and re-layouts  2.6 us (4%)
  other arithmetic  1.33 us (2%)
  matrix products  0.91 us (1%)
  between operations  0.76 us (1%)
    all_to_all x1, waiting for transfers between devices, spread_block(): returned = lax.all_to_all(produced, NODE, 0, 0, tiled=True)  22.5 us
    all_to_all x1, blocking collectives, spread_block(): same_core = lax.all_to_all(spread, 'chip', 0, 0, tiled=True)  18.2 us
    pallas_call x1, Pallas kernels, expert_mlp(): pl.pallas_call(mlp_kernel, grid_spec=grid_spec, out_shape=jax.ShapeDtypeS...  5.88 us
    all_to_all x1, starting transfers between devices, spread_block(): returned = lax.all_to_all(produced, NODE, 0, 0, tiled=True)  4.7 us
    ppermute x1, starting transfers between devices, spread_block(): lax.ppermute(same_core, 'core', [(i, (i + 1) % cores) for i in range(core...  2.16 us
    ppermute x1, waiting for transfers between devices, spread_block(): lax.ppermute(same_core, 'core', [(i, (i + 1) % cores) for i in range(core...  1.54 us
  transfers between devices with their start and end apart: 2, of which 2 were waited for; matrix products, arithmetic and copies ran while one was open for 4% of the time, Pallas kernels for 0%

profile of v16, /device:TPU:11, one launch (start us, length us, event | category | flops | bytes accessed | tf_op | source)
XLA Modules:
  0.0 60.6 jit_solution(17679662331981838320)
XLA Ops:
  0.6 0.0 copy-start
  0.6 1.0 %broadcast_in_dim.56 = bf16[8,16,2048]{2,1,0:T(8,128)(2,1)S(1)} broadcast(bf16[16,2048]{1,0:T(8,128)(2,1)} %param.13), dimensions={1,2} | broadcast | bytes 589824 | tf_op jit(solution)/shard_map/broadcast_in_dim | solution.py:181
  1.6 18.2 %all_to_all.10 = bf16[8,16,2048]{2,1,0:T(8,128)(2,1)S(1)} all-to-all(bf16[8,16,2048]{2,1,0:T(8,128)(2,1)S(1)} %broadcast_in_dim.56), channel_id=1, replica_groups=mesh['group'=2,'chip'=8,'core'=2] {'chip'}, dimensions={0} | all-to-all | bytes 1048576 | tf_op jit(solution)/shard_map/all_to_all | solution.py:182
  19.8 2.2 %collective-permute-start = (bf16[8,16,2048]{2,1,0:T(8,128)(2,1)S(1)}, bf16[8,16,2048]{2,1,0:T(8,128)(2,1)S(1)}, u32[]{:S(2)}, u32[]{:S(2)}) collective-permute-start(bf16[8,16,2048]{2,1,0:T(8,128)(2,1)S(1)} %all_to_all.10), channel_id=1, source_target_pairs={{0,1},{1,0},{2,3},{3,2},{4,5},{5,4},{6,7},{7,6},{8,9},{9,8},{10,11... | collective-permute-start | bytes 1572872 | tf_op jit(solution)/shard_map/ppermute | solution.py:183
  22.0 1.5 %collective-permute-done = bf16[8,16,2048]{2,1,0:T(8,128)(2,1)S(1)} collective-permute-done((bf16[8,16,2048]{2,1,0:T(8,128)(2,1)S(1)}, bf16[8,16,2048]{2,1,0:T(8,128)(2,1)S(1)}, u32[]{:S(2)}, u32[]{:S(2)}) %collective-permute-start) | collective-permute-done | bytes 524320 | tf_op jit(solution)/shard_map/ppermute | solution.py:183
  23.5 0.7 %broadcast_in_dim.55.gain_ref = f32[8,2048]{1,0:T(8,128)S(1)} broadcast(f32[2048]{0:T(1024)} %param.14), dimensions={1} | broadcast | bytes 73728 | tf_op jit(solution)/shard_map/broadcast_in_dim | solution.py:184
  24.2 0.0 copy-start.2
  24.2 0.0 copy-start.3
  24.2 0.0 copy-start.4
  24.3 0.0 copy-start.5
  24.3 0.0 copy-start.7
  24.3 0.0 copy-start.1
  24.3 5.9 %shard_map.140 = bf16[1,8,2,16,2048]{4,3,2,1,0:T(8,128)(2,1)} custom-call(s32[1]{0:T(128)} %bitcast.1.core_ref, f32[8,2048]{1,0:T(8,128)S(1)} %broadcast_in_dim.55.gain_ref, bf16[128,2048]{1,0:T(8,128)(2,1)S(1)} %bitcast.44, bf16[128,2048]{1,0:T(8,128)(2,1)S(1)} %bitcast.45, bf16[1,2048,768]{2,1,0:T(8,128)(2,1)} %gate_hbm.1, bf16[1,2048,768]{2,1,0:T(8,128)(2,1)} %up_hbm.1, ...), custom_call_target="tpu_custom_call" | custom-call | tf_op jit(solution)/shard_map/pallas_call | solution.py:161
  30.2 0.0 copy-start.6
  30.2 4.7 %all-to-all-start.1 = ((bf16[16,1,16,2048]{3,2,1,0:T(8,128)(2,1)}), bf16[16,1,16,2048]{3,2,1,0:T(8,128)(2,1)S(1)}, u32[]{:S(2)}, u32[]{:S(2)}) async-start(bf16[16,1,16,2048]{3,2,1,0:T(8,128)(2,1)} %bitcast.5), calls=%async_computation.1 | async-start | bytes 2097152 | tf_op jit(solution)/shard_map/all_to_all | solution.py:197
  34.9 0.0 copy-done.2
  34.9 0.1 copy.25
  35.0 0.0 copy-done.3
  35.0 0.1 copy.24
  35.1 0.1 select_reduce_fusion
  35.2 0.1 copy.26
  35.3 0.0 copy-done.4
  35.3 0.0 copy-done.5
  35.3 0.0 copy-done.7
  35.3 0.1 iota_compare_fusion.1
  35.4 0.0 copy-done.1
  35.4 0.1 fusion.13
  35.5 0.0 copy-done
  35.5 0.5 fusion.21
  36.0 0.2 fusion.8
  36.2 0.0 copy-done.6
  36.2 0.3 fusion.3
  36.6 0.6 %copy.57 = bf16[1,4,32,128]{3,1,2,0:T(4,128)(2,1)} copy(bf16[1,4,32,128]{3,2,1,0:T(8,128)(2,1)S(1)} %fusion.3) | data formatting | bytes 65536
  37.2 22.5 %all-to-all-done.1 = bf16[16,1,16,2048]{3,2,1,0:T(8,128)(2,1)S(1)} async-done(((bf16[16,1,16,2048]{3,2,1,0:T(8,128)(2,1)}), bf16[16,1,16,2048]{3,2,1,0:T(8,128)(2,1)S(1)}, u32[]{:S(2)}, u32[]{:S(2)}) %all-to-all-start.1) | async-done | bytes 1048608 | tf_op jit(solution)/shard_map/all_to_all | solution.py:197
  59.7 0.9 %fusion = bf16[16,2048]{1,0:T(8,128)(2,1)} fusion(bf16[16,1,16,2048]{3,2,1,0:T(8,128)(2,1)S(1)} %all-to-all-done.1, f32[16,16]{1,0:T(8,128)S(1)} %copy.26), kind=kLoop, calls=%fused_computation.1 | loop fusion | flops 1540096 | bytes 1115136 | tf_op jit(solution)/shard_map/reduce_sum | solution.py:204
  (6 shorter events, 0.1 us)
Async XLA Ops:
  0.6 34.9 %copy-start = (bf16[4,256,512]{2,1,0:T(8,128)(2,1)S(1)}, bf16[4,256,512]{2,1,0:T(8,128)(2,1)}, u32[]{:S(2)}) copy-start(bf16[4,256,512]{2,1,0:T(8,128)(2,1)} %param.21) | copy-start | bytes 3145732
  19.8 3.7 %collective-permute-start = (bf16[8,16,2048]{2,1,0:T(8,128)(2,1)S(1)}, bf16[8,16,2048]{2,1,0:T(8,128)(2,1)S(1)}, u32[]{:S(2)}, u32[]{:S(2)}) collective-permute-start(bf16[8,16,2048]{2,1,0:T(8,128)(2,1)S(1)} %all_to_all.10), channel_id=1, source_target_pairs={{0,1},{1,0},{2,3},{3,2},{4,5},{5,4},{6,7},{7,6},{8,9},{9,8},{10,11... | collective-permute-start | bytes 1572872 | tf_op jit(solution)/shard_map/ppermute | solution.py:183
  24.2 10.7 %copy-start.2 = (f32[16,8]{0,1:T(8,128)S(1)}, f32[16,8]{0,1:T(8,128)}, u32[]{:S(2)}) copy-start(f32[16,8]{0,1:T(8,128)} %param.16) | copy-start | bytes 1540
  24.2 10.8 %copy-start.3 = (s32[16,8]{0,1:T(8,128)S(1)}, s32[16,8]{0,1:T(8,128)}, u32[]{:S(2)}) copy-start(s32[16,8]{0,1:T(8,128)} %param.15) | copy-start | bytes 1540
  24.2 11.0 %copy-start.4 = (bf16[4,512]{1,0:T(4,128)(2,1)S(1)}, bf16[4,512]{1,0:T(4,128)(2,1)}, u32[]{:S(2)}) copy-start(bf16[4,512]{1,0:T(4,128)(2,1)} %param.23) | copy-start | bytes 12292
  24.3 11.0 %copy-start.5 = (bf16[4,512]{1,0:T(4,128)(2,1)S(1)}, bf16[4,512]{1,0:T(4,128)(2,1)}, u32[]{:S(2)}) copy-start(bf16[4,512]{1,0:T(4,128)(2,1)} %param.24) | copy-start | bytes 12292
  24.3 11.0 %copy-start.7 = (s32[4]{0:T(128)S(1)}, s32[4]{0:T(128)}, u32[]{:S(2)}) copy-start(s32[4]{0:T(128)} %param.25) | copy-start | bytes 52
  24.3 11.1 %copy-start.1 = (bf16[4,4096]{1,0:T(4,128)(2,1)S(1)}, bf16[4,4096]{1,0:T(4,128)(2,1)}, u32[]{:S(2)}) copy-start(bf16[4,4096]{1,0:T(4,128)(2,1)} %param.20) | copy-start | bytes 98308
  30.2 6.1 %copy-start.6 = (bf16[4,256,512]{2,1,0:T(8,128)(2,1)S(1)}, bf16[4,256,512]{2,1,0:T(8,128)(2,1)}, u32[]{:S(2)}) copy-start(bf16[4,256,512]{2,1,0:T(8,128)(2,1)} %param.22) | copy-start | bytes 3145732
  30.2 29.5 %all-to-all-start.1 = ((bf16[16,1,16,2048]{3,2,1,0:T(8,128)(2,1)}), bf16[16,1,16,2048]{3,2,1,0:T(8,128)(2,1)S(1)}, u32[]{:S(2)}, u32[]{:S(2)}) async-start(bf16[16,1,16,2048]{3,2,1,0:T(8,128)(2,1)} %bitcast.5), calls=%async_computation.1 | async-start | bytes 2097152 | tf_op jit(solution)/shard_map/all_to_all | solution.py:197

commit v17 on v16

--- a/solution.py
+++ b/solution.py
@@ -200,7 +200,12 @@
     expert_ids = jnp.arange(experts_all, dtype=jnp.int32)
     chosen = picks[:, :, None] == expert_ids[None, None, :]
     dense_shares = jnp.sum(jnp.where(chosen, shares[:, :, None], 0.0), axis=1)
-    weighted = dense_shares.T[:, :, None] * returned.astype(jnp.float32)
+    lanes = 128 if features % 128 == 0 else features
+    column_shares = lax.optimization_barrier(
+        jnp.broadcast_to(dense_shares.T[:, :, None], dense_shares.T.shape + (lanes,))
+    )
+    column_shares = jnp.tile(column_shares, (1, 1, features // lanes))
+    weighted = column_shares * returned.astype(jnp.float32)
     return jnp.sum(weighted, axis=0).astype(jnp.bfloat16)
 
 def attend(queries, keys, values, incoming_keys, incoming_values, lengths):

time: 60.9 us -> 62.7 us (1.030)
  waiting for transfers between devices: 24.1 us -> 19.6 us
  local copies, waits for them, and re-layouts: 2.6 us -> 5.96 us
  matrix products: 0.91 us -> 2.14 us
  other arithmetic: 1.33 us -> 2.55 us
    all_to_all x1, waiting for transfers between devices: 22.5 us -> 18 us  [spread_block(): returned = lax.all_to_all(produced, NODE, 0, 0, tiled=True)]
    another operation x0 -> x2, local copies, waits for them, and re-layouts: none -> 3.28 us  [spread_block(): column_shares = jnp.tile(column_shares, (1, 1, features // lanes))]
    dot_general x1, matrix products: 0.31 us -> 1.54 us  [attend(): jnp.einsum('rkgl,rlkd->rkgd', probs, stored_values, preferred_element_typ...]
    reduce_sum x1, other arithmetic: 0.89 us -> 2.11 us  [spread_block(): return jnp.sum(weighted, axis=0).astype(jnp.bfloat16)]
  transfers between devices with their start and end apart: 2 -> 2, of which waited for: 2 -> 2; matrix products, arithmetic and copies ran while one was open for 4% -> 11% of each run, Pallas kernels for 0% -> 0%
where the time goes in v17:
time: 62.7 us; the launch traced here: 62.2 us
  waiting for transfers between devices  19.6 us (31%)
  blocking collectives  18.2 us (29%)
  starting transfers between devices  7.18 us (11%)
  local copies, waits for them, and re-layouts  5.96 us (10%)
  Pallas kernels  5.86 us (9%)
  other arithmetic  2.55 us (4%)
  matrix products  2.14 us (3%)
  between operations  0.76 us (1%)
    all_to_all x1, blocking collectives, spread_block(): same_core = lax.all_to_all(spread, 'chip', 0, 0, tiled=True)  18.2 us
    all_to_all x1, waiting for transfers between devices, spread_block(): returned = lax.all_to_all(produced, NODE, 0, 0, tiled=True)  18 us
    pallas_call x1, Pallas kernels, expert_mlp(): pl.pallas_call(mlp_kernel, grid_spec=grid_spec, out_shape=jax.ShapeDtypeS...  5.86 us
    all_to_all x1, starting transfers between devices, spread_block(): returned = lax.all_to_all(produced, NODE, 0, 0, tiled=True)  5.02 us
    another operation x2, local copies, waits for them, and re-layouts, spread_block(): column_shares = jnp.tile(column_shares, (1, 1, features // lanes))  3.28 us
    ppermute x1, starting transfers between devices, spread_block(): lax.ppermute(same_core, 'core', [(i, (i + 1) % cores) for i in range(core...  2.16 us
    reduce_sum x1, other arithmetic, spread_block(): return jnp.sum(weighted, axis=0).astype(jnp.bfloat16)  2.11 us
    dot_general x1, matrix products, attend(): jnp.einsum('rkgl,rlkd->rkgd', probs, stored_values, preferred_element_typ...  1.54 us
  transfers between devices with their start and end apart: 2, of which 2 were waited for; matrix products, arithmetic and copies ran while one was open for 11% of the time, Pallas kernels for 0%

profile of v17, /device:TPU:11, one launch (start us, length us, event | category | flops | bytes accessed | tf_op | source)
XLA Modules:
  0.0 62.2 jit_solution(9016691447002389963)
XLA Ops:
  0.6 0.0 copy-start
  0.6 1.0 %broadcast_in_dim.62 = bf16[8,16,2048]{2,1,0:T(8,128)(2,1)S(1)} broadcast(bf16[16,2048]{1,0:T(8,128)(2,1)} %param.13), dimensions={1,2} | broadcast | bytes 589824 | tf_op jit(solution)/shard_map/broadcast_in_dim | solution.py:181
  1.6 18.2 %all_to_all.10 = bf16[8,16,2048]{2,1,0:T(8,128)(2,1)S(1)} all-to-all(bf16[8,16,2048]{2,1,0:T(8,128)(2,1)S(1)} %broadcast_in_dim.62), channel_id=1, replica_groups=mesh['group'=2,'chip'=8,'core'=2] {'chip'}, dimensions={0} | all-to-all | bytes 1048576 | tf_op jit(solution)/shard_map/all_to_all | solution.py:182
  19.8 2.2 %collective-permute-start = (bf16[8,16,2048]{2,1,0:T(8,128)(2,1)S(1)}, bf16[8,16,2048]{2,1,0:T(8,128)(2,1)S(1)}, u32[]{:S(2)}, u32[]{:S(2)}) collective-permute-start(bf16[8,16,2048]{2,1,0:T(8,128)(2,1)S(1)} %all_to_all.10), channel_id=1, source_target_pairs={{0,1},{1,0},{2,3},{3,2},{4,5},{5,4},{6,7},{7,6},{8,9},{9,8},{10,11... | collective-permute-start | bytes 1572872 | tf_op jit(solution)/shard_map/ppermute | solution.py:183
  22.0 1.5 %collective-permute-done = bf16[8,16,2048]{2,1,0:T(8,128)(2,1)S(1)} collective-permute-done((bf16[8,16,2048]{2,1,0:T(8,128)(2,1)S(1)}, bf16[8,16,2048]{2,1,0:T(8,128)(2,1)S(1)}, u32[]{:S(2)}, u32[]{:S(2)}) %collective-permute-start) | collective-permute-done | bytes 524320 | tf_op jit(solution)/shard_map/ppermute | solution.py:183
  23.5 0.7 %broadcast_in_dim.61.gain_ref = f32[8,2048]{1,0:T(8,128)S(1)} broadcast(f32[2048]{0:T(1024)} %param.14), dimensions={1} | broadcast | bytes 73728 | tf_op jit(solution)/shard_map/broadcast_in_dim | solution.py:184
  24.2 5.9 %shard_map.140 = bf16[1,8,2,16,2048]{4,3,2,1,0:T(8,128)(2,1)} custom-call(s32[1]{0:T(128)} %bitcast.1.core_ref, f32[8,2048]{1,0:T(8,128)S(1)} %broadcast_in_dim.61.gain_ref, bf16[128,2048]{1,0:T(8,128)(2,1)S(1)} %bitcast.43, bf16[128,2048]{1,0:T(8,128)(2,1)S(1)} %bitcast.44, bf16[1,2048,768]{2,1,0:T(8,128)(2,1)} %gate_hbm.1, bf16[1,2048,768]{2,1,0:T(8,128)(2,1)} %up_hbm.1, ...), custom_call_target="tpu_custom_call" | custom-call | tf_op jit(solution)/shard_map/pallas_call | solution.py:161
  30.1 0.0 copy-start.2
  30.1 0.0 copy-start.3
  30.1 5.0 %all-to-all-start.1 = ((bf16[16,1,16,2048]{3,2,1,0:T(8,128)(2,1)}), bf16[16,1,16,2048]{3,2,1,0:T(8,128)(2,1)}, u32[]{:S(2)}, u32[]{:S(2)}) async-start(bf16[16,1,16,2048]{3,2,1,0:T(8,128)(2,1)} %bitcast.5), calls=%async_computation.1 | async-start | bytes 2097152 | tf_op jit(solution)/shard_map/all_to_all | solution.py:197
  35.1 0.0 copy-done.2
  35.2 0.1 copy.25
  35.3 0.0 copy-done.3
  35.3 0.1 copy.24
  35.3 0.1 select_reduce_fusion
  35.5 0.1 copy.26
  35.5 0.1 broadcast_in_dim.60
  35.6 1.5 %tile.4 = f32[16,16,16,128]{3,2,1,0:T(8,128)} broadcast(f32[16,16,128]{2,1,0:T(8,128)S(1)} %broadcast_in_dim.60), dimensions={0,1,3} | broadcast | bytes 2228224 | tf_op jit(solution)/shard_map/tile | solution.py:207
  37.1 0.0 copy-start.4
  37.1 0.0 copy-start.5
  37.1 0.0 copy-start.6
  37.1 0.0 copy-start.1
  37.1 1.8 %tile.10 = f32[16,1,16,2048]{3,2,1,0:T(8,128)S(1)} reshape(f32[16,16,16,128]{3,2,1,0:T(8,128)} %tile.4) | data formatting | bytes 4194304 | tf_op jit(solution)/shard_map/tile | solution.py:207
  38.9 0.0 copy-done.4
  38.9 0.0 copy-done.5
  39.0 0.0 copy-done.6
  39.0 0.1 iota_compare_fusion.1
  39.1 0.0 copy-done.1
  39.1 0.1 fusion.12
  39.2 0.0 copy-done
  39.2 0.5 fusion.20
  39.7 0.2 fusion.7
  39.9 1.5 %fusion.2 = bf16[1,4,32,128]{3,2,1,0:T(8,128)(2,1)S(1)} fusion(f32[4,4,8,256]{3,2,1,0:T(8,128)S(1)} %get-tuple-element.5, f32[4,4,8]{2,1,0:T(4,128)S(1)} %get-tuple-element.3, f32[4,4,8]{2,1,0:T(4,128)S(1)} %multiply_maximum_fusion, pred[4,256]{1,0:T(4,128)(4,1)S(1)} %iota_compare_fusion.1, f32[4,4,128]{2,1,0:T(4,128)S(1)} %reshape.85, ...), kind=kOutput, calls=%fused_computation.5 | convolution fusion | flops 8568832 | bytes 1223168 | tf_op jit(solution)/shard_map/rkgl,rlkd->rkgd/dot_general | solution.py:242
  41.4 0.6 %copy.57 = bf16[1,4,32,128]{3,1,2,0:T(4,128)(2,1)} copy(bf16[1,4,32,128]{3,2,1,0:T(8,128)(2,1)S(1)} %fusion.2) | data formatting | bytes 65536
  42.1 18.0 %all-to-all-done.1 = bf16[16,1,16,2048]{3,2,1,0:T(8,128)(2,1)} async-done(((bf16[16,1,16,2048]{3,2,1,0:T(8,128)(2,1)}), bf16[16,1,16,2048]{3,2,1,0:T(8,128)(2,1)}, u32[]{:S(2)}, u32[]{:S(2)}) %all-to-all-start.1) | async-done | bytes 1048608 | tf_op jit(solution)/shard_map/all_to_all | solution.py:197
  60.1 2.1 %multiply_reduce_fusion = bf16[16,2048]{1,0:T(8,128)(2,1)} fusion(f32[16,1,16,2048]{3,2,1,0:T(8,128)S(1)} %tile.10, bf16[16,1,16,2048]{3,2,1,0:T(8,128)(2,1)} %all-to-all-done.1), kind=kLoop, calls=%fused_computation | loop fusion | flops 1540096 | bytes 3211264 | tf_op jit(solution)/shard_map/reduce_sum | solution.py:209
  (6 shorter events, 0.1 us)
Async XLA Ops:
  0.6 38.6 %copy-start = (bf16[4,256,512]{2,1,0:T(8,128)(2,1)S(1)}, bf16[4,256,512]{2,1,0:T(8,128)(2,1)}, u32[]{:S(2)}) copy-start(bf16[4,256,512]{2,1,0:T(8,128)(2,1)} %param.21) | copy-start | bytes 3145732
  19.8 3.7 %collective-permute-start = (bf16[8,16,2048]{2,1,0:T(8,128)(2,1)S(1)}, bf16[8,16,2048]{2,1,0:T(8,128)(2,1)S(1)}, u32[]{:S(2)}, u32[]{:S(2)}) collective-permute-start(bf16[8,16,2048]{2,1,0:T(8,128)(2,1)S(1)} %all_to_all.10), channel_id=1, source_target_pairs={{0,1},{1,0},{2,3},{3,2},{4,5},{5,4},{6,7},{7,6},{8,9},{9,8},{10,11... | collective-permute-start | bytes 1572872 | tf_op jit(solution)/shard_map/ppermute | solution.py:183
  30.1 5.0 %copy-start.2 = (f32[16,8]{0,1:T(8,128)S(1)}, f32[16,8]{0,1:T(8,128)}, u32[]{:S(2)}) copy-start(f32[16,8]{0,1:T(8,128)} %param.16) | copy-start | bytes 1540
  30.1 5.1 %copy-start.3 = (s32[16,8]{0,1:T(8,128)S(1)}, s32[16,8]{0,1:T(8,128)}, u32[]{:S(2)}) copy-start(s32[16,8]{0,1:T(8,128)} %param.15) | copy-start | bytes 1540
  30.1 30.0 %all-to-all-start.1 = ((bf16[16,1,16,2048]{3,2,1,0:T(8,128)(2,1)}), bf16[16,1,16,2048]{3,2,1,0:T(8,128)(2,1)}, u32[]{:S(2)}, u32[]{:S(2)}) async-start(bf16[16,1,16,2048]{3,2,1,0:T(8,128)(2,1)} %bitcast.5), calls=%async_computation.1 | async-start | bytes 2097152 | tf_op jit(solution)/shard_map/all_to_all | solution.py:197
  37.1 1.8 %copy-start.4 = (bf16[4,512]{1,0:T(4,128)(2,1)S(1)}, bf16[4,512]{1,0:T(4,128)(2,1)}, u32[]{:S(2)}) copy-start(bf16[4,512]{1,0:T(4,128)(2,1)} %param.23) | copy-start | bytes 12292
  37.1 1.8 %copy-start.5 = (bf16[4,512]{1,0:T(4,128)(2,1)S(1)}, bf16[4,512]{1,0:T(4,128)(2,1)}, u32[]{:S(2)}) copy-start(bf16[4,512]{1,0:T(4,128)(2,1)} %param.24) | copy-start | bytes 12292
  37.1 1.8 %copy-start.6 = (s32[4]{0:T(128)S(1)}, s32[4]{0:T(128)}, u32[]{:S(2)}) copy-start(s32[4]{0:T(128)} %param.25) | copy-start | bytes 52
  37.1 1.9 %copy-start.1 = (bf16[4,4096]{1,0:T(4,128)(2,1)S(1)}, bf16[4,4096]{1,0:T(4,128)(2,1)}, u32[]{:S(2)}) copy-start(bf16[4,4096]{1,0:T(4,128)(2,1)} %param.20) | copy-start | bytes 98308

commit v18 on v16

--- a/solution.py
+++ b/solution.py
@@ -170,6 +170,24 @@
     )(core.reshape(1), norm_gain, same_rows, other_rows, w_gate, w_up, w_down)
 
 
+def combine_kernel(share_ref, returned_ref, out_ref):
+    experts, _, lanes = share_ref.shape
+    for j in range(out_ref.shape[1] // lanes):
+        window = slice(j * lanes, (j + 1) * lanes)
+        total = None
+        for e in range(experts):
+            term = share_ref[e] * returned_ref[e, :, window].astype(jnp.float32)
+            total = term if total is None else total + term
+        out_ref[:, window] = total.astype(out_ref.dtype)
+
+
+def combine(column_shares, returned):
+    return pl.pallas_call(
+        combine_kernel,
+        out_shape=jax.ShapeDtypeStruct(returned.shape[1:], jnp.bfloat16),
+    )(column_shares, returned)
+
+
 def spread_block(states, norm_gain, picks, gate_weights, w_gate, w_up, w_down):
     chips = lax.axis_size("chip")
     cores = lax.axis_size("core")
@@ -200,8 +218,9 @@
     expert_ids = jnp.arange(experts_all, dtype=jnp.int32)
     chosen = picks[:, :, None] == expert_ids[None, None, :]
     dense_shares = jnp.sum(jnp.where(chosen, shares[:, :, None], 0.0), axis=1)
-    weighted = dense_shares.T[:, :, None] * returned.astype(jnp.float32)
-    return jnp.sum(weighted, axis=0).astype(jnp.bfloat16)
+    lanes = 128 if features % 128 == 0 else features
+    column_shares = jnp.broadcast_to(dense_shares.T[:, :, None], dense_shares.T.shape + (lanes,))
+    return combine(column_shares, returned)
 
 def attend(queries, keys, values, incoming_keys, incoming_values, lengths):
     request_rows = queries.shape[0]

time: 60.9 us -> 63.2 us (1.038)
  Pallas kernels: 5.88 us -> 8.07 us
  local copies, waits for them, and re-layouts: 2.6 us -> 3.62 us
  other arithmetic: 1.33 us -> 0.44 us
    pallas_call x0 -> x1, Pallas kernels: none -> 2.16 us  [combine(): pl.pallas_call(combine_kernel, out_shape=jax.ShapeDtypeStruct(returned.sh...]
    reduce_sum x1 -> x0, other arithmetic: 0.89 us -> none  [spread_block(): return jnp.sum(weighted, axis=0).astype(jnp.bfloat16)]
    broadcast_in_dim x0 -> x1, local copies, waits for them, and re-layouts: none -> 0.87 us  [spread_block(): jnp.broadcast_to(dense_shares.T[:, :, None], dense_shares.T.shape + (lane...]
where the time goes in v18:
time: 63.2 us; the launch traced here: 62.9 us
  waiting for transfers between devices  24.1 us (38%)
  blocking collectives  18.2 us (29%)
  Pallas kernels  8.07 us (13%)
  starting transfers between devices  6.8 us (11%)
  local copies, waits for them, and re-layouts  3.62 us (6%)
  matrix products  0.91 us (1%)
  between operations  0.76 us (1%)
    all_to_all x1, waiting for transfers between devices, spread_block(): returned = lax.all_to_all(produced, NODE, 0, 0, tiled=True)  22.5 us
    all_to_all x1, blocking collectives, spread_block(): same_core = lax.all_to_all(spread, 'chip', 0, 0, tiled=True)  18.2 us
    pallas_call x1, Pallas kernels, expert_mlp(): pl.pallas_call(mlp_kernel, grid_spec=grid_spec, out_shape=jax.ShapeDtypeS...  5.91 us
    all_to_all x1, starting transfers between devices, spread_block(): returned = lax.all_to_all(produced, NODE, 0, 0, tiled=True)  4.64 us
    ppermute x1, starting transfers between devices, spread_block(): lax.ppermute(same_core, 'core', [(i, (i + 1) % cores) for i in range(core...  2.16 us
    pallas_call x1, Pallas kernels, combine(): pl.pallas_call(combine_kernel, out_shape=jax.ShapeDtypeStruct(returned.sh...  2.16 us
    ppermute x1, waiting for transfers between devices, spread_block(): lax.ppermute(same_core, 'core', [(i, (i + 1) % cores) for i in range(core...  1.54 us
  transfers between devices with their start and end apart: 2, of which 2 were waited for; matrix products, arithmetic and copies ran while one was open for 4% of the time, Pallas kernels for 0%

profile of v18, /device:TPU:11, one launch (start us, length us, event | category | flops | bytes accessed | tf_op | source)
XLA Modules:
  0.0 62.9 jit_solution(18169256902809440833)
XLA Ops:
  0.6 0.0 copy-start
  0.6 1.0 %broadcast_in_dim.62 = bf16[8,16,2048]{2,1,0:T(8,128)(2,1)S(1)} broadcast(bf16[16,2048]{1,0:T(8,128)(2,1)} %param.13), dimensions={1,2} | broadcast | bytes 589824 | tf_op jit(solution)/shard_map/broadcast_in_dim | solution.py:199
  1.6 18.2 %all_to_all.10 = bf16[8,16,2048]{2,1,0:T(8,128)(2,1)S(1)} all-to-all(bf16[8,16,2048]{2,1,0:T(8,128)(2,1)S(1)} %broadcast_in_dim.62), channel_id=1, replica_groups=mesh['group'=2,'chip'=8,'core'=2] {'chip'}, dimensions={0} | all-to-all | bytes 1048576 | tf_op jit(solution)/shard_map/all_to_all | solution.py:200
  19.8 2.2 %collective-permute-start = (bf16[8,16,2048]{2,1,0:T(8,128)(2,1)S(1)}, bf16[8,16,2048]{2,1,0:T(8,128)(2,1)S(1)}, u32[]{:S(2)}, u32[]{:S(2)}) collective-permute-start(bf16[8,16,2048]{2,1,0:T(8,128)(2,1)S(1)} %all_to_all.10), channel_id=1, source_target_pairs={{0,1},{1,0},{2,3},{3,2},{4,5},{5,4},{6,7},{7,6},{8,9},{9,8},{10,11... | collective-permute-start | bytes 1572872 | tf_op jit(solution)/shard_map/ppermute | solution.py:201
  22.0 1.5 %collective-permute-done = bf16[8,16,2048]{2,1,0:T(8,128)(2,1)S(1)} collective-permute-done((bf16[8,16,2048]{2,1,0:T(8,128)(2,1)S(1)}, bf16[8,16,2048]{2,1,0:T(8,128)(2,1)S(1)}, u32[]{:S(2)}, u32[]{:S(2)}) %collective-permute-start) | collective-permute-done | bytes 524320 | tf_op jit(solution)/shard_map/ppermute | solution.py:201
  23.5 0.7 %broadcast_in_dim.61.gain_ref = f32[8,2048]{1,0:T(8,128)S(1)} broadcast(f32[2048]{0:T(1024)} %param.14), dimensions={1} | broadcast | bytes 73728 | tf_op jit(solution)/shard_map/broadcast_in_dim | solution.py:202
  24.2 0.0 copy-start.4
  24.2 0.0 copy-start.5
  24.2 0.0 copy-start.8
  24.3 0.0 copy-start.2
  24.3 5.9 %shard_map.140 = bf16[1,8,2,16,2048]{4,3,2,1,0:T(8,128)(2,1)} custom-call(s32[1]{0:T(128)} %bitcast.1.core_ref, f32[8,2048]{1,0:T(8,128)S(1)} %broadcast_in_dim.61.gain_ref, bf16[128,2048]{1,0:T(8,128)(2,1)S(1)} %bitcast.42, bf16[128,2048]{1,0:T(8,128)(2,1)S(1)} %bitcast.43, bf16[1,2048,768]{2,1,0:T(8,128)(2,1)} %gate_hbm.1, bf16[1,2048,768]{2,1,0:T(8,128)(2,1)} %up_hbm.1, ...), custom_call_target="tpu_custom_call" | custom-call | tf_op jit(solution)/shard_map/pallas_call | solution.py:161
  30.2 0.0 copy-start.7
  30.2 0.0 copy-start.3
  30.2 0.0 copy-start.6
  30.2 4.6 %all-to-all-start.1 = ((bf16[16,1,16,2048]{3,2,1,0:T(8,128)(2,1)}), bf16[16,1,16,2048]{3,2,1,0:T(8,128)(2,1)S(1)}, u32[]{:S(2)}, u32[]{:S(2)}) async-start(bf16[16,1,16,2048]{3,2,1,0:T(8,128)(2,1)} %bitcast.5), calls=%async_computation.1 | async-start | bytes 2097152 | tf_op jit(solution)/shard_map/all_to_all | solution.py:215
  34.9 0.0 copy-done.4
  34.9 0.0 copy-done.5
  34.9 0.0 copy-done.8
  34.9 0.1 iota_compare_fusion.1
  35.0 0.0 copy-done.2
  35.0 0.1 fusion.12
  35.1 0.0 copy-done
  35.1 0.5 fusion.20
  35.6 0.2 fusion.7
  35.8 0.0 copy-done.7
  35.8 0.3 fusion.2
  36.2 0.6 %copy.57 = bf16[1,4,32,128]{3,1,2,0:T(4,128)(2,1)} copy(bf16[1,4,32,128]{3,2,1,0:T(8,128)(2,1)S(1)} %fusion.2) | data formatting | bytes 65536
  36.8 0.0 copy-done.3
  36.8 0.1 copy.25
  36.9 0.0 copy-done.6
  36.9 0.1 copy.24
  37.0 0.1 select_reduce_fusion
  37.1 0.1 copy.26
  37.2 22.5 %all-to-all-done.1 = bf16[16,1,16,2048]{3,2,1,0:T(8,128)(2,1)S(1)} async-done(((bf16[16,1,16,2048]{3,2,1,0:T(8,128)(2,1)}), bf16[16,1,16,2048]{3,2,1,0:T(8,128)(2,1)S(1)}, u32[]{:S(2)}, u32[]{:S(2)}) %all-to-all-start.1) | async-done | bytes 1048608 | tf_op jit(solution)/shard_map/all_to_all | solution.py:215
  59.7 0.0 copy-start.1
  59.7 0.9 %broadcast_in_dim.60.share_ref = f32[16,16,128]{2,1,0:T(8,128)} broadcast(f32[16,16]{1,0:T(8,128)S(1)} %copy.26), dimensions={0,1} | broadcast | bytes 132096 | tf_op jit(solution)/shard_map/broadcast_in_dim | solution.py:222
  60.6 0.2 copy-done.1
  60.7 2.2 %shard_map.141 = bf16[16,2048]{1,0:T(8,128)(2,1)} custom-call(f32[16,16,128]{2,1,0:T(8,128)} %broadcast_in_dim.60.share_ref, bf16[16,16,2048]{2,1,0:T(8,128)(2,1)} %bitcast.44), custom_call_target="tpu_custom_call" | custom-call | tf_op jit(solution)/shard_map/pallas_call | solution.py:185
  (6 shorter events, 0.1 us)
Async XLA Ops:
  0.6 34.5 %copy-start = (bf16[4,256,512]{2,1,0:T(8,128)(2,1)S(1)}, bf16[4,256,512]{2,1,0:T(8,128)(2,1)}, u32[]{:S(2)}) copy-start(bf16[4,256,512]{2,1,0:T(8,128)(2,1)} %param.21) | copy-start | bytes 3145732
  19.8 3.7 %collective-permute-start = (bf16[8,16,2048]{2,1,0:T(8,128)(2,1)S(1)}, bf16[8,16,2048]{2,1,0:T(8,128)(2,1)S(1)}, u32[]{:S(2)}, u32[]{:S(2)}) collective-permute-start(bf16[8,16,2048]{2,1,0:T(8,128)(2,1)S(1)} %all_to_all.10), channel_id=1, source_target_pairs={{0,1},{1,0},{2,3},{3,2},{4,5},{5,4},{6,7},{7,6},{8,9},{9,8},{10,11... | collective-permute-start | bytes 1572872 | tf_op jit(solution)/shard_map/ppermute | solution.py:201
  24.2 10.6 %copy-start.4 = (bf16[4,512]{1,0:T(4,128)(2,1)S(1)}, bf16[4,512]{1,0:T(4,128)(2,1)}, u32[]{:S(2)}) copy-start(bf16[4,512]{1,0:T(4,128)(2,1)} %param.23) | copy-start | bytes 12292
  24.2 10.7 %copy-start.5 = (bf16[4,512]{1,0:T(4,128)(2,1)S(1)}, bf16[4,512]{1,0:T(4,128)(2,1)}, u32[]{:S(2)}) copy-start(bf16[4,512]{1,0:T(4,128)(2,1)} %param.24) | copy-start | bytes 12292
  24.2 10.7 %copy-start.8 = (s32[4]{0:T(128)S(1)}, s32[4]{0:T(128)}, u32[]{:S(2)}) copy-start(s32[4]{0:T(128)} %param.25) | copy-start | bytes 52
  24.3 10.7 %copy-start.2 = (bf16[4,4096]{1,0:T(4,128)(2,1)S(1)}, bf16[4,4096]{1,0:T(4,128)(2,1)}, u32[]{:S(2)}) copy-start(bf16[4,4096]{1,0:T(4,128)(2,1)} %param.20) | copy-start | bytes 98308
  30.2 5.7 %copy-start.7 = (bf16[4,256,512]{2,1,0:T(8,128)(2,1)S(1)}, bf16[4,256,512]{2,1,0:T(8,128)(2,1)}, u32[]{:S(2)}) copy-start(bf16[4,256,512]{2,1,0:T(8,128)(2,1)} %param.22) | copy-start | bytes 3145732
  30.2 6.6 %copy-start.3 = (f32[16,8]{0,1:T(8,128)S(1)}, f32[16,8]{0,1:T(8,128)}, u32[]{:S(2)}) copy-start(f32[16,8]{0,1:T(8,128)} %param.16) | copy-start | bytes 1540
  30.2 6.7 %copy-start.6 = (s32[16,8]{0,1:T(8,128)S(1)}, s32[16,8]{0,1:T(8,128)}, u32[]{:S(2)}) copy-start(s32[16,8]{0,1:T(8,128)} %param.15) | copy-start | bytes 1540
  30.2 29.5 %all-to-all-start.1 = ((bf16[16,1,16,2048]{3,2,1,0:T(8,128)(2,1)}), bf16[16,1,16,2048]{3,2,1,0:T(8,128)(2,1)S(1)}, u32[]{:S(2)}, u32[]{:S(2)}) async-start(bf16[16,1,16,2048]{3,2,1,0:T(8,128)(2,1)} %bitcast.5), calls=%async_computation.1 | async-start | bytes 2097152 | tf_op jit(solution)/shard_map/all_to_all | solution.py:215
  59.7 1.0 %copy-start.1 = (bf16[16,1,16,2048]{3,2,1,0:T(8,128)(2,1)}, bf16[16,1,16,2048]{3,2,1,0:T(8,128)(2,1)S(1)}, u32[]{:S(2)}) copy-start(bf16[16,1,16,2048]{3,2,1,0:T(8,128)(2,1)S(1)} %all-to-all-done.1) | copy-start | bytes 3145732
